TPU v7x, 128 devices: a whole 4x4x4 slice. The times are simulated.
128 devices in a mesh: dp: 4 (over x), tensor: 32 (over z, y, core).
Axes of the slice: x: 4, y: 4, z: 4, core: 2. Of those that a mesh axis runs over, the one named last changes fastest.
Arguments:
- inputs: bfloat16 [1024, 28672], P('dp', 'tensor'), may hold values from -0.1875 to 0.1875
- output_gradient: bfloat16 [1024, 8192], P('dp', 'tensor'), may hold values from -6 to 6
- frozen: bfloat16 [8192, 28672], P('dp', 'tensor'), may hold values from -0.5905695 to 0.5905695
- adapter_down_factor: bfloat16 [64, 28672], P(None, 'tensor'), may hold values from -0.03125 to 0.03125
- adapter_up_factor: bfloat16 [8192, 64], P('dp'), may hold values from -0.3125 to 0.3125
- magnitude: float32 [8192], P('dp'), may hold values from 0.5 to 2
Outputs:
- input_gradient_rows: bfloat16 [1024, 28672], P('dp', 'tensor')
- adapter_down_gradient: float32 [64, 28672], P(None, 'tensor')
- adapter_up_gradient: float32 [8192, 64], P('dp')
- magnitude_gradient: float32 [8192], P('dp')
All inputs are finite; a program needn't handle non-finite values.
Results may differ from a plain program's by a relative error of at most 0.0057.
Values may be sent and summed in bfloat16 or wider, within the bound.
No kernel may reach another device: no remote copies, remote signals or barrier semaphores. Data moves between devices by JAX's collectives and lax.ppermute only.
A program may use at most 128 MiB of HBM per device.

v0:
```python
import jax
import jax.numpy as jnp
from jax import lax
from jax.sharding import PartitionSpec as P


adapter_scale = 2.0
epsilon = 1e-06


def split_bf16(v):
    hi = v.astype(jnp.bfloat16)
    lo = (v - hi.astype(jnp.float32)).astype(jnp.bfloat16)
    return hi, lo


def dot2(spec, a, b_pair):
    hi, lo = b_pair
    return jnp.einsum(spec, a, hi, preferred_element_type=jnp.float32) + jnp.einsum(
        spec, a, lo, preferred_element_type=jnp.float32
    )


def transpose_pairs(n_dp, n_t):
    group = n_t // n_dp
    pairs = []
    for d in range(n_dp):
        for t in range(n_t):
            b, rest = divmod(t, group)
            pairs.append((d * n_t + t, b * n_t + d * group + rest))
    return pairs


def shift_pairs(n, k):
    return [(i, (i + k) % n) for i in range(n)]


def gather_dp(v, n_dp, d):
    out = jnp.zeros((n_dp,) + v.shape, v.dtype)
    out = lax.dynamic_update_index_in_dim(out, v, d, 0)
    for k in range(1, n_dp):
        piece = lax.ppermute(v, "dp", shift_pairs(n_dp, k))
        out = lax.dynamic_update_index_in_dim(out, piece, (d + n_dp - k) % n_dp, 0)
    return out


def allreduce(v, axis, n):
    k = 1
    while k < n:
        v = v + lax.ppermute(v, axis, [(i, i ^ k) for i in range(n)])
        k *= 2
    return v


def make_local(n_dp, n_t):
    pairs = transpose_pairs(n_dp, n_t)

    def body(inputs, output_gradient, frozen, adapter_down_factor, adapter_up_factor, magnitude):
        d = lax.axis_index("dp")
        tok, _ = inputs.shape
        rows = frozen.shape[0]
        rank = adapter_down_factor.shape[0]

        og_p = lax.ppermute(output_gradient, ("dp", "tensor"), pairs)
        og_all = lax.all_gather(og_p, "tensor", axis=1, tiled=True).reshape(tok, n_dp, rows)
        x_all = gather_dp(inputs, n_dp, d)

        merged = frozen.astype(jnp.float32) + adapter_scale * jnp.dot(
            adapter_up_factor, adapter_down_factor, preferred_element_type=jnp.float32
        )
        merged_b = merged.astype(jnp.bfloat16)
        squares = jnp.sum(merged * merged, axis=1)
        h_local = jnp.dot(inputs, adapter_down_factor.T, preferred_element_type=jnp.float32)

        first = allreduce(jnp.concatenate([squares, h_local.reshape(-1)]), "tensor", n_t)
        total_squares = first[:rows]
        h_all = gather_dp(first[rows:].reshape(tok, rank), n_dp, d)

        weight_row_norm = jnp.sqrt(total_squares + epsilon)
        col_scale = magnitude / weight_row_norm
        col_scale, weight_row_norm = lax.optimization_barrier((col_scale, weight_row_norm))

        scaled = (og_all.astype(jnp.float32) * col_scale).astype(jnp.bfloat16)
        ig_part = jnp.einsum("tbj,ji->bti", scaled, merged_b, preferred_element_type=jnp.float32)
        own = lax.dynamic_index_in_dim(ig_part, d, 0, keepdims=False)
        sends = [
            lax.dynamic_index_in_dim(ig_part, (d + k) % n_dp, 0, keepdims=False).astype(jnp.bfloat16)
            for k in range(1, n_dp)
        ]
        acc = own
        received = [lax.ppermute(sends[k - 1], "dp", shift_pairs(n_dp, k)) for k in range(1, n_dp)]
        for piece in received:
            acc = acc + piece.astype(jnp.float32)
        input_gradient_rows = acc.astype(jnp.bfloat16)

        product = jnp.einsum("tbj,bti->ji", og_all, x_all, preferred_element_type=jnp.float32)
        grad_scale_part = jnp.sum(product * merged, axis=1)
        grad_scale = allreduce(grad_scale_part, "tensor", n_t)

        w = col_scale[:, None] * adapter_up_factor.astype(jnp.float32)
        g_all = allreduce(dot2("tbj,jr->btr", og_all, split_bf16(w)), "dp", n_dp)

        gh, gl = split_bf16(g_all)
        adapter_down_gradient = adapter_scale * (
            jnp.einsum("btr,bti->ri", gh, x_all, preferred_element_type=jnp.float32)
            + jnp.einsum("btr,bti->ri", gl, x_all, preferred_element_type=jnp.float32)
        )
        up = dot2("tbj,btr->jr", og_all, split_bf16(h_all))
        adapter_up_gradient = adapter_scale * (col_scale[:, None] * up)
        magnitude_gradient = grad_scale / weight_row_norm
        return (input_gradient_rows, adapter_down_gradient, adapter_up_gradient, magnitude_gradient)

    return body


def solution(mesh):
    n_dp = mesh.shape["dp"]
    n_t = mesh.shape["tensor"]
    placed = (
        P("dp", "tensor"),
        P("dp", "tensor"),
        P("dp", "tensor"),
        P(None, "tensor"),
        P("dp", None),
        P("dp"),
    )
    return jax.shard_map(
        make_local(n_dp, n_t),
        mesh=mesh,
        in_specs=placed,
        out_specs=(P("dp", "tensor"), P(None, "tensor"), P("dp", None), P("dp")),
        check_vma=False,
    )
```

profile of v0, /device:TPU:0, one launch (start us, length us, event | category | flops | bytes accessed | tf_op | source)
XLA Modules:
  0.0 153.6 jit_solution(8122471330108340522)
XLA Ops:
  7.2 1.1 copy.19
  8.3 0.8 collective-permute-start
  9.1 0.6 copy-done.6
  9.8 6.2 %copy.18 = bf16[2048,896]{0,1:T(8,128)(2,1)} copy(bf16[2048,896]{1,0:T(8,128)(2,1)} %param.8) | data formatting | bytes 7340032 | tf_op args[2]
  16.0 0.3 fusion.32
  16.3 0.1 reshape.30
  16.4 6.4 %multiply_reduce_fusion = (f32[2048]{0:T(1024)S(1)}, f32[2048,896]{0,1:T(8,128)}) fusion(bf16[2048,64]{0,1:T(8,128)(2,1)S(1)} %copy-done.2, bf16[64,896]{1,0:T(8,128)(2,1)S(1)} %copy-done, bf16[2048,896]{0,1:T(8,128)(2,1)} %copy.18), kind=kOutput, calls=%fused_computation.3 | convolution fusion | flops 244054016 | bytes 11395072 | tf_op jit(solution)/shard_map/dot_general | solution.py:68
  22.8 0.1 collective-permute-start.1
  22.9 1.3 collective-permute-done.1
  24.2 1.8 %collective-permute-start.2 = (f32[18432]{0:T(1024)S(1)}, f32[18432]{0:T(1024)S(1)}, u32[]{:S(2)}, u32[]{:S(2)}) collective-permute-start(f32[18432]{0:T(1024)S(1)} %fusion.31), channel_id=1, source_target_pairs={{0,2},{1,3},{2,0},{3,1},{4,6},{5,7},{6,4},{7,5},{8,10},{9,11},{10,... | collective-permute-start | bytes 221192 | tf_op jit(solution)/shard_map/ppermute | solution.py:50
  26.0 2.7 %collective-permute-done.2 = f32[18432]{0:T(1024)S(1)} collective-permute-done((f32[18432]{0:T(1024)S(1)}, f32[18432]{0:T(1024)S(1)}, u32[]{:S(2)}, u32[]{:S(2)}) %collective-permute-start.2) | collective-permute-done | bytes 73760 | tf_op jit(solution)/shard_map/ppermute | solution.py:50
  28.6 3.4 %collective-permute-start.3 = (f32[18432]{0:T(1024)S(1)}, f32[18432]{0:T(1024)S(1)}, u32[]{:S(2)}, u32[]{:S(2)}) collective-permute-start(f32[18432]{0:T(1024)S(1)} %add.132), channel_id=1, source_target_pairs={{0,4},{1,5},{2,6},{3,7},{4,0},{5,1},{6,2},{7,3},{8,12},{9,13},{10,... | collective-permute-start | bytes 221192 | tf_op jit(solution)/shard_map/ppermute | solution.py:50
  32.0 2.6 %collective-permute-done.3 = f32[18432]{0:T(1024)S(1)} collective-permute-done((f32[18432]{0:T(1024)S(1)}, f32[18432]{0:T(1024)S(1)}, u32[]{:S(2)}, u32[]{:S(2)}) %collective-permute-start.3) | collective-permute-done | bytes 73760 | tf_op jit(solution)/shard_map/ppermute | solution.py:50
  34.6 10.4 %collective-permute-start.4 = (f32[18432]{0:T(1024)S(1)}, f32[18432]{0:T(1024)S(1)}, u32[]{:S(2)}, u32[]{:S(2)}) collective-permute-start(f32[18432]{0:T(1024)S(1)} %add.133), channel_id=1, source_target_pairs={{0,8},{1,9},{2,10},{3,11},{4,12},{5,13},{6,14},{7,15},{8,0},{9,1},... | collective-permute-start | bytes 221192 | tf_op jit(solution)/shard_map/ppermute | solution.py:50
  45.0 8.0 %collective-permute-start.12 = (bf16[256,896]{1,0:T(8,128)(2,1)S(1)}, bf16[256,896]{1,0:T(8,128)(2,1)S(1)}, u32[]{:S(2)}, u32[]{:S(2)}) collective-permute-start(bf16[256,896]{1,0:T(8,128)(2,1)S(1)} %copy-done.5), channel_id=1, source_target_pairs={{0,64},{32,96},{64,0},{96,32},{1,65},{33,97},{65,1},{97,33},{2,66}... | collective-permute-start | bytes 1376264 | tf_op jit(solution)/shard_map/ppermute | solution.py:42
  53.0 0.4 collective-permute-start.13
  53.4 0.2 copy.24
  53.7 3.0 %collective-permute-start.5 = (f32[18432]{0:T(1024)S(1)}, f32[18432]{0:T(1024)S(1)}, u32[]{:S(2)}, u32[]{:S(2)}) collective-permute-start(f32[18432]{0:T(1024)S(1)} %add.134), channel_id=1, source_target_pairs={{0,16},{1,17},{2,18},{3,19},{4,20},{5,21},{6,22},{7,23},{8,24},{9,... | collective-permute-start | bytes 221192 | tf_op jit(solution)/shard_map/ppermute | solution.py:50
  56.7 1.5 broadcast_in_dim.35
  58.1 0.8 constant_dynamic-update-slice_fusion.7
  58.9 2.2 %collective-permute-done.5 = f32[18432]{0:T(1024)S(1)} collective-permute-done((f32[18432]{0:T(1024)S(1)}, f32[18432]{0:T(1024)S(1)}, u32[]{:S(2)}, u32[]{:S(2)}) %collective-permute-start.5) | collective-permute-done | bytes 73760 | tf_op jit(solution)/shard_map/ppermute | solution.py:50
  61.1 0.1 broadcast_in_dim.41
  61.2 0.1 slice.18
  61.3 1.0 collective-permute-start.14
  62.3 1.7 %collective-permute-start.15 = (f32[256,64]{1,0:T(8,128)S(1)}, f32[256,64]{1,0:T(8,128)S(1)}, u32[]{:S(2)}, u32[]{:S(2)}) collective-permute-start(f32[256,64]{1,0:T(8,128)S(1)} %slice.18), channel_id=1, source_target_pairs={{0,64},{32,96},{64,0},{96,32},{1,65},{33,97},{65,1},{97,33},{2,66}... | collective-permute-start | bytes 196616 | tf_op jit(solution)/shard_map/ppermute | solution.py:42
  64.0 0.1 copy.30
  64.1 10.1 %collective-permute-done.14 = f32[256,64]{1,0:T(8,128)S(1)} collective-permute-done((f32[256,64]{1,0:T(8,128)S(1)}, f32[256,64]{1,0:T(8,128)S(1)}, u32[]{:S(2)}, u32[]{:S(2)}) %collective-permute-start.14) | collective-permute-done | bytes 65568 | tf_op jit(solution)/shard_map/ppermute | solution.py:42
  74.2 1.8 %collective-permute-start.16 = (f32[256,64]{1,0:T(8,128)S(1)}, f32[256,64]{1,0:T(8,128)S(1)}, u32[]{:S(2)}, u32[]{:S(2)}) collective-permute-start(f32[256,64]{1,0:T(8,128)S(1)} %slice.18), channel_id=1, source_target_pairs={{0,96},{32,0},{64,32},{96,64},{1,97},{33,1},{65,33},{97,65},{2,98}... | collective-permute-start | bytes 196616 | tf_op jit(solution)/shard_map/ppermute | solution.py:42
  76.0 0.1 copy.31
  76.1 0.7 collective-permute-done.15
  76.8 0.1 copy.32
  76.9 2.3 %collective-permute-done.16 = f32[256,64]{1,0:T(8,128)S(1)} collective-permute-done((f32[256,64]{1,0:T(8,128)S(1)}, f32[256,64]{1,0:T(8,128)S(1)}, u32[]{:S(2)}, u32[]{:S(2)}) %collective-permute-start.16) | collective-permute-done | bytes 65568 | tf_op jit(solution)/shard_map/ppermute | solution.py:42
  79.3 0.2 copy.25
  79.5 0.2 copy.26
  79.8 1.0 copy.27
  80.7 0.8 constant_dynamic-update-slice_fusion.6
  81.6 0.9 constant_dynamic-update-slice_fusion.5
  82.4 2.0 %constant_dynamic-update-slice_fusion.4 = bf16[4,256,896]{1,2,0:T(8,128)(2,1)} fusion(bf16[4,256,896]{1,2,0:T(8,128)(2,1)} %constant_dynamic-update-slice_fusion.5, bf16[1,256,896]{1,2,0:T(8,128)(2,1)} %copy.27, s32[]{:T(128)S(6)} %select_n.52), kind=kLoop, calls=%fused_computation.53 | loop fusion | bytes 917508 | tf_op jit(solution)/shard_map/jit(dynamic_update_index_in_dim)/dynamic_update_slice | solution.py:43
  84.4 9.0 %fusion = f32[2048]{0:T(1024)S(1)} fusion(f32[2048,896]{0,1:T(8,128)} %get-tuple-element.22, bf16[4,256,896]{1,2,0:T(8,128)(2,1)} %constant_dynamic-update-slice_fusion.4, bf16[256,4,2048]{0,2,1:T(8,128)(2,1)} %bitcast.81), kind=kOutput, calls=%fused_computation.2 | convolution fusion | flops 3761764352 | bytes 13377536 | tf_op jit(solution)/shard_map/tbj,bti->ji/dot_general | solution.py:96
  93.4 0.3 collective-permute-start.17
  93.8 4.0 %fusion.1 = f32[896,256,4]{1,0,2:T(8,128)S(1)} fusion(bf16[256,4,2048]{0,2,1:T(8,128)(2,1)S(1)} %bitcast.82, f32[2048]{0:T(1024)S(1)} %get-tuple-element.6, f32[2048,896]{0,1:T(8,128)S(1)} %bitcast.88), kind=kOutput, calls=%fused_computation.5 | convolution fusion | flops 3766222848 | bytes 15212544 | tf_op jit(solution)/shard_map/tbj,ji->bti/dot_general | solution.py:84
  97.8 0.8 fusion.22
  98.6 1.8 %collective-permute-start.18 = (f32[2048]{0:T(1024)S(1)}, f32[2048]{0:T(1024)S(1)}, u32[]{:S(2)}, u32[]{:S(2)}) collective-permute-start(f32[2048]{0:T(1024)S(1)} %add.157), channel_id=1, source_target_pairs={{0,2},{1,3},{2,0},{3,1},{4,6},{5,7},{6,4},{7,5},{8,10},{9,11},{10,... | collective-permute-start | bytes 24584 | tf_op jit(solution)/shard_map/ppermute | solution.py:50
  100.5 0.8 fusion.9
  101.3 1.1 collective-permute-done.18
  102.4 3.0 %collective-permute-start.19 = (f32[2048]{0:T(1024)S(1)}, f32[2048]{0:T(1024)S(1)}, u32[]{:S(2)}, u32[]{:S(2)}) collective-permute-start(f32[2048]{0:T(1024)S(1)} %add.158), channel_id=1, source_target_pairs={{0,4},{1,5},{2,6},{3,7},{4,0},{5,1},{6,2},{7,3},{8,12},{9,13},{10,... | collective-permute-start | bytes 24584 | tf_op jit(solution)/shard_map/ppermute | solution.py:50
  105.3 1.4 convolution_bitcast_fusion
  106.7 1.5 collective-permute-start.9
  108.2 1.7 %collective-permute-start.20 = (f32[2048]{0:T(1024)S(1)}, f32[2048]{0:T(1024)S(1)}, u32[]{:S(2)}, u32[]{:S(2)}) collective-permute-start(f32[2048]{0:T(1024)S(1)} %add.159), channel_id=1, source_target_pairs={{0,8},{1,9},{2,10},{3,11},{4,12},{5,13},{6,14},{7,15},{8,0},{9,1},... | collective-permute-start | bytes 24584 | tf_op jit(solution)/shard_map/ppermute | solution.py:50
  109.9 0.1 fusion.16
  110.0 1.0 collective-permute-start.6
  111.0 3.1 %collective-permute-start.7 = (bf16[256,896]{0,1:T(8,128)(2,1)S(1)}, bf16[256,896]{0,1:T(8,128)(2,1)S(1)}, u32[]{:S(2)}, u32[]{:S(2)}) collective-permute-start(bf16[256,896]{0,1:T(8,128)(2,1)S(1)} %get-tuple-element.18), channel_id=1, source_target_pairs={{0,64},{32,96},{64,0},{96,32},{1,65},{33,97},{65,1},{97,33},{2,66}... | collective-permute-start | bytes 1376264 | tf_op jit(solution)/shard_map/ppermute | solution.py:91
  114.1 1.7 %collective-permute-start.8 = (bf16[256,896]{0,1:T(8,128)(2,1)S(1)}, bf16[256,896]{0,1:T(8,128)(2,1)S(1)}, u32[]{:S(2)}, u32[]{:S(2)}) collective-permute-start(bf16[256,896]{0,1:T(8,128)(2,1)S(1)} %get-tuple-element.17), channel_id=1, source_target_pairs={{0,96},{32,0},{64,32},{96,64},{1,97},{33,1},{65,33},{97,65},{2,98}... | collective-permute-start | bytes 1376264 | tf_op jit(solution)/shard_map/ppermute | solution.py:91
  115.8 2.9 %collective-permute-start.21 = (f32[2048]{0:T(1024)S(1)}, f32[2048]{0:T(1024)S(1)}, u32[]{:S(2)}, u32[]{:S(2)}) collective-permute-start(f32[2048]{0:T(1024)S(1)} %add.160), channel_id=1, source_target_pairs={{0,16},{1,17},{2,18},{3,19},{4,20},{5,21},{6,22},{7,23},{8,24},{9,... | collective-permute-start | bytes 24584 | tf_op jit(solution)/shard_map/ppermute | solution.py:50
  118.7 2.2 %fusion.8 = f32[2048,64]{0,1:T(8,128)} fusion(f32[64,2048]{1,0:T(8,128)S(1)} %convolution_bitcast_fusion, bf16[256,4,2048]{0,2,1:T(8,128)(2,1)S(1)} %bitcast.86, f32[2048]{0:T(1024)S(1)} %get-tuple-element.6, f32[4,256,64]{1,2,0:T(8,128)S(1)} %copy-done.4), kind=kOutput, calls=%fused_computation.14 | convolution fusion | flops 268894208 | bytes 5513216 | tf_op jit(solution)/shard_map/tbj,btr->jr/dot_general | solution.py:19
  120.9 0.6 add_divide_fusion
  121.6 1.4 collective-permute-start.10
  123.0 1.7 %collective-permute-done.6 = bf16[256,896]{0,1:T(8,128)(2,1)S(1)} collective-permute-done((bf16[256,896]{0,1:T(8,128)(2,1)S(1)}, bf16[256,896]{0,1:T(8,128)(2,1)S(1)}, u32[]{:S(2)}, u32[]{:S(2)}) %collective-permute-start.6) | collective-permute-done | bytes 458784 | tf_op jit(solution)/shard_map/ppermute | solution.py:91
  124.7 13.4 %collective-permute-done.7 = bf16[256,896]{0,1:T(8,128)(2,1)S(1)} collective-permute-done((bf16[256,896]{0,1:T(8,128)(2,1)S(1)}, bf16[256,896]{0,1:T(8,128)(2,1)S(1)}, u32[]{:S(2)}, u32[]{:S(2)}) %collective-permute-start.7) | collective-permute-done | bytes 458784 | tf_op jit(solution)/shard_map/ppermute | solution.py:91
  138.1 0.2 fusion.14
  138.3 1.0 copy.37
  139.3 2.5 %collective-permute-done.10 = f32[4,256,64]{1,2,0:T(8,128)S(1)} collective-permute-done((f32[4,256,64]{1,2,0:T(8,128)S(1)}, f32[4,256,64]{1,2,0:T(8,128)S(1)}, u32[]{:S(2)}, u32[]{:S(2)}) %collective-permute-start.10) | collective-permute-done | bytes 262176 | tf_op jit(solution)/shard_map/ppermute | solution.py:50
  141.8 2.2 %convolution_bitcast_fusion.2 = f32[64,896]{1,0:T(8,128)S(1)} fusion(bf16[4,256,896]{1,2,0:T(8,128)(2,1)} %constant_dynamic-update-slice_fusion.4, f32[4,256,64]{1,2,0:T(8,128)S(1)} %add.153, f32[4,256,64]{1,2,0:T(8,128)S(1)} %collective-permute-done.10), kind=kOutput, calls=%fused_computation.17 | convolution fusion | flops 117768192 | bytes 2588672 | tf_op jit(solution)/shard_map/btr,bti->ri/dot_general | solution.py:106
  143.9 2.9 %fusion.11 = f32[64,896]{1,0:T(8,128)} fusion(f32[64,896]{1,0:T(8,128)S(1)} %convolution_bitcast_fusion.2, bf16[4,256,896]{1,2,0:T(8,128)(2,1)} %constant_dynamic-update-slice_fusion.4, f32[4,256,64]{1,2,0:T(8,128)S(1)} %add.153, f32[4,256,64]{1,2,0:T(8,128)S(1)} %collective-permute-done.10), kind=kOutput, calls=%fused_computation.20 | convolution fusion | flops 117686272 | bytes 2818048 | tf_op jit(solution)/shard_map/btr,bti->ri/dot_general | solution.py:105
  (54 shorter events, 0.5 us)
Async XLA Ops:
  7.2 8.9 %copy-start = (bf16[64,896]{1,0:T(8,128)(2,1)S(1)}, bf16[64,896]{1,0:T(8,128)(2,1)}, u32[]{:S(2)}) copy-start(bf16[64,896]{1,0:T(8,128)(2,1)} %param.9) | copy-start | bytes 344068
  7.2 8.9 %copy-start.5 = (bf16[256,896]{1,0:T(8,128)(2,1)S(1)}, bf16[256,896]{1,0:T(8,128)(2,1)}, u32[]{:S(2)}) copy-start(bf16[256,896]{1,0:T(8,128)(2,1)} %param.6) | copy-start | bytes 1376260
  7.2 77.2 %all-gather.2.cloned.1.call-start = ((), (), s32[]{:S(2)}) async-start(), calls=%async_computation | async-start | bytes 4325376 | tf_op jit(solution)/shard_map/all_gather | solution.py:65
  8.3 8.1 %copy-start.2 = (bf16[2048,64]{0,1:T(8,128)(2,1)S(1)}, bf16[2048,64]{0,1:T(8,128)(2,1)}, u32[]{:S(2)}) copy-start(bf16[2048,64]{0,1:T(8,128)(2,1)} %param.10) | copy-start | bytes 786436
  8.3 0.8 collective-permute-start
  9.1 0.7 copy-start.6
  22.8 41.2 %copy-start.7 = (f32[2048]{0:T(1024)S(1)}, f32[2048]{0:T(1024)}, u32[]{:S(2)}) copy-start(f32[2048]{0:T(1024)} %param.11) | copy-start | bytes 24580
  22.8 1.3 collective-permute-start.1
  24.2 4.4 %collective-permute-start.2 = (f32[18432]{0:T(1024)S(1)}, f32[18432]{0:T(1024)S(1)}, u32[]{:S(2)}, u32[]{:S(2)}) collective-permute-start(f32[18432]{0:T(1024)S(1)} %fusion.31), channel_id=1, source_target_pairs={{0,2},{1,3},{2,0},{3,1},{4,6},{5,7},{6,4},{7,5},{8,10},{9,11},{10,... | collective-permute-start | bytes 221192 | tf_op jit(solution)/shard_map/ppermute | solution.py:50
  28.6 5.9 %collective-permute-start.3 = (f32[18432]{0:T(1024)S(1)}, f32[18432]{0:T(1024)S(1)}, u32[]{:S(2)}, u32[]{:S(2)}) collective-permute-start(f32[18432]{0:T(1024)S(1)} %add.132), channel_id=1, source_target_pairs={{0,4},{1,5},{2,6},{3,7},{4,0},{5,1},{6,2},{7,3},{8,12},{9,13},{10,... | collective-permute-start | bytes 221192 | tf_op jit(solution)/shard_map/ppermute | solution.py:50
  34.6 19.0 %collective-permute-start.4 = (f32[18432]{0:T(1024)S(1)}, f32[18432]{0:T(1024)S(1)}, u32[]{:S(2)}, u32[]{:S(2)}) collective-permute-start(f32[18432]{0:T(1024)S(1)} %add.133), channel_id=1, source_target_pairs={{0,8},{1,9},{2,10},{3,11},{4,12},{5,13},{6,14},{7,15},{8,0},{9,1},... | collective-permute-start | bytes 221192 | tf_op jit(solution)/shard_map/ppermute | solution.py:50
  45.0 34.3 %collective-permute-start.11 = (bf16[256,896]{1,0:T(8,128)(2,1)S(1)}, bf16[256,896]{1,0:T(8,128)(2,1)S(1)}, u32[]{:S(2)}, u32[]{:S(2)}) collective-permute-start(bf16[256,896]{1,0:T(8,128)(2,1)S(1)} %copy-done.5), channel_id=1, source_target_pairs={{0,32},{32,64},{64,96},{96,0},{1,33},{33,65},{65,97},{97,1},{2,34}... | collective-permute-start | bytes 1376264 | tf_op jit(solution)/shard_map/ppermute | solution.py:42
  45.0 34.5 %collective-permute-start.12 = (bf16[256,896]{1,0:T(8,128)(2,1)S(1)}, bf16[256,896]{1,0:T(8,128)(2,1)S(1)}, u32[]{:S(2)}, u32[]{:S(2)}) collective-permute-start(bf16[256,896]{1,0:T(8,128)(2,1)S(1)} %copy-done.5), channel_id=1, source_target_pairs={{0,64},{32,96},{64,0},{96,32},{1,65},{33,97},{65,1},{97,33},{2,66}... | collective-permute-start | bytes 1376264 | tf_op jit(solution)/shard_map/ppermute | solution.py:42
  53.0 26.7 %collective-permute-start.13 = (bf16[256,896]{1,0:T(8,128)(2,1)S(1)}, bf16[256,896]{1,0:T(8,128)(2,1)S(1)}, u32[]{:S(2)}, u32[]{:S(2)}) collective-permute-start(bf16[256,896]{1,0:T(8,128)(2,1)S(1)} %copy-done.5), channel_id=1, source_target_pairs={{0,96},{32,0},{64,32},{96,64},{1,97},{33,1},{65,33},{97,65},{2,98}... | collective-permute-start | bytes 1376264 | tf_op jit(solution)/shard_map/ppermute | solution.py:42
  53.7 7.5 %collective-permute-start.5 = (f32[18432]{0:T(1024)S(1)}, f32[18432]{0:T(1024)S(1)}, u32[]{:S(2)}, u32[]{:S(2)}) collective-permute-start(f32[18432]{0:T(1024)S(1)} %add.134), channel_id=1, source_target_pairs={{0,16},{1,17},{2,18},{3,19},{4,20},{5,21},{6,22},{7,23},{8,24},{9,... | collective-permute-start | bytes 221192 | tf_op jit(solution)/shard_map/ppermute | solution.py:50
  61.3 12.9 %collective-permute-start.14 = (f32[256,64]{1,0:T(8,128)S(1)}, f32[256,64]{1,0:T(8,128)S(1)}, u32[]{:S(2)}, u32[]{:S(2)}) collective-permute-start(f32[256,64]{1,0:T(8,128)S(1)} %slice.18), channel_id=1, source_target_pairs={{0,32},{32,64},{64,96},{96,0},{1,33},{33,65},{65,97},{97,1},{2,34}... | collective-permute-start | bytes 196616 | tf_op jit(solution)/shard_map/ppermute | solution.py:42
  62.3 14.5 %collective-permute-start.15 = (f32[256,64]{1,0:T(8,128)S(1)}, f32[256,64]{1,0:T(8,128)S(1)}, u32[]{:S(2)}, u32[]{:S(2)}) collective-permute-start(f32[256,64]{1,0:T(8,128)S(1)} %slice.18), channel_id=1, source_target_pairs={{0,64},{32,96},{64,0},{96,32},{1,65},{33,97},{65,1},{97,33},{2,66}... | collective-permute-start | bytes 196616 | tf_op jit(solution)/shard_map/ppermute | solution.py:42
  74.2 5.0 %collective-permute-start.16 = (f32[256,64]{1,0:T(8,128)S(1)}, f32[256,64]{1,0:T(8,128)S(1)}, u32[]{:S(2)}, u32[]{:S(2)}) collective-permute-start(f32[256,64]{1,0:T(8,128)S(1)} %slice.18), channel_id=1, source_target_pairs={{0,96},{32,0},{64,32},{96,64},{1,97},{33,1},{65,33},{97,65},{2,98}... | collective-permute-start | bytes 196616 | tf_op jit(solution)/shard_map/ppermute | solution.py:42
  79.3 2.3 %copy-start.3 = (f32[4,256,64]{1,2,0:T(8,128)}, f32[4,256,64]{1,2,0:T(8,128)S(1)}, u32[]{:S(2)}) copy-start(f32[4,256,64]{1,2,0:T(8,128)S(1)} %constant_dynamic-update-slice_fusion) | copy-start | bytes 786436
  82.4 11.3 %slice-start = ((s8[7340032]{0:T(1024)(128)(4,1)}), s8[3145728]{0:T(1024)(128)(4,1)S(1)}, s32[]{:S(2)}) async-start(s8[7340032]{0:T(1024)(128)(4,1)} %bitcast.87), calls=%async_computation.1 | async-start | bytes 6291456
  84.4 9.3 %copy-start.1 = (bf16[256,8192]{0,1:T(8,128)(2,1)S(1)}, bf16[256,8192]{0,1:T(8,128)(2,1)}, u32[]{:S(2)}) copy-start(bf16[256,8192]{0,1:T(8,128)(2,1)} %all-gather.2.cloned.1.call-done) | copy-start | bytes 12582916
  84.4 9.3 %slice-start.1 = ((s8[7340032]{0:T(1024)(128)(4,1)}), s8[4194304]{0:T(1024)(128)(4,1)S(1)}, s32[]{:S(2)}) async-start(s8[7340032]{0:T(1024)(128)(4,1)} %bitcast.87), calls=%async_computation.2 | async-start | bytes 8388608
  93.4 5.2 %collective-permute-start.17 = (f32[2048]{0:T(1024)S(1)}, f32[2048]{0:T(1024)S(1)}, u32[]{:S(2)}, u32[]{:S(2)}) collective-permute-start(f32[2048]{0:T(1024)S(1)} %fusion), channel_id=1, source_target_pairs={{0,1},{1,0},{2,3},{3,2},{4,5},{5,4},{6,7},{7,6},{8,9},{9,8},{10,11... | collective-permute-start | bytes 24584 | tf_op jit(solution)/shard_map/ppermute | solution.py:50
  97.8 7.5 %copy-start.4 = (f32[4,256,64]{1,2,0:T(8,128)S(1)}, f32[4,256,64]{1,2,0:T(8,128)}, u32[]{:S(2)}) copy-start(f32[4,256,64]{1,2,0:T(8,128)} %copy-done.3) | copy-start | bytes 786436
  98.6 3.7 %collective-permute-start.18 = (f32[2048]{0:T(1024)S(1)}, f32[2048]{0:T(1024)S(1)}, u32[]{:S(2)}, u32[]{:S(2)}) collective-permute-start(f32[2048]{0:T(1024)S(1)} %add.157), channel_id=1, source_target_pairs={{0,2},{1,3},{2,0},{3,1},{4,6},{5,7},{6,4},{7,5},{8,10},{9,11},{10,... | collective-permute-start | bytes 24584 | tf_op jit(solution)/shard_map/ppermute | solution.py:50
  102.4 5.8 %collective-permute-start.19 = (f32[2048]{0:T(1024)S(1)}, f32[2048]{0:T(1024)S(1)}, u32[]{:S(2)}, u32[]{:S(2)}) collective-permute-start(f32[2048]{0:T(1024)S(1)} %add.158), channel_id=1, source_target_pairs={{0,4},{1,5},{2,6},{3,7},{4,0},{5,1},{6,2},{7,3},{8,12},{9,13},{10,... | collective-permute-start | bytes 24584 | tf_op jit(solution)/shard_map/ppermute | solution.py:50
  106.7 14.8 %collective-permute-start.9 = (f32[4,256,64]{1,2,0:T(8,128)S(1)}, f32[4,256,64]{1,2,0:T(8,128)S(1)}, u32[]{:S(2)}, u32[]{:S(2)}) collective-permute-start(f32[4,256,64]{1,2,0:T(8,128)S(1)} %fusion.9), channel_id=1, source_target_pairs={{0,32},{32,0},{64,96},{96,64},{1,33},{33,1},{65,97},{97,65},{2,34}... | collective-permute-start | bytes 786440 | tf_op jit(solution)/shard_map/ppermute | solution.py:50
  108.2 7.6 %collective-permute-start.20 = (f32[2048]{0:T(1024)S(1)}, f32[2048]{0:T(1024)S(1)}, u32[]{:S(2)}, u32[]{:S(2)}) collective-permute-start(f32[2048]{0:T(1024)S(1)} %add.159), channel_id=1, source_target_pairs={{0,8},{1,9},{2,10},{3,11},{4,12},{5,13},{6,14},{7,15},{8,0},{9,1},... | collective-permute-start | bytes 24584 | tf_op jit(solution)/shard_map/ppermute | solution.py:50
  110.0 14.7 %collective-permute-start.6 = (bf16[256,896]{0,1:T(8,128)(2,1)S(1)}, bf16[256,896]{0,1:T(8,128)(2,1)S(1)}, u32[]{:S(2)}, u32[]{:S(2)}) collective-permute-start(bf16[256,896]{0,1:T(8,128)(2,1)S(1)} %get-tuple-element.16), channel_id=1, source_target_pairs={{0,32},{32,64},{64,96},{96,0},{1,33},{33,65},{65,97},{97,1},{2,34}... | collective-permute-start | bytes 1376264 | tf_op jit(solution)/shard_map/ppermute | solution.py:91
  111.0 27.1 %collective-permute-start.7 = (bf16[256,896]{0,1:T(8,128)(2,1)S(1)}, bf16[256,896]{0,1:T(8,128)(2,1)S(1)}, u32[]{:S(2)}, u32[]{:S(2)}) collective-permute-start(bf16[256,896]{0,1:T(8,128)(2,1)S(1)} %get-tuple-element.18), channel_id=1, source_target_pairs={{0,64},{32,96},{64,0},{96,32},{1,65},{33,97},{65,1},{97,33},{2,66}... | collective-permute-start | bytes 1376264 | tf_op jit(solution)/shard_map/ppermute | solution.py:91
  114.1 24.0 %collective-permute-start.8 = (bf16[256,896]{0,1:T(8,128)(2,1)S(1)}, bf16[256,896]{0,1:T(8,128)(2,1)S(1)}, u32[]{:S(2)}, u32[]{:S(2)}) collective-permute-start(bf16[256,896]{0,1:T(8,128)(2,1)S(1)} %get-tuple-element.17), channel_id=1, source_target_pairs={{0,96},{32,0},{64,32},{96,64},{1,97},{33,1},{65,33},{97,65},{2,98}... | collective-permute-start | bytes 1376264 | tf_op jit(solution)/shard_map/ppermute | solution.py:91
  115.8 5.2 %collective-permute-start.21 = (f32[2048]{0:T(1024)S(1)}, f32[2048]{0:T(1024)S(1)}, u32[]{:S(2)}, u32[]{:S(2)}) collective-permute-start(f32[2048]{0:T(1024)S(1)} %add.160), channel_id=1, source_target_pairs={{0,16},{1,17},{2,18},{3,19},{4,20},{5,21},{6,22},{7,23},{8,24},{9,... | collective-permute-start | bytes 24584 | tf_op jit(solution)/shard_map/ppermute | solution.py:50
  121.6 20.2 %collective-permute-start.10 = (f32[4,256,64]{1,2,0:T(8,128)S(1)}, f32[4,256,64]{1,2,0:T(8,128)S(1)}, u32[]{:S(2)}, u32[]{:S(2)}) collective-permute-start(f32[4,256,64]{1,2,0:T(8,128)S(1)} %add.153), channel_id=1, source_target_pairs={{0,64},{32,96},{64,0},{96,32},{1,65},{33,97},{65,1},{97,33},{2,66}... | collective-permute-start | bytes 786440 | tf_op jit(solution)/shard_map/ppermute | solution.py:50
Sparse Core Ops, SparseCore 0:
  10.8 58.9 all-gather.1
where the time goes:
time: 154 us
  starting transfers between devices  50.6 us (33%)
  waiting for transfers between devices  40.5 us (26%)
  matrix products  29.9 us (19%)
  local copies, waits for them, and re-layouts  17.3 us (11%)
  between operations  14.4 us (9%)
    ppermute x12, starting transfers between devices, allreduce(): v = v + lax.ppermute(v, axis, [(i, i ^ k) for i in range(n)])  31.1 us
    ppermute x3, waiting for transfers between devices, body(): lax.ppermute(sends[k - 1], 'dp', shift_pairs(n_dp, k))  15.1 us
    ppermute x6, waiting for transfers between devices, gather_dp(): piece = lax.ppermute(v, 'dp', shift_pairs(n_dp, k))  13.1 us
    ppermute x6, starting transfers between devices, gather_dp(): piece = lax.ppermute(v, 'dp', shift_pairs(n_dp, k))  12.9 us
    ppermute x12, waiting for transfers between devices, allreduce(): v = v + lax.ppermute(v, axis, [(i, i ^ k) for i in range(n)])  12.3 us
    dot_general x1, matrix products, body(): jnp.einsum('tbj,bti->ji', og_all, x_all, preferred_element_type=jnp.float32)  9.02 us
    unnamed x23, local copies, waits for them, and re-layouts  8.96 us
    dot_general x1, matrix products, body(): jnp.dot(adapter_up_factor, adapter_down_factor, preferred_element_type=jn...  6.41 us
  transfers between devices with their start and end apart: 23, of which 12 were waited for; matrix products, arithmetic and copies ran while one was open for 21% of the time, Pallas kernels for 0%

commit v1 on v0

--- a/solution.py
+++ b/solution.py
@@ -95,10 +95,11 @@
 
         product = jnp.einsum("tbj,bti->ji", og_all, x_all, preferred_element_type=jnp.float32)
         grad_scale_part = jnp.sum(product * merged, axis=1)
-        grad_scale = allreduce(grad_scale_part, "tensor", n_t)
+        grad_scale = jnp.sum(lax.all_gather(grad_scale_part, "tensor"), axis=0)
 
         w = col_scale[:, None] * adapter_up_factor.astype(jnp.float32)
-        g_all = allreduce(dot2("tbj,jr->btr", og_all, split_bf16(w)), "dp", n_dp)
+        g_part = dot2("tbj,jr->btr", og_all, split_bf16(w))
+        g_all = allreduce(g_part, "dp", n_dp)
 
         gh, gl = split_bf16(g_all)
         adapter_down_gradient = adapter_scale * (

time: 154 us -> 164 us (1.065)
  blocking collectives: 0 us -> 26.1 us
  waiting for transfers between devices: 40.5 us -> 28.8 us
  starting transfers between devices: 50.6 us -> 41.3 us
  local copies, waits for them, and re-layouts: 17.3 us -> 19.5 us
    all_gather x0 -> x1, blocking collectives: none -> 26.1 us  [body(): grad_scale = jnp.sum(lax.all_gather(grad_scale_part, 'tensor'), axis=0)]
    ppermute x3, waiting for transfers between devices: 15.1 us -> 0.01 us  [body(): lax.ppermute(sends[k - 1], 'dp', shift_pairs(n_dp, k))]
    ppermute x12 -> x7, starting transfers between devices: 31.1 us -> 22.7 us  [allreduce(): v = v + lax.ppermute(v, axis, [(i, i ^ k) for i in range(n)])]
    dot_general x1, matrix products: 9.02 us -> 4.24 us  [body(): jnp.einsum('tbj,bti->ji', og_all, x_all, preferred_element_type=jnp.float32)]
    broadcast_in_dim x6, local copies, waits for them, and re-layouts: 1.64 us -> 5.57 us  [gather_dp(): out = lax.dynamic_update_index_in_dim(out, piece, (d + n_dp - k) % n_dp, 0)]
    ppermute x12 -> x7, waiting for transfers between devices: 12.3 us -> 16.1 us  [allreduce(): v = v + lax.ppermute(v, axis, [(i, i ^ k) for i in range(n)])]
    dot_general x1, matrix products: 4.04 us -> 6.6 us  [body(): jnp.einsum('tbj,ji->bti', scaled, merged_b, preferred_element_type=jnp.fl...]
    dynamic_update_slice x6, local copies, waits for them, and re-layouts: 3.69 us -> 1.16 us  [gather_dp(): out = lax.dynamic_update_index_in_dim(out, piece, (d + n_dp - k) % n_dp, 0)]
  transfers between devices with their start and end apart: 23 -> 18, of which waited for: 12 -> 8; matrix products, arithmetic and copies ran while one was open for 21% -> 19% of each run, Pallas kernels for 0% -> 0%
where the time goes in v1:
time: 164 us; the launch traced here: 163 us
  starting transfers between devices  41.3 us (25%)
  matrix products  30.2 us (18%)
  waiting for transfers between devices  28.8 us (18%)
  blocking collectives  26.1 us (16%)
  local copies, waits for them, and re-layouts  19.5 us (12%)
  between operations  14.4 us (9%)
  other arithmetic  2.55 us (2%)
    all_gather x1, blocking collectives, body(): grad_scale = jnp.sum(lax.all_gather(grad_scale_part, 'tensor'), axis=0)  26.1 us
    ppermute x7, starting transfers between devices, allreduce(): v = v + lax.ppermute(v, axis, [(i, i ^ k) for i in range(n)])  22.7 us
    ppermute x7, waiting for transfers between devices, allreduce(): v = v + lax.ppermute(v, axis, [(i, i ^ k) for i in range(n)])  16.1 us
    ppermute x6, waiting for transfers between devices, gather_dp(): piece = lax.ppermute(v, 'dp', shift_pairs(n_dp, k))  12.7 us
    ppermute x6, starting transfers between devices, gather_dp(): piece = lax.ppermute(v, 'dp', shift_pairs(n_dp, k))  12.6 us
    unnamed x21, local copies, waits for them, and re-layouts  9.86 us
    dot_general x1, matrix products, body(): jnp.einsum('tbj,ji->bti', scaled, merged_b, preferred_element_type=jnp.fl...  6.6 us
    dot_general x1, matrix products, body(): jnp.dot(adapter_up_factor, adapter_down_factor, preferred_element_type=jn...  6.43 us
  transfers between devices with their start and end apart: 18, of which 8 were waited for; matrix products, arithmetic and copies ran while one was open for 19% of the time, Pallas kernels for 0%

profile of v1, /device:TPU:0, one launch (start us, length us, event | category | flops | bytes accessed | tf_op | source)
XLA Modules:
  0.0 163.0 jit_solution(13319496968577207743)
XLA Ops:
  7.2 0.0 copy-start
  7.2 0.0 all-gather.3.cloned.1.call-start
  7.2 1.0 copy.59
  8.2 0.0 copy-start.2
  8.2 0.8 collective-permute-start
  9.1 0.0 copy-start.5
  9.1 0.6 copy-done.5
  9.7 0.0 all-gather.3.cloned.1.call-update
  9.7 6.2 %copy.58 = bf16[2048,896]{0,1:T(8,128)(2,1)} copy(bf16[2048,896]{1,0:T(8,128)(2,1)} %param.8) | data formatting | bytes 7340032 | tf_op args[2]
  15.9 1.3 fusion.32
  17.2 0.1 reshape.30
  17.3 6.4 %multiply_reduce_fusion = (f32[2048]{0:T(1024)S(1)}, f32[2048,896]{0,1:T(8,128)}) fusion(bf16[2048,64]{0,1:T(8,128)(2,1)S(1)} %copy-done.2, bf16[64,896]{1,0:T(8,128)(2,1)S(1)} %copy-done, bf16[2048,896]{0,1:T(8,128)(2,1)} %copy.58), kind=kOutput, calls=%fused_computation.3 | convolution fusion | flops 244054016 | bytes 11395072 | tf_op jit(solution)/shard_map/dot_general | solution.py:68
  23.7 0.1 collective-permute-start.1
  23.8 1.3 collective-permute-done.1
  25.1 1.8 %collective-permute-start.2 = (f32[18432]{0:T(1024)S(1)}, f32[18432]{0:T(1024)S(1)}, u32[]{:S(2)}, u32[]{:S(2)}) collective-permute-start(f32[18432]{0:T(1024)S(1)} %fusion.31), channel_id=1, source_target_pairs={{0,2},{1,3},{2,0},{3,1},{4,6},{5,7},{6,4},{7,5},{8,10},{9,11},{10,... | collective-permute-start | bytes 221192 | tf_op jit(solution)/shard_map/ppermute | solution.py:50
  26.9 2.7 %collective-permute-done.2 = f32[18432]{0:T(1024)S(1)} collective-permute-done((f32[18432]{0:T(1024)S(1)}, f32[18432]{0:T(1024)S(1)}, u32[]{:S(2)}, u32[]{:S(2)}) %collective-permute-start.2) | collective-permute-done | bytes 73760 | tf_op jit(solution)/shard_map/ppermute | solution.py:50
  29.5 3.4 %collective-permute-start.3 = (f32[18432]{0:T(1024)S(1)}, f32[18432]{0:T(1024)S(1)}, u32[]{:S(2)}, u32[]{:S(2)}) collective-permute-start(f32[18432]{0:T(1024)S(1)} %add.117), channel_id=1, source_target_pairs={{0,4},{1,5},{2,6},{3,7},{4,0},{5,1},{6,2},{7,3},{8,12},{9,13},{10,... | collective-permute-start | bytes 221192 | tf_op jit(solution)/shard_map/ppermute | solution.py:50
  32.9 2.6 %collective-permute-done.3 = f32[18432]{0:T(1024)S(1)} collective-permute-done((f32[18432]{0:T(1024)S(1)}, f32[18432]{0:T(1024)S(1)}, u32[]{:S(2)}, u32[]{:S(2)}) %collective-permute-start.3) | collective-permute-done | bytes 73760 | tf_op jit(solution)/shard_map/ppermute | solution.py:50
  35.5 9.7 %collective-permute-start.4 = (f32[18432]{0:T(1024)S(1)}, f32[18432]{0:T(1024)S(1)}, u32[]{:S(2)}, u32[]{:S(2)}) collective-permute-start(f32[18432]{0:T(1024)S(1)} %add.118), channel_id=1, source_target_pairs={{0,8},{1,9},{2,10},{3,11},{4,12},{5,13},{6,14},{7,15},{8,0},{9,1},... | collective-permute-start | bytes 221192 | tf_op jit(solution)/shard_map/ppermute | solution.py:50
  45.2 8.4 %collective-permute-start.12 = (bf16[256,896]{1,0:T(8,128)(2,1)}, bf16[256,896]{1,0:T(8,128)(2,1)S(1)}, u32[]{:S(2)}, u32[]{:S(2)}) collective-permute-start(bf16[256,896]{1,0:T(8,128)(2,1)} %param.6), channel_id=1, source_target_pairs={{0,64},{32,96},{64,0},{96,32},{1,65},{33,97},{65,1},{97,33},{2,66}... | collective-permute-start | bytes 1376264 | tf_op jit(solution)/shard_map/ppermute | solution.py:42
  53.6 0.7 collective-permute-start.13
  54.4 1.3 copy.64
  55.7 3.1 %collective-permute-start.5 = (f32[18432]{0:T(1024)S(1)}, f32[18432]{0:T(1024)S(1)}, u32[]{:S(2)}, u32[]{:S(2)}) collective-permute-start(f32[18432]{0:T(1024)S(1)} %add.119), channel_id=1, source_target_pairs={{0,16},{1,17},{2,18},{3,19},{4,20},{5,21},{6,22},{7,23},{8,24},{9,... | collective-permute-start | bytes 221192 | tf_op jit(solution)/shard_map/ppermute | solution.py:50
  58.8 0.1 broadcast_in_dim.35
  59.0 4.0 %collective-permute-done.5 = f32[18432]{0:T(1024)S(1)} collective-permute-done((f32[18432]{0:T(1024)S(1)}, f32[18432]{0:T(1024)S(1)}, u32[]{:S(2)}, u32[]{:S(2)}) %collective-permute-start.5) | collective-permute-done | bytes 73760 | tf_op jit(solution)/shard_map/ppermute | solution.py:50
  63.0 0.1 broadcast_in_dim.41
  63.1 0.1 slice.18
  63.2 0.6 collective-permute-start.14
  63.8 1.5 collective-permute-start.15
  65.3 0.1 copy.70
  65.4 10.2 %collective-permute-done.14 = f32[256,64]{1,0:T(8,128)} collective-permute-done((f32[256,64]{1,0:T(8,128)S(1)}, f32[256,64]{1,0:T(8,128)}, u32[]{:S(2)}, u32[]{:S(2)}) %collective-permute-start.14) | collective-permute-done | bytes 65568 | tf_op jit(solution)/shard_map/ppermute | solution.py:42
  75.6 1.4 collective-permute-start.16
  77.0 1.0 copy.71
  78.0 0.1 copy.72
  78.1 2.5 %collective-permute-done.16 = f32[256,64]{1,0:T(8,128)S(1)} collective-permute-done((f32[256,64]{1,0:T(8,128)S(1)}, f32[256,64]{1,0:T(8,128)S(1)}, u32[]{:S(2)}, u32[]{:S(2)}) %collective-permute-start.16) | collective-permute-done | bytes 65568 | tf_op jit(solution)/shard_map/ppermute | solution.py:42
  80.6 0.1 copy.73
  80.8 1.2 copy.65
  82.0 0.0 copy-start.4
  82.0 0.8 copy-done.4
  82.8 1.2 copy.66
  84.0 2.0 %copy.67 = bf16[1,256,896]{1,2,0:T(8,128)(2,1)} copy(bf16[1,256,896]{2,1,0:T(8,128)(2,1)} %bitcast.16) | data formatting | bytes 917504 | tf_op jit(solution)/shard_map/jit(dynamic_update_index_in_dim)/broadcast_in_dim | solution.py:43
  86.1 1.1 constant_dynamic-update-slice_fusion.4
  87.1 0.0 all-gather.3.cloned.1.call-done
  87.2 3.1 %fusion.22 = f32[64,256,4]{1,0,2:T(8,128)S(1)} fusion(bf16[256,4,2048]{0,2,1:T(8,128)(2,1)} %bitcast.81, bf16[2048,64]{0,1:T(8,128)(2,1)S(1)} %copy-done.2, f32[2048]{0:T(1024)S(1)} %get-tuple-element.6), kind=kOutput, calls=%fused_computation.36 | convolution fusion | flops 269221888 | bytes 4726784 | tf_op jit(solution)/shard_map/tbj,jr->btr/dot_general | solution.py:19
  90.3 0.3 copy-done.1
  90.6 6.6 %fusion.1 = f32[896,256,4]{1,0,2:T(8,128)S(1)} fusion(bf16[256,4,2048]{0,2,1:T(8,128)(2,1)S(1)} %bitcast.83, f32[2048]{0:T(1024)S(1)} %get-tuple-element.6, f32[2048,896]{0,1:T(8,128)} %get-tuple-element.30), kind=kOutput, calls=%fused_computation.5 | convolution fusion | flops 3766222848 | bytes 15212544 | tf_op jit(solution)/shard_map/tbj,ji->bti/dot_general | solution.py:84
  97.3 4.2 %fusion = f32[2048]{0:T(1024)S(1)} fusion(f32[2048,896]{0,1:T(8,128)S(1)} %bitcast.88, bf16[4,256,896]{1,2,0:T(8,128)(2,1)S(1)} %constant_dynamic-update-slice_fusion.4, bf16[256,4,2048]{0,2,1:T(8,128)(2,1)S(1)} %bitcast.84), kind=kOutput, calls=%fused_computation.2 | convolution fusion | flops 3761764352 | bytes 13377536 | tf_op jit(solution)/shard_map/tbj,bti->ji/dot_general | solution.py:96
  101.5 0.8 fusion.9
  102.3 1.1 fusion.16
  103.4 0.5 collective-permute-start.6
  103.9 3.6 %collective-permute-start.7 = (bf16[256,896]{0,1:T(8,128)(2,1)}, bf16[256,896]{0,1:T(8,128)(2,1)}, u32[]{:S(2)}, u32[]{:S(2)}) collective-permute-start(bf16[256,896]{0,1:T(8,128)(2,1)} %get-tuple-element.26), channel_id=1, source_target_pairs={{0,64},{32,96},{64,0},{96,32},{1,65},{33,97},{65,1},{97,33},{2,66}... | collective-permute-start | bytes 1376264 | tf_op jit(solution)/shard_map/ppermute | solution.py:91
  107.5 1.1 collective-permute-start.8
  108.6 1.4 convolution_bitcast_fusion
  110.0 26.1 %all-gather = f32[65536]{0:T(1024)S(1)} all-gather(f32[2048]{0:T(1024)S(1)} %fusion), channel_id=2, replica_groups=mesh['dp'=4,'tensor'=32] {'tensor'}, dimensions={0}, use_global_device_ids=true | all-gather | bytes 270336 | tf_op jit(solution)/shard_map/all_gather | solution.py:98
  136.1 1.5 collective-permute-start.9
  137.7 0.6 div.7
  138.3 4.4 %fusion.8 = f32[2048,64]{0,1:T(8,128)} fusion(f32[64,2048]{1,0:T(8,128)S(1)} %convolution_bitcast_fusion, bf16[256,4,2048]{0,2,1:T(8,128)(2,1)} %bitcast.82, f32[2048]{0:T(1024)S(1)} %get-tuple-element.6, f32[4,256,64]{1,2,0:T(8,128)S(1)} %constant_dynamic-update-slice_fusion), kind=kOutput, calls=%fused_computation.14 | convolution fusion | flops 268894208 | bytes 5513216 | tf_op jit(solution)/shard_map/tbj,btr->jr/dot_general | solution.py:19
  142.6 2.1 %collective-permute-done.9 = f32[4,256,64]{1,2,0:T(8,128)S(1)} collective-permute-done((f32[4,256,64]{1,2,0:T(8,128)S(1)}, f32[4,256,64]{1,2,0:T(8,128)S(1)}, u32[]{:S(2)}, u32[]{:S(2)}) %collective-permute-start.9) | collective-permute-done | bytes 262176 | tf_op jit(solution)/shard_map/ppermute | solution.py:50
  144.8 3.0 %collective-permute-start.10 = (f32[4,256,64]{1,2,0:T(8,128)S(1)}, f32[4,256,64]{1,2,0:T(8,128)S(1)}, u32[]{:S(2)}, u32[]{:S(2)}) collective-permute-start(f32[4,256,64]{1,2,0:T(8,128)S(1)} %add.138), channel_id=1, source_target_pairs={{0,64},{32,96},{64,0},{96,32},{1,65},{33,97},{65,1},{97,33},{2,66}... | collective-permute-start | bytes 786440 | tf_op jit(solution)/shard_map/ppermute | solution.py:50
  147.8 1.8 %fusion.14 = bf16[256,896]{0,1:T(8,128)(2,1)S(1)} fusion(bf16[256,896]{0,1:T(8,128)(2,1)} %collective-permute-done.8, bf16[256,896]{0,1:T(8,128)(2,1)} %collective-permute-done.7, bf16[256,896]{0,1:T(8,128)(2,1)} %collective-permute-done.6, f32[896,256,4]{1,0,2:T(8,128)} %copy-done.3, s32[]{:T(128)S(6)} %select_n.50), kind=kLoop, calls=%fused_computation.24 | loop fusion | flops 1605632 | bytes 2752516 | tf_op jit(solution)/shard_map/convert_element_type | solution.py:94
  149.6 1.0 copy.77
  150.6 3.5 %collective-permute-done.10 = f32[4,256,64]{1,2,0:T(8,128)S(1)} collective-permute-done((f32[4,256,64]{1,2,0:T(8,128)S(1)}, f32[4,256,64]{1,2,0:T(8,128)S(1)}, u32[]{:S(2)}, u32[]{:S(2)}) %collective-permute-start.10) | collective-permute-done | bytes 262176 | tf_op jit(solution)/shard_map/ppermute | solution.py:50
  154.1 0.7 convolution_bitcast_fusion.2
  154.8 1.4 fusion.11
  (41 shorter events, 0.4 us)
Async XLA Ops:
  7.2 8.7 %copy-start = (bf16[64,896]{1,0:T(8,128)(2,1)S(1)}, bf16[64,896]{1,0:T(8,128)(2,1)}, u32[]{:S(2)}) copy-start(bf16[64,896]{1,0:T(8,128)(2,1)} %param.9) | copy-start | bytes 344068
  7.2 80.0 %all-gather.3.cloned.1.call-start = ((), (), s32[]{:S(2)}) async-start(), calls=%async_computation | async-start | bytes 4325376 | tf_op jit(solution)/shard_map/all_gather | solution.py:65
  8.2 9.1 %copy-start.2 = (bf16[2048,64]{0,1:T(8,128)(2,1)S(1)}, bf16[2048,64]{0,1:T(8,128)(2,1)}, u32[]{:S(2)}) copy-start(bf16[2048,64]{0,1:T(8,128)(2,1)} %param.10) | copy-start | bytes 786436
  8.2 0.8 collective-permute-start
  9.1 0.7 copy-start.5
  23.7 41.6 %copy-start.6 = (f32[2048]{0:T(1024)S(1)}, f32[2048]{0:T(1024)}, u32[]{:S(2)}) copy-start(f32[2048]{0:T(1024)} %param.11) | copy-start | bytes 24580
  23.7 1.3 collective-permute-start.1
  25.1 4.4 %collective-permute-start.2 = (f32[18432]{0:T(1024)S(1)}, f32[18432]{0:T(1024)S(1)}, u32[]{:S(2)}, u32[]{:S(2)}) collective-permute-start(f32[18432]{0:T(1024)S(1)} %fusion.31), channel_id=1, source_target_pairs={{0,2},{1,3},{2,0},{3,1},{4,6},{5,7},{6,4},{7,5},{8,10},{9,11},{10,... | collective-permute-start | bytes 221192 | tf_op jit(solution)/shard_map/ppermute | solution.py:50
  29.5 5.9 %collective-permute-start.3 = (f32[18432]{0:T(1024)S(1)}, f32[18432]{0:T(1024)S(1)}, u32[]{:S(2)}, u32[]{:S(2)}) collective-permute-start(f32[18432]{0:T(1024)S(1)} %add.117), channel_id=1, source_target_pairs={{0,4},{1,5},{2,6},{3,7},{4,0},{5,1},{6,2},{7,3},{8,12},{9,13},{10,... | collective-permute-start | bytes 221192 | tf_op jit(solution)/shard_map/ppermute | solution.py:50
  35.5 20.1 %collective-permute-start.4 = (f32[18432]{0:T(1024)S(1)}, f32[18432]{0:T(1024)S(1)}, u32[]{:S(2)}, u32[]{:S(2)}) collective-permute-start(f32[18432]{0:T(1024)S(1)} %add.118), channel_id=1, source_target_pairs={{0,8},{1,9},{2,10},{3,11},{4,12},{5,13},{6,14},{7,15},{8,0},{9,1},... | collective-permute-start | bytes 221192 | tf_op jit(solution)/shard_map/ppermute | solution.py:50
  45.2 35.5 %collective-permute-start.11 = (bf16[256,896]{1,0:T(8,128)(2,1)}, bf16[256,896]{1,0:T(8,128)(2,1)}, u32[]{:S(2)}, u32[]{:S(2)}) collective-permute-start(bf16[256,896]{1,0:T(8,128)(2,1)} %param.6), channel_id=1, source_target_pairs={{0,32},{32,64},{64,96},{96,0},{1,33},{33,65},{65,97},{97,1},{2,34}... | collective-permute-start | bytes 1376264 | tf_op jit(solution)/shard_map/ppermute | solution.py:42
  45.2 36.7 %collective-permute-start.12 = (bf16[256,896]{1,0:T(8,128)(2,1)}, bf16[256,896]{1,0:T(8,128)(2,1)S(1)}, u32[]{:S(2)}, u32[]{:S(2)}) collective-permute-start(bf16[256,896]{1,0:T(8,128)(2,1)} %param.6), channel_id=1, source_target_pairs={{0,64},{32,96},{64,0},{96,32},{1,65},{33,97},{65,1},{97,33},{2,66}... | collective-permute-start | bytes 1376264 | tf_op jit(solution)/shard_map/ppermute | solution.py:42
  53.6 30.3 %collective-permute-start.13 = (bf16[256,896]{1,0:T(8,128)(2,1)}, bf16[256,896]{1,0:T(8,128)(2,1)}, u32[]{:S(2)}, u32[]{:S(2)}) collective-permute-start(bf16[256,896]{1,0:T(8,128)(2,1)} %param.6), channel_id=1, source_target_pairs={{0,96},{32,0},{64,32},{96,64},{1,97},{33,1},{65,33},{97,65},{2,98}... | collective-permute-start | bytes 1376264 | tf_op jit(solution)/shard_map/ppermute | solution.py:42
  55.7 7.3 %collective-permute-start.5 = (f32[18432]{0:T(1024)S(1)}, f32[18432]{0:T(1024)S(1)}, u32[]{:S(2)}, u32[]{:S(2)}) collective-permute-start(f32[18432]{0:T(1024)S(1)} %add.119), channel_id=1, source_target_pairs={{0,16},{1,17},{2,18},{3,19},{4,20},{5,21},{6,22},{7,23},{8,24},{9,... | collective-permute-start | bytes 221192 | tf_op jit(solution)/shard_map/ppermute | solution.py:50
  63.2 12.5 %collective-permute-start.14 = (f32[256,64]{1,0:T(8,128)S(1)}, f32[256,64]{1,0:T(8,128)}, u32[]{:S(2)}, u32[]{:S(2)}) collective-permute-start(f32[256,64]{1,0:T(8,128)S(1)} %slice.18), channel_id=1, source_target_pairs={{0,32},{32,64},{64,96},{96,0},{1,33},{33,65},{65,97},{97,1},{2,34}... | collective-permute-start | bytes 196616 | tf_op jit(solution)/shard_map/ppermute | solution.py:42
  63.8 14.3 %collective-permute-start.15 = (f32[256,64]{1,0:T(8,128)S(1)}, f32[256,64]{1,0:T(8,128)S(1)}, u32[]{:S(2)}, u32[]{:S(2)}) collective-permute-start(f32[256,64]{1,0:T(8,128)S(1)} %slice.18), channel_id=1, source_target_pairs={{0,64},{32,96},{64,0},{96,32},{1,65},{33,97},{65,1},{97,33},{2,66}... | collective-permute-start | bytes 196616 | tf_op jit(solution)/shard_map/ppermute | solution.py:42
  75.6 5.0 %collective-permute-start.16 = (f32[256,64]{1,0:T(8,128)S(1)}, f32[256,64]{1,0:T(8,128)S(1)}, u32[]{:S(2)}, u32[]{:S(2)}) collective-permute-start(f32[256,64]{1,0:T(8,128)S(1)} %slice.18), channel_id=1, source_target_pairs={{0,96},{32,0},{64,32},{96,64},{1,97},{33,1},{65,33},{97,65},{2,98}... | collective-permute-start | bytes 196616 | tf_op jit(solution)/shard_map/ppermute | solution.py:42
  82.0 0.8 copy-start.4
  87.2 3.5 %copy-start.1 = (bf16[256,8192]{0,1:T(8,128)(2,1)S(1)}, bf16[256,8192]{0,1:T(8,128)(2,1)}, u32[]{:S(2)}) copy-start(bf16[256,8192]{0,1:T(8,128)(2,1)} %all-gather.3.cloned.1.call-done) | copy-start | bytes 12582916
  87.2 10.1 %slice-start = ((s8[7340032]{0:T(1024)(128)(4,1)}), s8[4194304]{0:T(1024)(128)(4,1)S(1)}, s32[]{:S(2)}) async-start(s8[7340032]{0:T(1024)(128)(4,1)} %bitcast.87), calls=%async_computation.1 | async-start | bytes 8388608
  90.6 6.6 %slice-start.1 = ((s8[7340032]{0:T(1024)(128)(4,1)}), s8[3145728]{0:T(1024)(128)(4,1)S(1)}, s32[]{:S(2)}) async-start(s8[7340032]{0:T(1024)(128)(4,1)} %bitcast.87), calls=%async_computation.2 | async-start | bytes 6291456
  97.2 5.1 %copy-start.3 = (f32[896,256,4]{1,0,2:T(8,128)}, f32[896,256,4]{1,0,2:T(8,128)S(1)}, u32[]{:S(2)}) copy-start(f32[896,256,4]{1,0,2:T(8,128)S(1)} %fusion.1) | copy-start | bytes 11010052
  103.4 44.4 %collective-permute-start.6 = (bf16[256,896]{0,1:T(8,128)(2,1)}, bf16[256,896]{0,1:T(8,128)(2,1)}, u32[]{:S(2)}, u32[]{:S(2)}) collective-permute-start(bf16[256,896]{0,1:T(8,128)(2,1)} %get-tuple-element.24), channel_id=1, source_target_pairs={{0,32},{32,64},{64,96},{96,0},{1,33},{33,65},{65,97},{97,1},{2,34}... | collective-permute-start | bytes 1376264 | tf_op jit(solution)/shard_map/ppermute | solution.py:91
  103.9 43.9 %collective-permute-start.7 = (bf16[256,896]{0,1:T(8,128)(2,1)}, bf16[256,896]{0,1:T(8,128)(2,1)}, u32[]{:S(2)}, u32[]{:S(2)}) collective-permute-start(bf16[256,896]{0,1:T(8,128)(2,1)} %get-tuple-element.26), channel_id=1, source_target_pairs={{0,64},{32,96},{64,0},{96,32},{1,65},{33,97},{65,1},{97,33},{2,66}... | collective-permute-start | bytes 1376264 | tf_op jit(solution)/shard_map/ppermute | solution.py:91
  107.5 40.3 %collective-permute-start.8 = (bf16[256,896]{0,1:T(8,128)(2,1)}, bf16[256,896]{0,1:T(8,128)(2,1)}, u32[]{:S(2)}, u32[]{:S(2)}) collective-permute-start(bf16[256,896]{0,1:T(8,128)(2,1)} %get-tuple-element.25), channel_id=1, source_target_pairs={{0,96},{32,0},{64,32},{96,64},{1,97},{33,1},{65,33},{97,65},{2,98}... | collective-permute-start | bytes 1376264 | tf_op jit(solution)/shard_map/ppermute | solution.py:91
  136.1 8.6 %collective-permute-start.9 = (f32[4,256,64]{1,2,0:T(8,128)S(1)}, f32[4,256,64]{1,2,0:T(8,128)S(1)}, u32[]{:S(2)}, u32[]{:S(2)}) collective-permute-start(f32[4,256,64]{1,2,0:T(8,128)S(1)} %fusion.9), channel_id=1, source_target_pairs={{0,32},{32,0},{64,96},{96,64},{1,33},{33,1},{65,97},{97,65},{2,34}... | collective-permute-start | bytes 786440 | tf_op jit(solution)/shard_map/ppermute | solution.py:50
  144.8 9.3 %collective-permute-start.10 = (f32[4,256,64]{1,2,0:T(8,128)S(1)}, f32[4,256,64]{1,2,0:T(8,128)S(1)}, u32[]{:S(2)}, u32[]{:S(2)}) collective-permute-start(f32[4,256,64]{1,2,0:T(8,128)S(1)} %add.138), channel_id=1, source_target_pairs={{0,64},{32,96},{64,0},{96,32},{1,65},{33,97},{65,1},{97,33},{2,66}... | collective-permute-start | bytes 786440 | tf_op jit(solution)/shard_map/ppermute | solution.py:50
Sparse Core Ops, SparseCore 0:
  10.8 59.4 all-gather.2

commit v2 on v1

--- a/solution.py
+++ b/solution.py
@@ -47,7 +47,8 @@
 def allreduce(v, axis, n):
     k = 1
     while k < n:
-        v = v + lax.ppermute(v, axis, [(i, i ^ k) for i in range(n)])
+        other = lax.ppermute(v, axis, [(i, i ^ k) for i in range(n)])
+        v = v + other
         k *= 2
     return v
 
@@ -95,7 +96,7 @@
 
         product = jnp.einsum("tbj,bti->ji", og_all, x_all, preferred_element_type=jnp.float32)
         grad_scale_part = jnp.sum(product * merged, axis=1)
-        grad_scale = jnp.sum(lax.all_gather(grad_scale_part, "tensor"), axis=0)
+        grad_scale = allreduce(grad_scale_part, "tensor", n_t)
 
         w = col_scale[:, None] * adapter_up_factor.astype(jnp.float32)
         g_part = dot2("tbj,jr->btr", og_all, split_bf16(w))

time: 164 us -> 154 us (0.939)
  blocking collectives: 26.1 us -> 0 us
  waiting for transfers between devices: 28.8 us -> 40.5 us
  starting transfers between devices: 41.3 us -> 50.6 us
  local copies, waits for them, and re-layouts: 19.5 us -> 17.3 us
    all_gather x1 -> x0, blocking collectives: 26.1 us -> none  [body(): grad_scale = jnp.sum(lax.all_gather(grad_scale_part, 'tensor'), axis=0)]
    ppermute x3, waiting for transfers between devices: 0.01 us -> 15.1 us  [body(): lax.ppermute(sends[k - 1], 'dp', shift_pairs(n_dp, k))]
    ppermute x7 -> x12, starting transfers between devices: 22.7 us -> 31.1 us  [allreduce(): other = lax.ppermute(v, axis, [(i, i ^ k) for i in range(n)])]
    dot_general x1, matrix products: 4.24 us -> 9.02 us  [body(): jnp.einsum('tbj,bti->ji', og_all, x_all, preferred_element_type=jnp.float32)]
    broadcast_in_dim x6, local copies, waits for them, and re-layouts: 5.57 us -> 1.64 us  [gather_dp(): out = lax.dynamic_update_index_in_dim(out, piece, (d + n_dp - k) % n_dp, 0)]
    ppermute x7 -> x12, waiting for transfers between devices: 16.1 us -> 12.3 us  [allreduce(): other = lax.ppermute(v, axis, [(i, i ^ k) for i in range(n)])]
    dot_general x1, matrix products: 6.6 us -> 4.04 us  [body(): jnp.einsum('tbj,ji->bti', scaled, merged_b, preferred_element_type=jnp.fl...]
    dynamic_update_slice x6, local copies, waits for them, and re-layouts: 1.16 us -> 3.69 us  [gather_dp(): out = lax.dynamic_update_index_in_dim(out, piece, (d + n_dp - k) % n_dp, 0)]
  transfers between devices with their start and end apart: 18 -> 23, of which waited for: 8 -> 12; matrix products, arithmetic and copies ran while one was open for 19% -> 21% of each run, Pallas kernels for 0% -> 0%
where the time goes in v2:
time: 154 us
  starting transfers between devices  50.6 us (33%)
  waiting for transfers between devices  40.5 us (26%)
  matrix products  29.9 us (19%)
  local copies, waits for them, and re-layouts  17.3 us (11%)
  between operations  14.4 us (9%)
    ppermute x12, starting transfers between devices, allreduce(): other = lax.ppermute(v, axis, [(i, i ^ k) for i in range(n)])  31.1 us
    ppermute x3, waiting for transfers between devices, body(): lax.ppermute(sends[k - 1], 'dp', shift_pairs(n_dp, k))  15.1 us
    ppermute x6, waiting for transfers between devices, gather_dp(): piece = lax.ppermute(v, 'dp', shift_pairs(n_dp, k))  13.1 us
    ppermute x6, starting transfers between devices, gather_dp(): piece = lax.ppermute(v, 'dp', shift_pairs(n_dp, k))  12.9 us
    ppermute x12, waiting for transfers between devices, allreduce(): other = lax.ppermute(v, axis, [(i, i ^ k) for i in range(n)])  12.3 us
    dot_general x1, matrix products, body(): jnp.einsum('tbj,bti->ji', og_all, x_all, preferred_element_type=jnp.float32)  9.02 us
    unnamed x23, local copies, waits for them, and re-layouts  8.96 us
    dot_general x1, matrix products, body(): jnp.dot(adapter_up_factor, adapter_down_factor, preferred_element_type=jn...  6.41 us
  transfers between devices with their start and end apart: 23, of which 12 were waited for; matrix products, arithmetic and copies ran while one was open for 21% of the time, Pallas kernels for 0%

profile of v2, /device:TPU:0, one launch (start us, length us, event | category | flops | bytes accessed | tf_op | source)
XLA Modules:
  0.0 153.6 jit_solution(8122471330108340522)
XLA Ops:
  7.2 1.1 copy.19
  8.3 0.8 collective-permute-start
  9.1 0.6 copy-done.6
  9.8 6.2 %copy.18 = bf16[2048,896]{0,1:T(8,128)(2,1)} copy(bf16[2048,896]{1,0:T(8,128)(2,1)} %param.8) | data formatting | bytes 7340032 | tf_op args[2]
  16.0 0.3 fusion.32
  16.3 0.1 reshape.30
  16.4 6.4 %multiply_reduce_fusion = (f32[2048]{0:T(1024)S(1)}, f32[2048,896]{0,1:T(8,128)}) fusion(bf16[2048,64]{0,1:T(8,128)(2,1)S(1)} %copy-done.2, bf16[64,896]{1,0:T(8,128)(2,1)S(1)} %copy-done, bf16[2048,896]{0,1:T(8,128)(2,1)} %copy.18), kind=kOutput, calls=%fused_computation.3 | convolution fusion | flops 244054016 | bytes 11395072 | tf_op jit(solution)/shard_map/dot_general | solution.py:69
  22.8 0.1 collective-permute-start.1
  22.9 1.3 collective-permute-done.1
  24.2 1.8 %collective-permute-start.2 = (f32[18432]{0:T(1024)S(1)}, f32[18432]{0:T(1024)S(1)}, u32[]{:S(2)}, u32[]{:S(2)}) collective-permute-start(f32[18432]{0:T(1024)S(1)} %fusion.31), channel_id=1, source_target_pairs={{0,2},{1,3},{2,0},{3,1},{4,6},{5,7},{6,4},{7,5},{8,10},{9,11},{10,... | collective-permute-start | bytes 221192 | tf_op jit(solution)/shard_map/ppermute | solution.py:50
  26.0 2.7 %collective-permute-done.2 = f32[18432]{0:T(1024)S(1)} collective-permute-done((f32[18432]{0:T(1024)S(1)}, f32[18432]{0:T(1024)S(1)}, u32[]{:S(2)}, u32[]{:S(2)}) %collective-permute-start.2) | collective-permute-done | bytes 73760 | tf_op jit(solution)/shard_map/ppermute | solution.py:50
  28.6 3.4 %collective-permute-start.3 = (f32[18432]{0:T(1024)S(1)}, f32[18432]{0:T(1024)S(1)}, u32[]{:S(2)}, u32[]{:S(2)}) collective-permute-start(f32[18432]{0:T(1024)S(1)} %add.132), channel_id=1, source_target_pairs={{0,4},{1,5},{2,6},{3,7},{4,0},{5,1},{6,2},{7,3},{8,12},{9,13},{10,... | collective-permute-start | bytes 221192 | tf_op jit(solution)/shard_map/ppermute | solution.py:50
  32.0 2.6 %collective-permute-done.3 = f32[18432]{0:T(1024)S(1)} collective-permute-done((f32[18432]{0:T(1024)S(1)}, f32[18432]{0:T(1024)S(1)}, u32[]{:S(2)}, u32[]{:S(2)}) %collective-permute-start.3) | collective-permute-done | bytes 73760 | tf_op jit(solution)/shard_map/ppermute | solution.py:50
  34.6 10.4 %collective-permute-start.4 = (f32[18432]{0:T(1024)S(1)}, f32[18432]{0:T(1024)S(1)}, u32[]{:S(2)}, u32[]{:S(2)}) collective-permute-start(f32[18432]{0:T(1024)S(1)} %add.133), channel_id=1, source_target_pairs={{0,8},{1,9},{2,10},{3,11},{4,12},{5,13},{6,14},{7,15},{8,0},{9,1},... | collective-permute-start | bytes 221192 | tf_op jit(solution)/shard_map/ppermute | solution.py:50
  45.0 8.0 %collective-permute-start.12 = (bf16[256,896]{1,0:T(8,128)(2,1)S(1)}, bf16[256,896]{1,0:T(8,128)(2,1)S(1)}, u32[]{:S(2)}, u32[]{:S(2)}) collective-permute-start(bf16[256,896]{1,0:T(8,128)(2,1)S(1)} %copy-done.5), channel_id=1, source_target_pairs={{0,64},{32,96},{64,0},{96,32},{1,65},{33,97},{65,1},{97,33},{2,66}... | collective-permute-start | bytes 1376264 | tf_op jit(solution)/shard_map/ppermute | solution.py:42
  53.0 0.4 collective-permute-start.13
  53.4 0.2 copy.24
  53.7 3.0 %collective-permute-start.5 = (f32[18432]{0:T(1024)S(1)}, f32[18432]{0:T(1024)S(1)}, u32[]{:S(2)}, u32[]{:S(2)}) collective-permute-start(f32[18432]{0:T(1024)S(1)} %add.134), channel_id=1, source_target_pairs={{0,16},{1,17},{2,18},{3,19},{4,20},{5,21},{6,22},{7,23},{8,24},{9,... | collective-permute-start | bytes 221192 | tf_op jit(solution)/shard_map/ppermute | solution.py:50
  56.7 1.5 broadcast_in_dim.35
  58.1 0.8 constant_dynamic-update-slice_fusion.7
  58.9 2.2 %collective-permute-done.5 = f32[18432]{0:T(1024)S(1)} collective-permute-done((f32[18432]{0:T(1024)S(1)}, f32[18432]{0:T(1024)S(1)}, u32[]{:S(2)}, u32[]{:S(2)}) %collective-permute-start.5) | collective-permute-done | bytes 73760 | tf_op jit(solution)/shard_map/ppermute | solution.py:50
  61.1 0.1 broadcast_in_dim.41
  61.2 0.1 slice.18
  61.3 1.0 collective-permute-start.14
  62.3 1.7 %collective-permute-start.15 = (f32[256,64]{1,0:T(8,128)S(1)}, f32[256,64]{1,0:T(8,128)S(1)}, u32[]{:S(2)}, u32[]{:S(2)}) collective-permute-start(f32[256,64]{1,0:T(8,128)S(1)} %slice.18), channel_id=1, source_target_pairs={{0,64},{32,96},{64,0},{96,32},{1,65},{33,97},{65,1},{97,33},{2,66}... | collective-permute-start | bytes 196616 | tf_op jit(solution)/shard_map/ppermute | solution.py:42
  64.0 0.1 copy.30
  64.1 10.1 %collective-permute-done.14 = f32[256,64]{1,0:T(8,128)S(1)} collective-permute-done((f32[256,64]{1,0:T(8,128)S(1)}, f32[256,64]{1,0:T(8,128)S(1)}, u32[]{:S(2)}, u32[]{:S(2)}) %collective-permute-start.14) | collective-permute-done | bytes 65568 | tf_op jit(solution)/shard_map/ppermute | solution.py:42
  74.2 1.8 %collective-permute-start.16 = (f32[256,64]{1,0:T(8,128)S(1)}, f32[256,64]{1,0:T(8,128)S(1)}, u32[]{:S(2)}, u32[]{:S(2)}) collective-permute-start(f32[256,64]{1,0:T(8,128)S(1)} %slice.18), channel_id=1, source_target_pairs={{0,96},{32,0},{64,32},{96,64},{1,97},{33,1},{65,33},{97,65},{2,98}... | collective-permute-start | bytes 196616 | tf_op jit(solution)/shard_map/ppermute | solution.py:42
  76.0 0.1 copy.31
  76.1 0.7 collective-permute-done.15
  76.8 0.1 copy.32
  76.9 2.3 %collective-permute-done.16 = f32[256,64]{1,0:T(8,128)S(1)} collective-permute-done((f32[256,64]{1,0:T(8,128)S(1)}, f32[256,64]{1,0:T(8,128)S(1)}, u32[]{:S(2)}, u32[]{:S(2)}) %collective-permute-start.16) | collective-permute-done | bytes 65568 | tf_op jit(solution)/shard_map/ppermute | solution.py:42
  79.3 0.2 copy.25
  79.5 0.2 copy.26
  79.8 1.0 copy.27
  80.7 0.8 constant_dynamic-update-slice_fusion.6
  81.6 0.9 constant_dynamic-update-slice_fusion.5
  82.4 2.0 %constant_dynamic-update-slice_fusion.4 = bf16[4,256,896]{1,2,0:T(8,128)(2,1)} fusion(bf16[4,256,896]{1,2,0:T(8,128)(2,1)} %constant_dynamic-update-slice_fusion.5, bf16[1,256,896]{1,2,0:T(8,128)(2,1)} %copy.27, s32[]{:T(128)S(6)} %select_n.52), kind=kLoop, calls=%fused_computation.53 | loop fusion | bytes 917508 | tf_op jit(solution)/shard_map/jit(dynamic_update_index_in_dim)/dynamic_update_slice | solution.py:43
  84.4 9.0 %fusion = f32[2048]{0:T(1024)S(1)} fusion(f32[2048,896]{0,1:T(8,128)} %get-tuple-element.22, bf16[4,256,896]{1,2,0:T(8,128)(2,1)} %constant_dynamic-update-slice_fusion.4, bf16[256,4,2048]{0,2,1:T(8,128)(2,1)} %bitcast.81), kind=kOutput, calls=%fused_computation.2 | convolution fusion | flops 3761764352 | bytes 13377536 | tf_op jit(solution)/shard_map/tbj,bti->ji/dot_general | solution.py:97
  93.4 0.3 collective-permute-start.17
  93.8 4.0 %fusion.1 = f32[896,256,4]{1,0,2:T(8,128)S(1)} fusion(bf16[256,4,2048]{0,2,1:T(8,128)(2,1)S(1)} %bitcast.82, f32[2048]{0:T(1024)S(1)} %get-tuple-element.6, f32[2048,896]{0,1:T(8,128)S(1)} %bitcast.88), kind=kOutput, calls=%fused_computation.5 | convolution fusion | flops 3766222848 | bytes 15212544 | tf_op jit(solution)/shard_map/tbj,ji->bti/dot_general | solution.py:85
  97.8 0.8 fusion.22
  98.6 1.8 %collective-permute-start.18 = (f32[2048]{0:T(1024)S(1)}, f32[2048]{0:T(1024)S(1)}, u32[]{:S(2)}, u32[]{:S(2)}) collective-permute-start(f32[2048]{0:T(1024)S(1)} %add.157), channel_id=1, source_target_pairs={{0,2},{1,3},{2,0},{3,1},{4,6},{5,7},{6,4},{7,5},{8,10},{9,11},{10,... | collective-permute-start | bytes 24584 | tf_op jit(solution)/shard_map/ppermute | solution.py:50
  100.5 0.8 fusion.9
  101.3 1.1 collective-permute-done.18
  102.4 3.0 %collective-permute-start.19 = (f32[2048]{0:T(1024)S(1)}, f32[2048]{0:T(1024)S(1)}, u32[]{:S(2)}, u32[]{:S(2)}) collective-permute-start(f32[2048]{0:T(1024)S(1)} %add.158), channel_id=1, source_target_pairs={{0,4},{1,5},{2,6},{3,7},{4,0},{5,1},{6,2},{7,3},{8,12},{9,13},{10,... | collective-permute-start | bytes 24584 | tf_op jit(solution)/shard_map/ppermute | solution.py:50
  105.3 1.4 convolution_bitcast_fusion
  106.7 1.5 collective-permute-start.9
  108.2 1.7 %collective-permute-start.20 = (f32[2048]{0:T(1024)S(1)}, f32[2048]{0:T(1024)S(1)}, u32[]{:S(2)}, u32[]{:S(2)}) collective-permute-start(f32[2048]{0:T(1024)S(1)} %add.159), channel_id=1, source_target_pairs={{0,8},{1,9},{2,10},{3,11},{4,12},{5,13},{6,14},{7,15},{8,0},{9,1},... | collective-permute-start | bytes 24584 | tf_op jit(solution)/shard_map/ppermute | solution.py:50
  109.9 0.1 fusion.16
  110.0 1.0 collective-permute-start.6
  111.0 3.1 %collective-permute-start.7 = (bf16[256,896]{0,1:T(8,128)(2,1)S(1)}, bf16[256,896]{0,1:T(8,128)(2,1)S(1)}, u32[]{:S(2)}, u32[]{:S(2)}) collective-permute-start(bf16[256,896]{0,1:T(8,128)(2,1)S(1)} %get-tuple-element.18), channel_id=1, source_target_pairs={{0,64},{32,96},{64,0},{96,32},{1,65},{33,97},{65,1},{97,33},{2,66}... | collective-permute-start | bytes 1376264 | tf_op jit(solution)/shard_map/ppermute | solution.py:92
  114.1 1.7 %collective-permute-start.8 = (bf16[256,896]{0,1:T(8,128)(2,1)S(1)}, bf16[256,896]{0,1:T(8,128)(2,1)S(1)}, u32[]{:S(2)}, u32[]{:S(2)}) collective-permute-start(bf16[256,896]{0,1:T(8,128)(2,1)S(1)} %get-tuple-element.17), channel_id=1, source_target_pairs={{0,96},{32,0},{64,32},{96,64},{1,97},{33,1},{65,33},{97,65},{2,98}... | collective-permute-start | bytes 1376264 | tf_op jit(solution)/shard_map/ppermute | solution.py:92
  115.8 2.9 %collective-permute-start.21 = (f32[2048]{0:T(1024)S(1)}, f32[2048]{0:T(1024)S(1)}, u32[]{:S(2)}, u32[]{:S(2)}) collective-permute-start(f32[2048]{0:T(1024)S(1)} %add.160), channel_id=1, source_target_pairs={{0,16},{1,17},{2,18},{3,19},{4,20},{5,21},{6,22},{7,23},{8,24},{9,... | collective-permute-start | bytes 24584 | tf_op jit(solution)/shard_map/ppermute | solution.py:50
  118.7 2.2 %fusion.8 = f32[2048,64]{0,1:T(8,128)} fusion(f32[64,2048]{1,0:T(8,128)S(1)} %convolution_bitcast_fusion, bf16[256,4,2048]{0,2,1:T(8,128)(2,1)S(1)} %bitcast.86, f32[2048]{0:T(1024)S(1)} %get-tuple-element.6, f32[4,256,64]{1,2,0:T(8,128)S(1)} %copy-done.4), kind=kOutput, calls=%fused_computation.14 | convolution fusion | flops 268894208 | bytes 5513216 | tf_op jit(solution)/shard_map/tbj,btr->jr/dot_general | solution.py:19
  120.9 0.6 add_divide_fusion
  121.6 1.4 collective-permute-start.10
  123.0 1.7 %collective-permute-done.6 = bf16[256,896]{0,1:T(8,128)(2,1)S(1)} collective-permute-done((bf16[256,896]{0,1:T(8,128)(2,1)S(1)}, bf16[256,896]{0,1:T(8,128)(2,1)S(1)}, u32[]{:S(2)}, u32[]{:S(2)}) %collective-permute-start.6) | collective-permute-done | bytes 458784 | tf_op jit(solution)/shard_map/ppermute | solution.py:92
  124.7 13.4 %collective-permute-done.7 = bf16[256,896]{0,1:T(8,128)(2,1)S(1)} collective-permute-done((bf16[256,896]{0,1:T(8,128)(2,1)S(1)}, bf16[256,896]{0,1:T(8,128)(2,1)S(1)}, u32[]{:S(2)}, u32[]{:S(2)}) %collective-permute-start.7) | collective-permute-done | bytes 458784 | tf_op jit(solution)/shard_map/ppermute | solution.py:92
  138.1 0.2 fusion.14
  138.3 1.0 copy.37
  139.3 2.5 %collective-permute-done.10 = f32[4,256,64]{1,2,0:T(8,128)S(1)} collective-permute-done((f32[4,256,64]{1,2,0:T(8,128)S(1)}, f32[4,256,64]{1,2,0:T(8,128)S(1)}, u32[]{:S(2)}, u32[]{:S(2)}) %collective-permute-start.10) | collective-permute-done | bytes 262176 | tf_op jit(solution)/shard_map/ppermute | solution.py:50
  141.8 2.2 %convolution_bitcast_fusion.2 = f32[64,896]{1,0:T(8,128)S(1)} fusion(bf16[4,256,896]{1,2,0:T(8,128)(2,1)} %constant_dynamic-update-slice_fusion.4, f32[4,256,64]{1,2,0:T(8,128)S(1)} %add.153, f32[4,256,64]{1,2,0:T(8,128)S(1)} %collective-permute-done.10), kind=kOutput, calls=%fused_computation.17 | convolution fusion | flops 117768192 | bytes 2588672 | tf_op jit(solution)/shard_map/btr,bti->ri/dot_general | solution.py:108
  143.9 2.9 %fusion.11 = f32[64,896]{1,0:T(8,128)} fusion(f32[64,896]{1,0:T(8,128)S(1)} %convolution_bitcast_fusion.2, bf16[4,256,896]{1,2,0:T(8,128)(2,1)} %constant_dynamic-update-slice_fusion.4, f32[4,256,64]{1,2,0:T(8,128)S(1)} %add.153, f32[4,256,64]{1,2,0:T(8,128)S(1)} %collective-permute-done.10), kind=kOutput, calls=%fused_computation.20 | convolution fusion | flops 117686272 | bytes 2818048 | tf_op jit(solution)/shard_map/btr,bti->ri/dot_general | solution.py:107
  (54 shorter events, 0.5 us)
Async XLA Ops:
  7.2 8.9 %copy-start = (bf16[64,896]{1,0:T(8,128)(2,1)S(1)}, bf16[64,896]{1,0:T(8,128)(2,1)}, u32[]{:S(2)}) copy-start(bf16[64,896]{1,0:T(8,128)(2,1)} %param.9) | copy-start | bytes 344068
  7.2 8.9 %copy-start.5 = (bf16[256,896]{1,0:T(8,128)(2,1)S(1)}, bf16[256,896]{1,0:T(8,128)(2,1)}, u32[]{:S(2)}) copy-start(bf16[256,896]{1,0:T(8,128)(2,1)} %param.6) | copy-start | bytes 1376260
  7.2 77.2 %all-gather.2.cloned.1.call-start = ((), (), s32[]{:S(2)}) async-start(), calls=%async_computation | async-start | bytes 4325376 | tf_op jit(solution)/shard_map/all_gather | solution.py:66
  8.3 8.1 %copy-start.2 = (bf16[2048,64]{0,1:T(8,128)(2,1)S(1)}, bf16[2048,64]{0,1:T(8,128)(2,1)}, u32[]{:S(2)}) copy-start(bf16[2048,64]{0,1:T(8,128)(2,1)} %param.10) | copy-start | bytes 786436
  8.3 0.8 collective-permute-start
  9.1 0.7 copy-start.6
  22.8 41.2 %copy-start.7 = (f32[2048]{0:T(1024)S(1)}, f32[2048]{0:T(1024)}, u32[]{:S(2)}) copy-start(f32[2048]{0:T(1024)} %param.11) | copy-start | bytes 24580
  22.8 1.3 collective-permute-start.1
  24.2 4.4 %collective-permute-start.2 = (f32[18432]{0:T(1024)S(1)}, f32[18432]{0:T(1024)S(1)}, u32[]{:S(2)}, u32[]{:S(2)}) collective-permute-start(f32[18432]{0:T(1024)S(1)} %fusion.31), channel_id=1, source_target_pairs={{0,2},{1,3},{2,0},{3,1},{4,6},{5,7},{6,4},{7,5},{8,10},{9,11},{10,... | collective-permute-start | bytes 221192 | tf_op jit(solution)/shard_map/ppermute | solution.py:50
  28.6 5.9 %collective-permute-start.3 = (f32[18432]{0:T(1024)S(1)}, f32[18432]{0:T(1024)S(1)}, u32[]{:S(2)}, u32[]{:S(2)}) collective-permute-start(f32[18432]{0:T(1024)S(1)} %add.132), channel_id=1, source_target_pairs={{0,4},{1,5},{2,6},{3,7},{4,0},{5,1},{6,2},{7,3},{8,12},{9,13},{10,... | collective-permute-start | bytes 221192 | tf_op jit(solution)/shard_map/ppermute | solution.py:50
  34.6 19.0 %collective-permute-start.4 = (f32[18432]{0:T(1024)S(1)}, f32[18432]{0:T(1024)S(1)}, u32[]{:S(2)}, u32[]{:S(2)}) collective-permute-start(f32[18432]{0:T(1024)S(1)} %add.133), channel_id=1, source_target_pairs={{0,8},{1,9},{2,10},{3,11},{4,12},{5,13},{6,14},{7,15},{8,0},{9,1},... | collective-permute-start | bytes 221192 | tf_op jit(solution)/shard_map/ppermute | solution.py:50
  45.0 34.3 %collective-permute-start.11 = (bf16[256,896]{1,0:T(8,128)(2,1)S(1)}, bf16[256,896]{1,0:T(8,128)(2,1)S(1)}, u32[]{:S(2)}, u32[]{:S(2)}) collective-permute-start(bf16[256,896]{1,0:T(8,128)(2,1)S(1)} %copy-done.5), channel_id=1, source_target_pairs={{0,32},{32,64},{64,96},{96,0},{1,33},{33,65},{65,97},{97,1},{2,34}... | collective-permute-start | bytes 1376264 | tf_op jit(solution)/shard_map/ppermute | solution.py:42
  45.0 34.5 %collective-permute-start.12 = (bf16[256,896]{1,0:T(8,128)(2,1)S(1)}, bf16[256,896]{1,0:T(8,128)(2,1)S(1)}, u32[]{:S(2)}, u32[]{:S(2)}) collective-permute-start(bf16[256,896]{1,0:T(8,128)(2,1)S(1)} %copy-done.5), channel_id=1, source_target_pairs={{0,64},{32,96},{64,0},{96,32},{1,65},{33,97},{65,1},{97,33},{2,66}... | collective-permute-start | bytes 1376264 | tf_op jit(solution)/shard_map/ppermute | solution.py:42
  53.0 26.7 %collective-permute-start.13 = (bf16[256,896]{1,0:T(8,128)(2,1)S(1)}, bf16[256,896]{1,0:T(8,128)(2,1)S(1)}, u32[]{:S(2)}, u32[]{:S(2)}) collective-permute-start(bf16[256,896]{1,0:T(8,128)(2,1)S(1)} %copy-done.5), channel_id=1, source_target_pairs={{0,96},{32,0},{64,32},{96,64},{1,97},{33,1},{65,33},{97,65},{2,98}... | collective-permute-start | bytes 1376264 | tf_op jit(solution)/shard_map/ppermute | solution.py:42
  53.7 7.5 %collective-permute-start.5 = (f32[18432]{0:T(1024)S(1)}, f32[18432]{0:T(1024)S(1)}, u32[]{:S(2)}, u32[]{:S(2)}) collective-permute-start(f32[18432]{0:T(1024)S(1)} %add.134), channel_id=1, source_target_pairs={{0,16},{1,17},{2,18},{3,19},{4,20},{5,21},{6,22},{7,23},{8,24},{9,... | collective-permute-start | bytes 221192 | tf_op jit(solution)/shard_map/ppermute | solution.py:50
  61.3 12.9 %collective-permute-start.14 = (f32[256,64]{1,0:T(8,128)S(1)}, f32[256,64]{1,0:T(8,128)S(1)}, u32[]{:S(2)}, u32[]{:S(2)}) collective-permute-start(f32[256,64]{1,0:T(8,128)S(1)} %slice.18), channel_id=1, source_target_pairs={{0,32},{32,64},{64,96},{96,0},{1,33},{33,65},{65,97},{97,1},{2,34}... | collective-permute-start | bytes 196616 | tf_op jit(solution)/shard_map/ppermute | solution.py:42
  62.3 14.5 %collective-permute-start.15 = (f32[256,64]{1,0:T(8,128)S(1)}, f32[256,64]{1,0:T(8,128)S(1)}, u32[]{:S(2)}, u32[]{:S(2)}) collective-permute-start(f32[256,64]{1,0:T(8,128)S(1)} %slice.18), channel_id=1, source_target_pairs={{0,64},{32,96},{64,0},{96,32},{1,65},{33,97},{65,1},{97,33},{2,66}... | collective-permute-start | bytes 196616 | tf_op jit(solution)/shard_map/ppermute | solution.py:42
  74.2 5.0 %collective-permute-start.16 = (f32[256,64]{1,0:T(8,128)S(1)}, f32[256,64]{1,0:T(8,128)S(1)}, u32[]{:S(2)}, u32[]{:S(2)}) collective-permute-start(f32[256,64]{1,0:T(8,128)S(1)} %slice.18), channel_id=1, source_target_pairs={{0,96},{32,0},{64,32},{96,64},{1,97},{33,1},{65,33},{97,65},{2,98}... | collective-permute-start | bytes 196616 | tf_op jit(solution)/shard_map/ppermute | solution.py:42
  79.3 2.3 %copy-start.3 = (f32[4,256,64]{1,2,0:T(8,128)}, f32[4,256,64]{1,2,0:T(8,128)S(1)}, u32[]{:S(2)}) copy-start(f32[4,256,64]{1,2,0:T(8,128)S(1)} %constant_dynamic-update-slice_fusion) | copy-start | bytes 786436
  82.4 11.3 %slice-start = ((s8[7340032]{0:T(1024)(128)(4,1)}), s8[3145728]{0:T(1024)(128)(4,1)S(1)}, s32[]{:S(2)}) async-start(s8[7340032]{0:T(1024)(128)(4,1)} %bitcast.87), calls=%async_computation.1 | async-start | bytes 6291456
  84.4 9.3 %copy-start.1 = (bf16[256,8192]{0,1:T(8,128)(2,1)S(1)}, bf16[256,8192]{0,1:T(8,128)(2,1)}, u32[]{:S(2)}) copy-start(bf16[256,8192]{0,1:T(8,128)(2,1)} %all-gather.2.cloned.1.call-done) | copy-start | bytes 12582916
  84.4 9.3 %slice-start.1 = ((s8[7340032]{0:T(1024)(128)(4,1)}), s8[4194304]{0:T(1024)(128)(4,1)S(1)}, s32[]{:S(2)}) async-start(s8[7340032]{0:T(1024)(128)(4,1)} %bitcast.87), calls=%async_computation.2 | async-start | bytes 8388608
  93.4 5.2 %collective-permute-start.17 = (f32[2048]{0:T(1024)S(1)}, f32[2048]{0:T(1024)S(1)}, u32[]{:S(2)}, u32[]{:S(2)}) collective-permute-start(f32[2048]{0:T(1024)S(1)} %fusion), channel_id=1, source_target_pairs={{0,1},{1,0},{2,3},{3,2},{4,5},{5,4},{6,7},{7,6},{8,9},{9,8},{10,11... | collective-permute-start | bytes 24584 | tf_op jit(solution)/shard_map/ppermute | solution.py:50
  97.8 7.5 %copy-start.4 = (f32[4,256,64]{1,2,0:T(8,128)S(1)}, f32[4,256,64]{1,2,0:T(8,128)}, u32[]{:S(2)}) copy-start(f32[4,256,64]{1,2,0:T(8,128)} %copy-done.3) | copy-start | bytes 786436
  98.6 3.7 %collective-permute-start.18 = (f32[2048]{0:T(1024)S(1)}, f32[2048]{0:T(1024)S(1)}, u32[]{:S(2)}, u32[]{:S(2)}) collective-permute-start(f32[2048]{0:T(1024)S(1)} %add.157), channel_id=1, source_target_pairs={{0,2},{1,3},{2,0},{3,1},{4,6},{5,7},{6,4},{7,5},{8,10},{9,11},{10,... | collective-permute-start | bytes 24584 | tf_op jit(solution)/shard_map/ppermute | solution.py:50
  102.4 5.8 %collective-permute-start.19 = (f32[2048]{0:T(1024)S(1)}, f32[2048]{0:T(1024)S(1)}, u32[]{:S(2)}, u32[]{:S(2)}) collective-permute-start(f32[2048]{0:T(1024)S(1)} %add.158), channel_id=1, source_target_pairs={{0,4},{1,5},{2,6},{3,7},{4,0},{5,1},{6,2},{7,3},{8,12},{9,13},{10,... | collective-permute-start | bytes 24584 | tf_op jit(solution)/shard_map/ppermute | solution.py:50
  106.7 14.8 %collective-permute-start.9 = (f32[4,256,64]{1,2,0:T(8,128)S(1)}, f32[4,256,64]{1,2,0:T(8,128)S(1)}, u32[]{:S(2)}, u32[]{:S(2)}) collective-permute-start(f32[4,256,64]{1,2,0:T(8,128)S(1)} %fusion.9), channel_id=1, source_target_pairs={{0,32},{32,0},{64,96},{96,64},{1,33},{33,1},{65,97},{97,65},{2,34}... | collective-permute-start | bytes 786440 | tf_op jit(solution)/shard_map/ppermute | solution.py:50
  108.2 7.6 %collective-permute-start.20 = (f32[2048]{0:T(1024)S(1)}, f32[2048]{0:T(1024)S(1)}, u32[]{:S(2)}, u32[]{:S(2)}) collective-permute-start(f32[2048]{0:T(1024)S(1)} %add.159), channel_id=1, source_target_pairs={{0,8},{1,9},{2,10},{3,11},{4,12},{5,13},{6,14},{7,15},{8,0},{9,1},... | collective-permute-start | bytes 24584 | tf_op jit(solution)/shard_map/ppermute | solution.py:50
  110.0 14.7 %collective-permute-start.6 = (bf16[256,896]{0,1:T(8,128)(2,1)S(1)}, bf16[256,896]{0,1:T(8,128)(2,1)S(1)}, u32[]{:S(2)}, u32[]{:S(2)}) collective-permute-start(bf16[256,896]{0,1:T(8,128)(2,1)S(1)} %get-tuple-element.16), channel_id=1, source_target_pairs={{0,32},{32,64},{64,96},{96,0},{1,33},{33,65},{65,97},{97,1},{2,34}... | collective-permute-start | bytes 1376264 | tf_op jit(solution)/shard_map/ppermute | solution.py:92
  111.0 27.1 %collective-permute-start.7 = (bf16[256,896]{0,1:T(8,128)(2,1)S(1)}, bf16[256,896]{0,1:T(8,128)(2,1)S(1)}, u32[]{:S(2)}, u32[]{:S(2)}) collective-permute-start(bf16[256,896]{0,1:T(8,128)(2,1)S(1)} %get-tuple-element.18), channel_id=1, source_target_pairs={{0,64},{32,96},{64,0},{96,32},{1,65},{33,97},{65,1},{97,33},{2,66}... | collective-permute-start | bytes 1376264 | tf_op jit(solution)/shard_map/ppermute | solution.py:92
  114.1 24.0 %collective-permute-start.8 = (bf16[256,896]{0,1:T(8,128)(2,1)S(1)}, bf16[256,896]{0,1:T(8,128)(2,1)S(1)}, u32[]{:S(2)}, u32[]{:S(2)}) collective-permute-start(bf16[256,896]{0,1:T(8,128)(2,1)S(1)} %get-tuple-element.17), channel_id=1, source_target_pairs={{0,96},{32,0},{64,32},{96,64},{1,97},{33,1},{65,33},{97,65},{2,98}... | collective-permute-start | bytes 1376264 | tf_op jit(solution)/shard_map/ppermute | solution.py:92
  115.8 5.2 %collective-permute-start.21 = (f32[2048]{0:T(1024)S(1)}, f32[2048]{0:T(1024)S(1)}, u32[]{:S(2)}, u32[]{:S(2)}) collective-permute-start(f32[2048]{0:T(1024)S(1)} %add.160), channel_id=1, source_target_pairs={{0,16},{1,17},{2,18},{3,19},{4,20},{5,21},{6,22},{7,23},{8,24},{9,... | collective-permute-start | bytes 24584 | tf_op jit(solution)/shard_map/ppermute | solution.py:50
  121.6 20.2 %collective-permute-start.10 = (f32[4,256,64]{1,2,0:T(8,128)S(1)}, f32[4,256,64]{1,2,0:T(8,128)S(1)}, u32[]{:S(2)}, u32[]{:S(2)}) collective-permute-start(f32[4,256,64]{1,2,0:T(8,128)S(1)} %add.153), channel_id=1, source_target_pairs={{0,64},{32,96},{64,0},{96,32},{1,65},{33,97},{65,1},{97,33},{2,66}... | collective-permute-start | bytes 786440 | tf_op jit(solution)/shard_map/ppermute | solution.py:50
Sparse Core Ops, SparseCore 0:
  10.8 58.9 all-gather.1

commit v3 on v1

--- a/solution.py
+++ b/solution.py
@@ -81,12 +81,13 @@
         col_scale, weight_row_norm = lax.optimization_barrier((col_scale, weight_row_norm))
 
         scaled = (og_all.astype(jnp.float32) * col_scale).astype(jnp.bfloat16)
-        ig_part = jnp.einsum("tbj,ji->bti", scaled, merged_b, preferred_element_type=jnp.float32)
-        own = lax.dynamic_index_in_dim(ig_part, d, 0, keepdims=False)
-        sends = [
-            lax.dynamic_index_in_dim(ig_part, (d + k) % n_dp, 0, keepdims=False).astype(jnp.bfloat16)
-            for k in range(1, n_dp)
-        ]
+
+        def ig_for(group):
+            block = lax.dynamic_index_in_dim(scaled, group, 1, keepdims=False)
+            return jnp.dot(block, merged_b, preferred_element_type=jnp.float32)
+
+        sends = [ig_for((d + k) % n_dp).astype(jnp.bfloat16) for k in range(1, n_dp)]
+        own = ig_for(d)
         acc = own
         received = [lax.ppermute(sends[k - 1], "dp", shift_pairs(n_dp, k)) for k in range(1, n_dp)]
         for piece in received:
@@ -95,7 +96,7 @@
 
         product = jnp.einsum("tbj,bti->ji", og_all, x_all, preferred_element_type=jnp.float32)
         grad_scale_part = jnp.sum(product * merged, axis=1)
-        grad_scale = jnp.sum(lax.all_gather(grad_scale_part, "tensor"), axis=0)
+        grad_scale = allreduce(grad_scale_part, "tensor", n_t)
 
         w = col_scale[:, None] * adapter_up_factor.astype(jnp.float32)
         g_part = dot2("tbj,jr->btr", og_all, split_bf16(w))

time: 164 us -> 156 us (0.951)
  blocking collectives: 26.1 us -> 0 us
  waiting for transfers between devices: 28.8 us -> 43.6 us
  starting transfers between devices: 41.3 us -> 48.2 us
  matrix products: 30.2 us -> 26.6 us
    all_gather x1 -> x0, blocking collectives: 26.1 us -> none  [body(): grad_scale = jnp.sum(lax.all_gather(grad_scale_part, 'tensor'), axis=0)]
    ppermute x3, waiting for transfers between devices: 0.01 us -> 16.7 us  [body(): lax.ppermute(sends[k - 1], 'dp', shift_pairs(n_dp, k))]
    ppermute x7 -> x12, starting transfers between devices: 22.7 us -> 29.4 us  [allreduce(): v = v + lax.ppermute(v, axis, [(i, i ^ k) for i in range(n)])]
    dot_general x2, matrix products: 4.51 us -> 2.16 us  [dot2(): jnp.einsum(spec, a, lo, preferred_element_type=jnp.float32)]
    dot_general x2, matrix products: 5.16 us -> 2.98 us  [dot2(): jnp.einsum(spec, a, hi, preferred_element_type=jnp.float32)]
    ppermute x7 -> x12, waiting for transfers between devices: 16.1 us -> 14.4 us  [allreduce(): v = v + lax.ppermute(v, axis, [(i, i ^ k) for i in range(n)])]
    dot_general x1 -> x4, matrix products: 6.6 us -> 6.12 us  [ig_for(): return jnp.dot(block, merged_b, preferred_element_type=jnp.float32)]
    unnamed x21 -> x20, local copies, waits for them, and re-layouts: 9.86 us -> 9.92 us
  transfers between devices with their start and end apart: 18 -> 23, of which waited for: 8 -> 11; matrix products, arithmetic and copies ran while one was open for 19% -> 21% of each run, Pallas kernels for 0% -> 0%
where the time goes in v3:
time: 156 us; the launch traced here: 155 us
  starting transfers between devices  48.2 us (31%)
  waiting for transfers between devices  43.6 us (28%)
  matrix products  26.6 us (17%)
  local copies, waits for them, and re-layouts  18.4 us (12%)
  between operations  14.5 us (9%)
  other arithmetic  3.81 us (2%)
    ppermute x12, starting transfers between devices, allreduce(): v = v + lax.ppermute(v, axis, [(i, i ^ k) for i in range(n)])  29.4 us
    ppermute x3, waiting for transfers between devices, body(): lax.ppermute(sends[k - 1], 'dp', shift_pairs(n_dp, k))  16.7 us
    ppermute x12, waiting for transfers between devices, allreduce(): v = v + lax.ppermute(v, axis, [(i, i ^ k) for i in range(n)])  14.4 us
    ppermute x6, waiting for transfers between devices, gather_dp(): piece = lax.ppermute(v, 'dp', shift_pairs(n_dp, k))  12.4 us
    ppermute x6, starting transfers between devices, gather_dp(): piece = lax.ppermute(v, 'dp', shift_pairs(n_dp, k))  12.2 us
    unnamed x20, local copies, waits for them, and re-layouts  9.92 us
    dot_general x1, matrix products, body(): jnp.dot(adapter_up_factor, adapter_down_factor, preferred_element_type=jn...  7.77 us
    dot_general x4, matrix products, ig_for(): return jnp.dot(block, merged_b, preferred_element_type=jnp.float32)  6.12 us
  transfers between devices with their start and end apart: 23, of which 11 were waited for; matrix products, arithmetic and copies ran while one was open for 21% of the time, Pallas kernels for 0%

profile of v3, /device:TPU:0, one launch (start us, length us, event | category | flops | bytes accessed | tf_op | source)
XLA Modules:
  0.0 155.1 jit_solution(16528783837222495719)
XLA Ops:
  7.2 1.0 copy.17
  8.2 0.8 collective-permute-start
  9.1 0.6 copy-done.5
  9.7 6.2 %copy.18 = bf16[2048,896]{0,1:T(8,128)(2,1)} copy(bf16[2048,896]{1,0:T(8,128)(2,1)} %param.8) | data formatting | bytes 7340032 | tf_op args[2]
  16.0 1.3 fusion.47
  17.3 0.1 reshape.27
  17.4 7.8 %multiply_reduce_fusion = (f32[2048]{0:T(1024)S(1)}, bf16[2048,896]{0,1:T(8,128)(2,1)}, f32[2048,896]{0,1:T(8,128)}) fusion(bf16[2048,64]{0,1:T(8,128)(2,1)S(1)} %copy-done.3, bf16[64,896]{1,0:T(8,128)(2,1)S(1)} %copy-done, bf16[2048,896]{0,1:T(8,128)(2,1)} %copy.18), kind=kOutput, calls=%fused_computation.3 | convolution fusion | flops 245889024 | bytes 15065088 | tf_op jit(solution)/shard_map/dot_general | solution.py:68
  25.1 0.1 collective-permute-start.1
  25.2 1.3 collective-permute-done.1
  26.5 1.8 %collective-permute-start.2 = (f32[18432]{0:T(1024)S(1)}, f32[18432]{0:T(1024)S(1)}, u32[]{:S(2)}, u32[]{:S(2)}) collective-permute-start(f32[18432]{0:T(1024)S(1)} %fusion.46), channel_id=1, source_target_pairs={{0,2},{1,3},{2,0},{3,1},{4,6},{5,7},{6,4},{7,5},{8,10},{9,11},{10,... | collective-permute-start | bytes 221192 | tf_op jit(solution)/shard_map/ppermute | solution.py:50
  28.3 2.7 %collective-permute-done.2 = f32[18432]{0:T(1024)S(1)} collective-permute-done((f32[18432]{0:T(1024)S(1)}, f32[18432]{0:T(1024)S(1)}, u32[]{:S(2)}, u32[]{:S(2)}) %collective-permute-start.2) | collective-permute-done | bytes 73760 | tf_op jit(solution)/shard_map/ppermute | solution.py:50
  31.0 3.4 %collective-permute-start.3 = (f32[18432]{0:T(1024)S(1)}, f32[18432]{0:T(1024)S(1)}, u32[]{:S(2)}, u32[]{:S(2)}) collective-permute-start(f32[18432]{0:T(1024)S(1)} %add.132), channel_id=1, source_target_pairs={{0,4},{1,5},{2,6},{3,7},{4,0},{5,1},{6,2},{7,3},{8,12},{9,13},{10,... | collective-permute-start | bytes 221192 | tf_op jit(solution)/shard_map/ppermute | solution.py:50
  34.3 3.2 %collective-permute-done.3 = f32[18432]{0:T(1024)S(1)} collective-permute-done((f32[18432]{0:T(1024)S(1)}, f32[18432]{0:T(1024)S(1)}, u32[]{:S(2)}, u32[]{:S(2)}) %collective-permute-start.3) | collective-permute-done | bytes 73760 | tf_op jit(solution)/shard_map/ppermute | solution.py:50
  37.5 9.6 %collective-permute-start.4 = (f32[18432]{0:T(1024)S(1)}, f32[18432]{0:T(1024)S(1)}, u32[]{:S(2)}, u32[]{:S(2)}) collective-permute-start(f32[18432]{0:T(1024)S(1)} %add.133), channel_id=1, source_target_pairs={{0,8},{1,9},{2,10},{3,11},{4,12},{5,13},{6,14},{7,15},{8,0},{9,1},... | collective-permute-start | bytes 221192 | tf_op jit(solution)/shard_map/ppermute | solution.py:50
  47.1 8.0 %collective-permute-start.12 = (bf16[256,896]{1,0:T(8,128)(2,1)}, bf16[256,896]{1,0:T(8,128)(2,1)S(1)}, u32[]{:S(2)}, u32[]{:S(2)}) collective-permute-start(bf16[256,896]{1,0:T(8,128)(2,1)} %param.6), channel_id=1, source_target_pairs={{0,64},{32,96},{64,0},{96,32},{1,65},{33,97},{65,1},{97,33},{2,66}... | collective-permute-start | bytes 1376264 | tf_op jit(solution)/shard_map/ppermute | solution.py:42
  55.1 0.6 collective-permute-start.13
  55.7 1.3 copy.22
  57.0 2.9 %collective-permute-start.5 = (f32[18432]{0:T(1024)S(1)}, f32[18432]{0:T(1024)S(1)}, u32[]{:S(2)}, u32[]{:S(2)}) collective-permute-start(f32[18432]{0:T(1024)S(1)} %add.134), channel_id=1, source_target_pairs={{0,16},{1,17},{2,18},{3,19},{4,20},{5,21},{6,22},{7,23},{8,24},{9,... | collective-permute-start | bytes 221192 | tf_op jit(solution)/shard_map/ppermute | solution.py:50
  59.9 0.1 broadcast_in_dim.35
  60.1 4.3 %collective-permute-done.5 = f32[18432]{0:T(1024)S(1)} collective-permute-done((f32[18432]{0:T(1024)S(1)}, f32[18432]{0:T(1024)S(1)}, u32[]{:S(2)}, u32[]{:S(2)}) %collective-permute-start.5) | collective-permute-done | bytes 73760 | tf_op jit(solution)/shard_map/ppermute | solution.py:50
  64.4 0.1 broadcast_in_dim.41
  64.5 0.1 slice.18
  64.6 1.4 collective-permute-start.14
  66.0 0.8 collective-permute-start.15
  66.8 0.1 copy.28
  66.9 10.0 %collective-permute-done.14 = f32[256,64]{1,0:T(8,128)} collective-permute-done((f32[256,64]{1,0:T(8,128)S(1)}, f32[256,64]{1,0:T(8,128)}, u32[]{:S(2)}, u32[]{:S(2)}) %collective-permute-start.14) | collective-permute-done | bytes 65568 | tf_op jit(solution)/shard_map/ppermute | solution.py:42
  76.8 1.4 collective-permute-start.16
  78.3 1.0 copy.29
  79.4 2.4 %collective-permute-done.16 = f32[256,64]{1,0:T(8,128)S(1)} collective-permute-done((f32[256,64]{1,0:T(8,128)S(1)}, f32[256,64]{1,0:T(8,128)S(1)}, u32[]{:S(2)}, u32[]{:S(2)}) %collective-permute-start.16) | collective-permute-done | bytes 65568 | tf_op jit(solution)/shard_map/ppermute | solution.py:42
  82.0 1.2 copy.23
  83.2 0.8 copy-done.4
  84.0 1.2 copy.24
  85.2 2.0 %copy.25 = bf16[1,256,896]{1,2,0:T(8,128)(2,1)} copy(bf16[1,256,896]{2,1,0:T(8,128)(2,1)} %bitcast.11) | data formatting | bytes 917504 | tf_op jit(solution)/shard_map/jit(dynamic_update_index_in_dim)/broadcast_in_dim | solution.py:43
  87.3 1.1 constant_dynamic-update-slice_fusion.4
  88.4 3.1 %multiply_convert_fusion = bf16[256,4,2048]{0,2,1:T(8,128)(2,1)S(1)} fusion(f32[2048]{0:T(1024)S(1)} %get-tuple-element.6, bf16[256,8192]{0,1:T(8,128)(2,1)} %all-gather.2.cloned.1.call-done), kind=kLoop, calls=%fused_computation | loop fusion | flops 6291456 | bytes 8396800 | tf_op jit(solution)/shard_map/convert_element_type | solution.py:83
  91.5 0.2 copy-done.2
  91.7 1.3 convolution_convert_fusion.2
  93.0 1.3 convolution_convert_fusion.1
  94.3 1.1 copy-done.1
  95.4 4.2 %fusion = f32[2048]{0:T(1024)S(1)} fusion(f32[2048,896]{0,1:T(8,128)S(1)} %bitcast.87, bf16[4,256,896]{1,2,0:T(8,128)(2,1)S(1)} %constant_dynamic-update-slice_fusion.4, bf16[256,4,2048]{0,2,1:T(8,128)(2,1)S(1)} %bitcast.81), kind=kOutput, calls=%fused_computation.2 | convolution fusion | flops 3761764352 | bytes 13377536 | tf_op jit(solution)/shard_map/tbj,bti->ji/dot_general | solution.py:97
  99.6 0.1 collective-permute-start.17
  99.7 1.3 convolution_convert_fusion
  101.0 1.5 collective-permute-start.18
  102.5 0.8 fusion.33
  103.3 1.4 collective-permute-done.18
  104.7 3.3 %collective-permute-start.19 = (f32[2048]{0:T(1024)S(1)}, f32[2048]{0:T(1024)S(1)}, u32[]{:S(2)}, u32[]{:S(2)}) collective-permute-start(f32[2048]{0:T(1024)S(1)} %add.158), channel_id=1, source_target_pairs={{0,4},{1,5},{2,6},{3,7},{4,0},{5,1},{6,2},{7,3},{8,12},{9,13},{10,... | collective-permute-start | bytes 24584 | tf_op jit(solution)/shard_map/ppermute | solution.py:50
  108.0 0.8 fusion.5
  108.8 1.1 collective-permute-done.19
  109.9 1.5 collective-permute-start.20
  111.4 1.4 convolution_bitcast_fusion
  112.8 1.0 collective-permute-start.9
  113.7 1.1 collective-permute-start.6
  114.9 3.0 %collective-permute-start.7 = (bf16[256,896]{1,0:T(8,128)(2,1)S(1)}, bf16[256,896]{1,0:T(8,128)(2,1)S(1)}, u32[]{:S(2)}, u32[]{:S(2)}) collective-permute-start(bf16[256,896]{1,0:T(8,128)(2,1)S(1)} %convolution_convert_fusion.1), channel_id=1, source_target_pairs={{0,64},{32,96},{64,0},{96,32},{1,65},{33,97},{65,1},{97,33},{2,66}... | collective-permute-start | bytes 1376264 | tf_op jit(solution)/shard_map/ppermute | solution.py:92
  117.8 1.7 %collective-permute-start.8 = (bf16[256,896]{1,0:T(8,128)(2,1)S(1)}, bf16[256,896]{1,0:T(8,128)(2,1)S(1)}, u32[]{:S(2)}, u32[]{:S(2)}) collective-permute-start(bf16[256,896]{1,0:T(8,128)(2,1)S(1)} %convolution_convert_fusion), channel_id=1, source_target_pairs={{0,96},{32,0},{64,32},{96,64},{1,97},{33,1},{65,33},{97,65},{2,98}... | collective-permute-start | bytes 1376264 | tf_op jit(solution)/shard_map/ppermute | solution.py:92
  119.5 3.4 %collective-permute-start.21 = (f32[2048]{0:T(1024)S(1)}, f32[2048]{0:T(1024)S(1)}, u32[]{:S(2)}, u32[]{:S(2)}) collective-permute-start(f32[2048]{0:T(1024)S(1)} %add.160), channel_id=1, source_target_pairs={{0,16},{1,17},{2,18},{3,19},{4,20},{5,21},{6,22},{7,23},{8,24},{9,... | collective-permute-start | bytes 24584 | tf_op jit(solution)/shard_map/ppermute | solution.py:50
  122.9 2.2 %fusion.4 = f32[2048,64]{0,1:T(8,128)} fusion(f32[64,2048]{1,0:T(8,128)S(1)} %convolution_bitcast_fusion, bf16[256,4,2048]{0,2,1:T(8,128)(2,1)S(1)} %bitcast.85, f32[2048]{0:T(1024)S(1)} %get-tuple-element.6, f32[4,256,64]{1,2,0:T(8,128)S(1)} %constant_dynamic-update-slice_fusion), kind=kOutput, calls=%fused_computation.10 | convolution fusion | flops 268894208 | bytes 5513216 | tf_op jit(solution)/shard_map/tbj,btr->jr/dot_general | solution.py:19
  125.0 0.6 add_divide_fusion
  125.7 1.0 collective-permute-start.10
  126.7 3.6 %collective-permute-done.6 = bf16[256,896]{1,0:T(8,128)(2,1)S(1)} collective-permute-done((bf16[256,896]{1,0:T(8,128)(2,1)S(1)}, bf16[256,896]{1,0:T(8,128)(2,1)S(1)}, u32[]{:S(2)}, u32[]{:S(2)}) %collective-permute-start.6) | collective-permute-done | bytes 458784 | tf_op jit(solution)/shard_map/ppermute | solution.py:92
  130.3 13.2 %collective-permute-done.7 = bf16[256,896]{1,0:T(8,128)(2,1)S(1)} collective-permute-done((bf16[256,896]{1,0:T(8,128)(2,1)S(1)}, bf16[256,896]{1,0:T(8,128)(2,1)S(1)}, u32[]{:S(2)}, u32[]{:S(2)}) %collective-permute-start.7) | collective-permute-done | bytes 458784 | tf_op jit(solution)/shard_map/ppermute | solution.py:92
  143.4 2.2 %fusion.22 = bf16[256,896]{1,0:T(8,128)(2,1)} fusion(bf16[2048,896]{0,1:T(8,128)(2,1)S(1)} %copy-done.2, bf16[256,4,2048]{0,2,1:T(8,128)(2,1)S(1)} %multiply_convert_fusion, s32[]{:T(128)S(6)} %select_n.50, bf16[256,896]{1,0:T(8,128)(2,1)S(1)} %collective-permute-done.8, bf16[256,896]{1,0:T(8,128)(2,1)S(1)} %collective-permute-done.7, ...), kind=kOutput, calls=%fused_computation.28 | convolution fusion | flops 941129728 | bytes 6553604 | tf_op jit(solution)/shard_map/dot_general | solution.py:87
  145.7 0.6 collective-permute-done.10
  146.3 0.7 convolution_bitcast_fusion.2
  146.9 1.4 fusion.7
  (53 shorter events, 0.6 us)
Async XLA Ops:
  7.2 8.8 %copy-start = (bf16[64,896]{1,0:T(8,128)(2,1)S(1)}, bf16[64,896]{1,0:T(8,128)(2,1)}, u32[]{:S(2)}) copy-start(bf16[64,896]{1,0:T(8,128)(2,1)} %param.9) | copy-start | bytes 344068
  7.2 81.2 %all-gather.2.cloned.1.call-start = ((), (), s32[]{:S(2)}) async-start(), calls=%async_computation | async-start | bytes 4325376 | tf_op jit(solution)/shard_map/all_gather | solution.py:65
  8.2 9.1 %copy-start.3 = (bf16[2048,64]{0,1:T(8,128)(2,1)S(1)}, bf16[2048,64]{0,1:T(8,128)(2,1)}, u32[]{:S(2)}) copy-start(bf16[2048,64]{0,1:T(8,128)(2,1)} %param.10) | copy-start | bytes 786436
  8.2 0.8 collective-permute-start
  9.1 0.7 copy-start.5
  25.1 41.6 %copy-start.6 = (f32[2048]{0:T(1024)S(1)}, f32[2048]{0:T(1024)}, u32[]{:S(2)}) copy-start(f32[2048]{0:T(1024)} %param.11) | copy-start | bytes 24580
  25.1 1.3 collective-permute-start.1
  26.5 4.4 %collective-permute-start.2 = (f32[18432]{0:T(1024)S(1)}, f32[18432]{0:T(1024)S(1)}, u32[]{:S(2)}, u32[]{:S(2)}) collective-permute-start(f32[18432]{0:T(1024)S(1)} %fusion.46), channel_id=1, source_target_pairs={{0,2},{1,3},{2,0},{3,1},{4,6},{5,7},{6,4},{7,5},{8,10},{9,11},{10,... | collective-permute-start | bytes 221192 | tf_op jit(solution)/shard_map/ppermute | solution.py:50
  31.0 6.5 %collective-permute-start.3 = (f32[18432]{0:T(1024)S(1)}, f32[18432]{0:T(1024)S(1)}, u32[]{:S(2)}, u32[]{:S(2)}) collective-permute-start(f32[18432]{0:T(1024)S(1)} %add.132), channel_id=1, source_target_pairs={{0,4},{1,5},{2,6},{3,7},{4,0},{5,1},{6,2},{7,3},{8,12},{9,13},{10,... | collective-permute-start | bytes 221192 | tf_op jit(solution)/shard_map/ppermute | solution.py:50
  37.5 19.5 %collective-permute-start.4 = (f32[18432]{0:T(1024)S(1)}, f32[18432]{0:T(1024)S(1)}, u32[]{:S(2)}, u32[]{:S(2)}) collective-permute-start(f32[18432]{0:T(1024)S(1)} %add.133), channel_id=1, source_target_pairs={{0,8},{1,9},{2,10},{3,11},{4,12},{5,13},{6,14},{7,15},{8,0},{9,1},... | collective-permute-start | bytes 221192 | tf_op jit(solution)/shard_map/ppermute | solution.py:50
  47.1 34.9 %collective-permute-start.11 = (bf16[256,896]{1,0:T(8,128)(2,1)}, bf16[256,896]{1,0:T(8,128)(2,1)}, u32[]{:S(2)}, u32[]{:S(2)}) collective-permute-start(bf16[256,896]{1,0:T(8,128)(2,1)} %param.6), channel_id=1, source_target_pairs={{0,32},{32,64},{64,96},{96,0},{1,33},{33,65},{65,97},{97,1},{2,34}... | collective-permute-start | bytes 1376264 | tf_op jit(solution)/shard_map/ppermute | solution.py:42
  47.1 36.1 %collective-permute-start.12 = (bf16[256,896]{1,0:T(8,128)(2,1)}, bf16[256,896]{1,0:T(8,128)(2,1)S(1)}, u32[]{:S(2)}, u32[]{:S(2)}) collective-permute-start(bf16[256,896]{1,0:T(8,128)(2,1)} %param.6), channel_id=1, source_target_pairs={{0,64},{32,96},{64,0},{96,32},{1,65},{33,97},{65,1},{97,33},{2,66}... | collective-permute-start | bytes 1376264 | tf_op jit(solution)/shard_map/ppermute | solution.py:42
  55.1 30.1 %collective-permute-start.13 = (bf16[256,896]{1,0:T(8,128)(2,1)}, bf16[256,896]{1,0:T(8,128)(2,1)}, u32[]{:S(2)}, u32[]{:S(2)}) collective-permute-start(bf16[256,896]{1,0:T(8,128)(2,1)} %param.6), channel_id=1, source_target_pairs={{0,96},{32,0},{64,32},{96,64},{1,97},{33,1},{65,33},{97,65},{2,98}... | collective-permute-start | bytes 1376264 | tf_op jit(solution)/shard_map/ppermute | solution.py:42
  57.0 7.4 %collective-permute-start.5 = (f32[18432]{0:T(1024)S(1)}, f32[18432]{0:T(1024)S(1)}, u32[]{:S(2)}, u32[]{:S(2)}) collective-permute-start(f32[18432]{0:T(1024)S(1)} %add.134), channel_id=1, source_target_pairs={{0,16},{1,17},{2,18},{3,19},{4,20},{5,21},{6,22},{7,23},{8,24},{9,... | collective-permute-start | bytes 221192 | tf_op jit(solution)/shard_map/ppermute | solution.py:50
  64.6 12.3 %collective-permute-start.14 = (f32[256,64]{1,0:T(8,128)S(1)}, f32[256,64]{1,0:T(8,128)}, u32[]{:S(2)}, u32[]{:S(2)}) collective-permute-start(f32[256,64]{1,0:T(8,128)S(1)} %slice.18), channel_id=1, source_target_pairs={{0,32},{32,64},{64,96},{96,0},{1,33},{33,65},{65,97},{97,1},{2,34}... | collective-permute-start | bytes 196616 | tf_op jit(solution)/shard_map/ppermute | solution.py:42
  66.0 13.3 %collective-permute-start.15 = (f32[256,64]{1,0:T(8,128)S(1)}, f32[256,64]{1,0:T(8,128)S(1)}, u32[]{:S(2)}, u32[]{:S(2)}) collective-permute-start(f32[256,64]{1,0:T(8,128)S(1)} %slice.18), channel_id=1, source_target_pairs={{0,64},{32,96},{64,0},{96,32},{1,65},{33,97},{65,1},{97,33},{2,66}... | collective-permute-start | bytes 196616 | tf_op jit(solution)/shard_map/ppermute | solution.py:42
  76.8 5.0 %collective-permute-start.16 = (f32[256,64]{1,0:T(8,128)S(1)}, f32[256,64]{1,0:T(8,128)S(1)}, u32[]{:S(2)}, u32[]{:S(2)}) collective-permute-start(f32[256,64]{1,0:T(8,128)S(1)} %slice.18), channel_id=1, source_target_pairs={{0,96},{32,0},{64,32},{96,64},{1,97},{33,1},{65,33},{97,65},{2,98}... | collective-permute-start | bytes 196616 | tf_op jit(solution)/shard_map/ppermute | solution.py:42
  83.2 0.8 copy-start.4
  88.4 3.3 %copy-start.2 = (bf16[2048,896]{0,1:T(8,128)(2,1)S(1)}, bf16[2048,896]{0,1:T(8,128)(2,1)}, u32[]{:S(2)}) copy-start(bf16[2048,896]{0,1:T(8,128)(2,1)} %get-tuple-element.9) | copy-start | bytes 11010052
  88.4 5.9 %slice-start = ((s8[7340032]{0:T(1024)(128)(4,1)}), s8[4194304]{0:T(1024)(128)(4,1)S(1)}, s32[]{:S(2)}) async-start(s8[7340032]{0:T(1024)(128)(4,1)} %bitcast.86), calls=%async_computation.1 | async-start | bytes 8388608
  91.7 2.6 %slice-start.1 = ((s8[7340032]{0:T(1024)(128)(4,1)}), s8[3145728]{0:T(1024)(128)(4,1)S(1)}, s32[]{:S(2)}) async-start(s8[7340032]{0:T(1024)(128)(4,1)} %bitcast.86), calls=%async_computation.2 | async-start | bytes 6291456
  93.0 2.4 %copy-start.1 = (bf16[256,8192]{0,1:T(8,128)(2,1)S(1)}, bf16[256,8192]{0,1:T(8,128)(2,1)}, u32[]{:S(2)}) copy-start(bf16[256,8192]{0,1:T(8,128)(2,1)} %all-gather.2.cloned.1.call-done) | copy-start | bytes 12582916
  99.6 1.4 collective-permute-start.17
  101.0 3.7 %collective-permute-start.18 = (f32[2048]{0:T(1024)S(1)}, f32[2048]{0:T(1024)S(1)}, u32[]{:S(2)}, u32[]{:S(2)}) collective-permute-start(f32[2048]{0:T(1024)S(1)} %add.157), channel_id=1, source_target_pairs={{0,2},{1,3},{2,0},{3,1},{4,6},{5,7},{6,4},{7,5},{8,10},{9,11},{10,... | collective-permute-start | bytes 24584 | tf_op jit(solution)/shard_map/ppermute | solution.py:50
  104.7 5.2 %collective-permute-start.19 = (f32[2048]{0:T(1024)S(1)}, f32[2048]{0:T(1024)S(1)}, u32[]{:S(2)}, u32[]{:S(2)}) collective-permute-start(f32[2048]{0:T(1024)S(1)} %add.158), channel_id=1, source_target_pairs={{0,4},{1,5},{2,6},{3,7},{4,0},{5,1},{6,2},{7,3},{8,12},{9,13},{10,... | collective-permute-start | bytes 24584 | tf_op jit(solution)/shard_map/ppermute | solution.py:50
  109.9 9.6 %collective-permute-start.20 = (f32[2048]{0:T(1024)S(1)}, f32[2048]{0:T(1024)S(1)}, u32[]{:S(2)}, u32[]{:S(2)}) collective-permute-start(f32[2048]{0:T(1024)S(1)} %add.159), channel_id=1, source_target_pairs={{0,8},{1,9},{2,10},{3,11},{4,12},{5,13},{6,14},{7,15},{8,0},{9,1},... | collective-permute-start | bytes 24584 | tf_op jit(solution)/shard_map/ppermute | solution.py:50
  112.8 12.9 %collective-permute-start.9 = (f32[4,256,64]{1,2,0:T(8,128)S(1)}, f32[4,256,64]{1,2,0:T(8,128)S(1)}, u32[]{:S(2)}, u32[]{:S(2)}) collective-permute-start(f32[4,256,64]{1,2,0:T(8,128)S(1)} %fusion.5), channel_id=1, source_target_pairs={{0,32},{32,0},{64,96},{96,64},{1,33},{33,1},{65,97},{97,65},{2,34}... | collective-permute-start | bytes 786440 | tf_op jit(solution)/shard_map/ppermute | solution.py:50
  113.7 16.5 %collective-permute-start.6 = (bf16[256,896]{1,0:T(8,128)(2,1)S(1)}, bf16[256,896]{1,0:T(8,128)(2,1)S(1)}, u32[]{:S(2)}, u32[]{:S(2)}) collective-permute-start(bf16[256,896]{1,0:T(8,128)(2,1)S(1)} %convolution_convert_fusion.2), channel_id=1, source_target_pairs={{0,32},{32,64},{64,96},{96,0},{1,33},{33,65},{65,97},{97,1},{2,34}... | collective-permute-start | bytes 1376264 | tf_op jit(solution)/shard_map/ppermute | solution.py:92
  114.9 28.6 %collective-permute-start.7 = (bf16[256,896]{1,0:T(8,128)(2,1)S(1)}, bf16[256,896]{1,0:T(8,128)(2,1)S(1)}, u32[]{:S(2)}, u32[]{:S(2)}) collective-permute-start(bf16[256,896]{1,0:T(8,128)(2,1)S(1)} %convolution_convert_fusion.1), channel_id=1, source_target_pairs={{0,64},{32,96},{64,0},{96,32},{1,65},{33,97},{65,1},{97,33},{2,66}... | collective-permute-start | bytes 1376264 | tf_op jit(solution)/shard_map/ppermute | solution.py:92
  117.8 25.6 %collective-permute-start.8 = (bf16[256,896]{1,0:T(8,128)(2,1)S(1)}, bf16[256,896]{1,0:T(8,128)(2,1)S(1)}, u32[]{:S(2)}, u32[]{:S(2)}) collective-permute-start(bf16[256,896]{1,0:T(8,128)(2,1)S(1)} %convolution_convert_fusion), channel_id=1, source_target_pairs={{0,96},{32,0},{64,32},{96,64},{1,97},{33,1},{65,33},{97,65},{2,98}... | collective-permute-start | bytes 1376264 | tf_op jit(solution)/shard_map/ppermute | solution.py:92
  119.5 5.5 %collective-permute-start.21 = (f32[2048]{0:T(1024)S(1)}, f32[2048]{0:T(1024)S(1)}, u32[]{:S(2)}, u32[]{:S(2)}) collective-permute-start(f32[2048]{0:T(1024)S(1)} %add.160), channel_id=1, source_target_pairs={{0,16},{1,17},{2,18},{3,19},{4,20},{5,21},{6,22},{7,23},{8,24},{9,... | collective-permute-start | bytes 24584 | tf_op jit(solution)/shard_map/ppermute | solution.py:50
  125.7 20.6 %collective-permute-start.10 = (f32[4,256,64]{1,2,0:T(8,128)S(1)}, f32[4,256,64]{1,2,0:T(8,128)S(1)}, u32[]{:S(2)}, u32[]{:S(2)}) collective-permute-start(f32[4,256,64]{1,2,0:T(8,128)S(1)} %add.153), channel_id=1, source_target_pairs={{0,64},{32,96},{64,0},{96,32},{1,65},{33,97},{65,1},{97,33},{2,66}... | collective-permute-start | bytes 786440 | tf_op jit(solution)/shard_map/ppermute | solution.py:50
Sparse Core Ops, SparseCore 0:
  10.8 58.8 all-gather.1

commit v4 on v3

--- a/solution.py
+++ b/solution.py
@@ -16,9 +16,9 @@
 
 def dot2(spec, a, b_pair):
     hi, lo = b_pair
-    return jnp.einsum(spec, a, hi, preferred_element_type=jnp.float32) + jnp.einsum(
-        spec, a, lo, preferred_element_type=jnp.float32
-    )
+    both = jnp.einsum(spec, a, jnp.concatenate([hi, lo], -1), preferred_element_type=jnp.float32)
+    n = hi.shape[-1]
+    return both[..., :n] + both[..., n:]
 
 
 def transpose_pairs(n_dp, n_t):
@@ -103,10 +103,8 @@
         g_all = allreduce(g_part, "dp", n_dp)
 
         gh, gl = split_bf16(g_all)
-        adapter_down_gradient = adapter_scale * (
-            jnp.einsum("btr,bti->ri", gh, x_all, preferred_element_type=jnp.float32)
-            + jnp.einsum("btr,bti->ri", gl, x_all, preferred_element_type=jnp.float32)
-        )
+        down = jnp.einsum("btr,bti->ri", jnp.concatenate([gh, gl], -1), x_all, preferred_element_type=jnp.float32)
+        adapter_down_gradient = adapter_scale * (down[:rank] + down[rank:])
         up = dot2("tbj,btr->jr", og_all, split_bf16(h_all))
         adapter_up_gradient = adapter_scale * (col_scale[:, None] * up)
         magnitude_gradient = grad_scale / weight_row_norm

time: 156 us -> 154 us (0.987)
  starting transfers between devices: 48.2 us -> 52.6 us
  local copies, waits for them, and re-layouts: 18.4 us -> 14.6 us
    ppermute x6, waiting for transfers between devices: 12.4 us -> 7.67 us  [gather_dp(): piece = lax.ppermute(v, 'dp', shift_pairs(n_dp, k))]
    dot_general x6 -> x3, matrix products: 7.16 us -> 2.89 us  [the longest x2 2.19 us: dot2(): jnp.einsum(spec, a, jnp.concatenate([hi, lo], -1), preferred_element_type...]
    dot_general x1, matrix products: 4.22 us -> 8.34 us  [body(): jnp.einsum('tbj,bti->ji', og_all, x_all, preferred_element_type=jnp.float32)]
    ppermute x6, starting transfers between devices: 12.2 us -> 15.7 us  [gather_dp(): piece = lax.ppermute(v, 'dp', shift_pairs(n_dp, k))]
    ppermute x12, starting transfers between devices: 29.4 us -> 32.9 us  [allreduce(): v = v + lax.ppermute(v, axis, [(i, i ^ k) for i in range(n)])]
    ppermute x3, starting transfers between devices: 5.77 us -> 3.3 us  [body(): lax.ppermute(sends[k - 1], 'dp', shift_pairs(n_dp, k))]
    convert_element_type x1, other arithmetic: 3.08 us -> 0.75 us  [body(): scaled = (og_all.astype(jnp.float32) * col_scale).astype(jnp.bfloat16)]
    ppermute x3, waiting for transfers between devices: 16.7 us -> 18.9 us  [body(): lax.ppermute(sends[k - 1], 'dp', shift_pairs(n_dp, k))]
  transfers between devices with their start and end apart: 23 -> 23, of which waited for: 11 -> 11; matrix products, arithmetic and copies ran while one was open for 21% -> 20% of each run, Pallas kernels for 0% -> 0%
where the time goes in v4:
time: 154 us; the launch traced here: 153 us
  starting transfers between devices  52.6 us (34%)
  waiting for transfers between devices  42.5 us (28%)
  matrix products  25.3 us (16%)
  local copies, waits for them, and re-layouts  14.6 us (9%)
  between operations  14.5 us (9%)
  other arithmetic  3.89 us (3%)
    ppermute x12, starting transfers between devices, allreduce(): v = v + lax.ppermute(v, axis, [(i, i ^ k) for i in range(n)])  32.9 us
    ppermute x3, waiting for transfers between devices, body(): lax.ppermute(sends[k - 1], 'dp', shift_pairs(n_dp, k))  18.9 us
    ppermute x12, waiting for transfers between devices, allreduce(): v = v + lax.ppermute(v, axis, [(i, i ^ k) for i in range(n)])  15.8 us
    ppermute x6, starting transfers between devices, gather_dp(): piece = lax.ppermute(v, 'dp', shift_pairs(n_dp, k))  15.7 us
    unnamed x22, local copies, waits for them, and re-layouts  10 us
    dot_general x1, matrix products, body(): jnp.einsum('tbj,bti->ji', og_all, x_all, preferred_element_type=jnp.float32)  8.34 us
    dot_general x1, matrix products, body(): jnp.dot(adapter_up_factor, adapter_down_factor, preferred_element_type=jn...  7.73 us
    ppermute x6, waiting for transfers between devices, gather_dp(): piece = lax.ppermute(v, 'dp', shift_pairs(n_dp, k))  7.67 us
  transfers between devices with their start and end apart: 23, of which 11 were waited for; matrix products, arithmetic and copies ran while one was open for 20% of the time, Pallas kernels for 0%

profile of v4, /device:TPU:0, one launch (start us, length us, event | category | flops | bytes accessed | tf_op | source)
XLA Modules:
  0.0 153.4 jit_solution(341765159135479529)
XLA Ops:
  7.2 0.0 all-gather.2.cloned.1.call-start
  7.2 1.0 copy.16
  8.2 0.7 collective-permute-start
  8.9 0.6 copy-done.8
  9.6 6.3 %copy.17 = bf16[2048,896]{0,1:T(8,128)(2,1)} copy(bf16[2048,896]{1,0:T(8,128)(2,1)} %param.8) | data formatting | bytes 7340032 | tf_op args[2]
  15.9 0.3 fusion.44
  16.2 0.1 reshape.27
  16.3 7.7 %multiply_reduce_fusion = (f32[2048]{0:T(1024)S(1)}, bf16[2048,896]{0,1:T(8,128)(2,1)}, f32[2048,896]{0,1:T(8,128)}) fusion(bf16[2048,64]{0,1:T(8,128)(2,1)S(1)} %copy-done.4, bf16[64,896]{1,0:T(8,128)(2,1)S(1)} %copy-done, bf16[2048,896]{0,1:T(8,128)(2,1)} %copy.17), kind=kOutput, calls=%fused_computation.3 | convolution fusion | flops 245889024 | bytes 15065088 | tf_op jit(solution)/shard_map/dot_general | solution.py:68
  24.0 0.1 collective-permute-start.1
  24.1 1.3 collective-permute-done.1
  25.4 1.8 %collective-permute-start.2 = (f32[18432]{0:T(1024)S(1)}, f32[18432]{0:T(1024)S(1)}, u32[]{:S(2)}, u32[]{:S(2)}) collective-permute-start(f32[18432]{0:T(1024)S(1)} %fusion.43), channel_id=1, source_target_pairs={{0,2},{1,3},{2,0},{3,1},{4,6},{5,7},{6,4},{7,5},{8,10},{9,11},{10,... | collective-permute-start | bytes 221192 | tf_op jit(solution)/shard_map/ppermute | solution.py:50
  27.2 2.7 %collective-permute-done.2 = f32[18432]{0:T(1024)S(1)} collective-permute-done((f32[18432]{0:T(1024)S(1)}, f32[18432]{0:T(1024)S(1)}, u32[]{:S(2)}, u32[]{:S(2)}) %collective-permute-start.2) | collective-permute-done | bytes 73760 | tf_op jit(solution)/shard_map/ppermute | solution.py:50
  29.8 3.4 %collective-permute-start.3 = (f32[18432]{0:T(1024)S(1)}, f32[18432]{0:T(1024)S(1)}, u32[]{:S(2)}, u32[]{:S(2)}) collective-permute-start(f32[18432]{0:T(1024)S(1)} %add.128), channel_id=1, source_target_pairs={{0,4},{1,5},{2,6},{3,7},{4,0},{5,1},{6,2},{7,3},{8,12},{9,13},{10,... | collective-permute-start | bytes 221192 | tf_op jit(solution)/shard_map/ppermute | solution.py:50
  33.2 2.6 %collective-permute-done.3 = f32[18432]{0:T(1024)S(1)} collective-permute-done((f32[18432]{0:T(1024)S(1)}, f32[18432]{0:T(1024)S(1)}, u32[]{:S(2)}, u32[]{:S(2)}) %collective-permute-start.3) | collective-permute-done | bytes 73760 | tf_op jit(solution)/shard_map/ppermute | solution.py:50
  35.8 9.6 %collective-permute-start.4 = (f32[18432]{0:T(1024)S(1)}, f32[18432]{0:T(1024)S(1)}, u32[]{:S(2)}, u32[]{:S(2)}) collective-permute-start(f32[18432]{0:T(1024)S(1)} %add.129), channel_id=1, source_target_pairs={{0,8},{1,9},{2,10},{3,11},{4,12},{5,13},{6,14},{7,15},{8,0},{9,1},... | collective-permute-start | bytes 221192 | tf_op jit(solution)/shard_map/ppermute | solution.py:50
  45.4 8.6 %collective-permute-start.12 = (bf16[256,896]{1,0:T(8,128)(2,1)S(1)}, bf16[256,896]{1,0:T(8,128)(2,1)S(1)}, u32[]{:S(2)}, u32[]{:S(2)}) collective-permute-start(bf16[256,896]{1,0:T(8,128)(2,1)S(1)} %copy-done.3), channel_id=1, source_target_pairs={{0,64},{32,96},{64,0},{96,32},{1,65},{33,97},{65,1},{97,33},{2,66}... | collective-permute-start | bytes 1376264 | tf_op jit(solution)/shard_map/ppermute | solution.py:42
  53.9 0.7 collective-permute-start.13
  54.6 0.2 copy.20
  54.9 3.1 %collective-permute-start.5 = (f32[18432]{0:T(1024)S(1)}, f32[18432]{0:T(1024)S(1)}, u32[]{:S(2)}, u32[]{:S(2)}) collective-permute-start(f32[18432]{0:T(1024)S(1)} %add.130), channel_id=1, source_target_pairs={{0,16},{1,17},{2,18},{3,19},{4,20},{5,21},{6,22},{7,23},{8,24},{9,... | collective-permute-start | bytes 221192 | tf_op jit(solution)/shard_map/ppermute | solution.py:50
  58.0 0.1 broadcast_in_dim.35
  58.2 4.3 %collective-permute-done.5 = f32[18432]{0:T(1024)S(1)} collective-permute-done((f32[18432]{0:T(1024)S(1)}, f32[18432]{0:T(1024)S(1)}, u32[]{:S(2)}, u32[]{:S(2)}) %collective-permute-start.5) | collective-permute-done | bytes 73760 | tf_op jit(solution)/shard_map/ppermute | solution.py:50
  62.5 0.1 broadcast_in_dim.41
  62.6 0.1 slice.40
  62.7 0.1 copy.26
  62.8 1.1 collective-permute-start.14
  63.8 1.3 collective-permute-start.15
  65.1 0.1 copy.25
  65.3 5.8 %collective-permute-done.14 = f32[256,64]{0,1:T(8,128)S(1)} collective-permute-done((f32[256,64]{0,1:T(8,128)S(1)}, f32[256,64]{0,1:T(8,128)S(1)}, u32[]{:S(2)}, u32[]{:S(2)}) %collective-permute-start.14) | collective-permute-done | bytes 65568 | tf_op jit(solution)/shard_map/ppermute | solution.py:42
  71.0 4.1 %collective-permute-start.16 = (f32[256,64]{0,1:T(8,128)S(1)}, f32[256,64]{0,1:T(8,128)S(1)}, u32[]{:S(2)}, u32[]{:S(2)}) collective-permute-start(f32[256,64]{0,1:T(8,128)S(1)} %copy.26), channel_id=1, source_target_pairs={{0,96},{32,0},{64,32},{96,64},{1,97},{33,1},{65,33},{97,65},{2,98}... | collective-permute-start | bytes 196616 | tf_op jit(solution)/shard_map/ppermute | solution.py:42
  75.1 0.1 collective-permute-done.15
  75.3 1.8 %collective-permute-done.16 = f32[256,64]{0,1:T(8,128)S(1)} collective-permute-done((f32[256,64]{0,1:T(8,128)S(1)}, f32[256,64]{0,1:T(8,128)S(1)}, u32[]{:S(2)}, u32[]{:S(2)}) %collective-permute-start.16) | collective-permute-done | bytes 65568 | tf_op jit(solution)/shard_map/ppermute | solution.py:42
  77.0 0.7 subtract_convert_fusion.1
  77.7 1.2 copy.21
  79.0 0.8 copy-done.7
  79.7 1.2 copy.22
  81.0 1.2 copy.23
  82.4 8.3 %fusion = f32[2048]{0:T(1024)S(1)} fusion(f32[2048,896]{0,1:T(8,128)} %get-tuple-element.19, bf16[4,256,896]{1,2,0:T(8,128)(2,1)S(1)} %constant_dynamic-update-slice_fusion.1, bf16[256,4,2048]{0,2,1:T(8,128)(2,1)} %bitcast.62), kind=kOutput, calls=%fused_computation.2 | convolution fusion | flops 3761764352 | bytes 13377536 | tf_op jit(solution)/shard_map/tbj,bti->ji/dot_general | solution.py:97
  90.7 0.3 collective-permute-start.17
  91.0 1.5 convolution_bitcast_fusion
  92.5 0.9 fusion.26
  93.4 0.7 multiply_convert_fusion
  94.2 1.3 copy-done.2
  95.5 1.3 convolution_convert_fusion.2
  96.8 1.2 collective-permute-start.18
  98.0 1.3 convolution_convert_fusion.1
  99.3 1.2 collective-permute-done.18
  100.5 2.3 %collective-permute-start.19 = (f32[2048]{0:T(1024)S(1)}, f32[2048]{0:T(1024)S(1)}, u32[]{:S(2)}, u32[]{:S(2)}) collective-permute-start(f32[2048]{0:T(1024)S(1)} %add.153), channel_id=1, source_target_pairs={{0,4},{1,5},{2,6},{3,7},{4,0},{5,1},{6,2},{7,3},{8,12},{9,13},{10,... | collective-permute-start | bytes 24584 | tf_op jit(solution)/shard_map/ppermute | solution.py:50
  102.8 0.7 convolution_bitcast_fusion.1
  103.5 2.1 %collective-permute-done.19 = f32[2048]{0:T(1024)S(1)} collective-permute-done((f32[2048]{0:T(1024)S(1)}, f32[2048]{0:T(1024)S(1)}, u32[]{:S(2)}, u32[]{:S(2)}) %collective-permute-start.19) | collective-permute-done | bytes 8224 | tf_op jit(solution)/shard_map/ppermute | solution.py:50
  105.7 0.7 collective-permute-start.20
  106.4 1.2 collective-permute-start.9
  107.6 1.7 %collective-permute-done.20 = f32[2048]{0:T(1024)S(1)} collective-permute-done((f32[2048]{0:T(1024)S(1)}, f32[2048]{0:T(1024)S(1)}, u32[]{:S(2)}, u32[]{:S(2)}) %collective-permute-start.20) | collective-permute-done | bytes 8224 | tf_op jit(solution)/shard_map/ppermute | solution.py:50
  109.3 6.2 %collective-permute-start.21 = (f32[2048]{0:T(1024)S(1)}, f32[2048]{0:T(1024)S(1)}, u32[]{:S(2)}, u32[]{:S(2)}) collective-permute-start(f32[2048]{0:T(1024)S(1)} %add.155), channel_id=1, source_target_pairs={{0,16},{1,17},{2,18},{3,19},{4,20},{5,21},{6,22},{7,23},{8,24},{9,... | collective-permute-start | bytes 24584 | tf_op jit(solution)/shard_map/ppermute | solution.py:50
  115.6 1.3 convolution_convert_fusion
  116.9 0.1 collective-permute-start.6
  117.0 2.7 %collective-permute-start.7 = (bf16[256,896]{1,0:T(8,128)(2,1)S(1)}, bf16[256,896]{1,0:T(8,128)(2,1)S(1)}, u32[]{:S(2)}, u32[]{:S(2)}) collective-permute-start(bf16[256,896]{1,0:T(8,128)(2,1)S(1)} %convolution_convert_fusion.1), channel_id=1, source_target_pairs={{0,64},{32,96},{64,0},{96,32},{1,65},{33,97},{65,1},{97,33},{2,66}... | collective-permute-start | bytes 1376264 | tf_op jit(solution)/shard_map/ppermute | solution.py:92
  119.6 0.6 collective-permute-start.8
  120.2 0.6 add_divide_fusion
  120.8 0.1 fusion.58
  120.9 3.0 %collective-permute-start.10 = (f32[4,256,64]{1,2,0:T(8,128)S(1)}, f32[4,256,64]{1,2,0:T(8,128)S(1)}, u32[]{:S(2)}, u32[]{:S(2)}) collective-permute-start(f32[4,256,64]{1,2,0:T(8,128)S(1)} %fusion.58), channel_id=1, source_target_pairs={{0,64},{32,96},{64,0},{96,32},{1,65},{33,97},{65,1},{97,33},{2,66}... | collective-permute-start | bytes 786440 | tf_op jit(solution)/shard_map/ppermute | solution.py:50
  123.9 18.9 %collective-permute-done.6 = bf16[256,896]{1,0:T(8,128)(2,1)S(1)} collective-permute-done((bf16[256,896]{1,0:T(8,128)(2,1)S(1)}, bf16[256,896]{1,0:T(8,128)(2,1)S(1)}, u32[]{:S(2)}, u32[]{:S(2)}) %collective-permute-start.6) | collective-permute-done | bytes 458784 | tf_op jit(solution)/shard_map/ppermute | solution.py:92
  142.8 2.2 %fusion.15 = bf16[256,896]{1,0:T(8,128)(2,1)} fusion(bf16[2048,896]{0,1:T(8,128)(2,1)S(1)} %copy-done.2, bf16[256,4,2048]{0,2,1:T(8,128)(2,1)S(1)} %multiply_convert_fusion, s32[]{:T(128)S(6)} %select_n.50, bf16[256,896]{1,0:T(8,128)(2,1)S(1)} %collective-permute-done.8, bf16[256,896]{1,0:T(8,128)(2,1)S(1)} %collective-permute-done.7, ...), kind=kOutput, calls=%fused_computation.19 | convolution fusion | flops 941129728 | bytes 6553604 | tf_op jit(solution)/shard_map/dot_general | solution.py:87
  145.1 0.7 convolution_bitcast_fusion.2
  145.8 0.7 fusion.33
  (54 shorter events, 0.5 us)
Async XLA Ops:
  7.2 8.8 %copy-start = (bf16[64,896]{1,0:T(8,128)(2,1)S(1)}, bf16[64,896]{1,0:T(8,128)(2,1)}, u32[]{:S(2)}) copy-start(bf16[64,896]{1,0:T(8,128)(2,1)} %param.9) | copy-start | bytes 344068
  7.2 75.2 %all-gather.2.cloned.1.call-start = ((), (), s32[]{:S(2)}) async-start(), calls=%async_computation | async-start | bytes 4325376 | tf_op jit(solution)/shard_map/all_gather | solution.py:65
  8.2 0.7 collective-permute-start
  8.9 0.7 copy-start.8
  9.6 6.3 %copy-start.3 = (bf16[256,896]{1,0:T(8,128)(2,1)S(1)}, bf16[256,896]{1,0:T(8,128)(2,1)}, u32[]{:S(2)}) copy-start(bf16[256,896]{1,0:T(8,128)(2,1)} %param.6) | copy-start | bytes 1376260
  9.6 6.7 %copy-start.4 = (bf16[2048,64]{0,1:T(8,128)(2,1)S(1)}, bf16[2048,64]{0,1:T(8,128)(2,1)}, u32[]{:S(2)}) copy-start(bf16[2048,64]{0,1:T(8,128)(2,1)} %param.10) | copy-start | bytes 786436
  24.0 41.1 %copy-start.9 = (f32[2048]{0:T(1024)S(1)}, f32[2048]{0:T(1024)}, u32[]{:S(2)}) copy-start(f32[2048]{0:T(1024)} %param.11) | copy-start | bytes 24580
  24.0 1.3 collective-permute-start.1
  25.4 4.4 %collective-permute-start.2 = (f32[18432]{0:T(1024)S(1)}, f32[18432]{0:T(1024)S(1)}, u32[]{:S(2)}, u32[]{:S(2)}) collective-permute-start(f32[18432]{0:T(1024)S(1)} %fusion.43), channel_id=1, source_target_pairs={{0,2},{1,3},{2,0},{3,1},{4,6},{5,7},{6,4},{7,5},{8,10},{9,11},{10,... | collective-permute-start | bytes 221192 | tf_op jit(solution)/shard_map/ppermute | solution.py:50
  29.8 5.9 %collective-permute-start.3 = (f32[18432]{0:T(1024)S(1)}, f32[18432]{0:T(1024)S(1)}, u32[]{:S(2)}, u32[]{:S(2)}) collective-permute-start(f32[18432]{0:T(1024)S(1)} %add.128), channel_id=1, source_target_pairs={{0,4},{1,5},{2,6},{3,7},{4,0},{5,1},{6,2},{7,3},{8,12},{9,13},{10,... | collective-permute-start | bytes 221192 | tf_op jit(solution)/shard_map/ppermute | solution.py:50
  35.8 19.1 %collective-permute-start.4 = (f32[18432]{0:T(1024)S(1)}, f32[18432]{0:T(1024)S(1)}, u32[]{:S(2)}, u32[]{:S(2)}) collective-permute-start(f32[18432]{0:T(1024)S(1)} %add.129), channel_id=1, source_target_pairs={{0,8},{1,9},{2,10},{3,11},{4,12},{5,13},{6,14},{7,15},{8,0},{9,1},... | collective-permute-start | bytes 221192 | tf_op jit(solution)/shard_map/ppermute | solution.py:50
  45.4 32.3 %collective-permute-start.11 = (bf16[256,896]{1,0:T(8,128)(2,1)S(1)}, bf16[256,896]{1,0:T(8,128)(2,1)}, u32[]{:S(2)}, u32[]{:S(2)}) collective-permute-start(bf16[256,896]{1,0:T(8,128)(2,1)S(1)} %copy-done.3), channel_id=1, source_target_pairs={{0,32},{32,64},{64,96},{96,0},{1,33},{33,65},{65,97},{97,1},{2,34}... | collective-permute-start | bytes 1376264 | tf_op jit(solution)/shard_map/ppermute | solution.py:42
  45.4 33.6 %collective-permute-start.12 = (bf16[256,896]{1,0:T(8,128)(2,1)S(1)}, bf16[256,896]{1,0:T(8,128)(2,1)S(1)}, u32[]{:S(2)}, u32[]{:S(2)}) collective-permute-start(bf16[256,896]{1,0:T(8,128)(2,1)S(1)} %copy-done.3), channel_id=1, source_target_pairs={{0,64},{32,96},{64,0},{96,32},{1,65},{33,97},{65,1},{97,33},{2,66}... | collective-permute-start | bytes 1376264 | tf_op jit(solution)/shard_map/ppermute | solution.py:42
  53.9 27.0 %collective-permute-start.13 = (bf16[256,896]{1,0:T(8,128)(2,1)S(1)}, bf16[256,896]{1,0:T(8,128)(2,1)}, u32[]{:S(2)}, u32[]{:S(2)}) collective-permute-start(bf16[256,896]{1,0:T(8,128)(2,1)S(1)} %copy-done.3), channel_id=1, source_target_pairs={{0,96},{32,0},{64,32},{96,64},{1,97},{33,1},{65,33},{97,65},{2,98}... | collective-permute-start | bytes 1376264 | tf_op jit(solution)/shard_map/ppermute | solution.py:42
  54.9 7.6 %collective-permute-start.5 = (f32[18432]{0:T(1024)S(1)}, f32[18432]{0:T(1024)S(1)}, u32[]{:S(2)}, u32[]{:S(2)}) collective-permute-start(f32[18432]{0:T(1024)S(1)} %add.130), channel_id=1, source_target_pairs={{0,16},{1,17},{2,18},{3,19},{4,20},{5,21},{6,22},{7,23},{8,24},{9,... | collective-permute-start | bytes 221192 | tf_op jit(solution)/shard_map/ppermute | solution.py:50
  62.8 8.3 %collective-permute-start.14 = (f32[256,64]{0,1:T(8,128)S(1)}, f32[256,64]{0,1:T(8,128)S(1)}, u32[]{:S(2)}, u32[]{:S(2)}) collective-permute-start(f32[256,64]{0,1:T(8,128)S(1)} %copy.26), channel_id=1, source_target_pairs={{0,32},{32,64},{64,96},{96,0},{1,33},{33,65},{65,97},{97,1},{2,34}... | collective-permute-start | bytes 196616 | tf_op jit(solution)/shard_map/ppermute | solution.py:42
  63.8 11.4 %collective-permute-start.15 = (f32[256,64]{0,1:T(8,128)S(1)}, f32[256,64]{0,1:T(8,128)S(1)}, u32[]{:S(2)}, u32[]{:S(2)}) collective-permute-start(f32[256,64]{0,1:T(8,128)S(1)} %copy.26), channel_id=1, source_target_pairs={{0,64},{32,96},{64,0},{96,32},{1,65},{33,97},{65,1},{97,33},{2,66}... | collective-permute-start | bytes 196616 | tf_op jit(solution)/shard_map/ppermute | solution.py:42
  71.0 6.0 %collective-permute-start.16 = (f32[256,64]{0,1:T(8,128)S(1)}, f32[256,64]{0,1:T(8,128)S(1)}, u32[]{:S(2)}, u32[]{:S(2)}) collective-permute-start(f32[256,64]{0,1:T(8,128)S(1)} %copy.26), channel_id=1, source_target_pairs={{0,96},{32,0},{64,32},{96,64},{1,97},{33,1},{65,33},{97,65},{2,98}... | collective-permute-start | bytes 196616 | tf_op jit(solution)/shard_map/ppermute | solution.py:42
  78.9 0.8 copy-start.7
  82.3 8.7 %copy-start.1 = (bf16[256,8192]{0,1:T(8,128)(2,1)S(1)}, bf16[256,8192]{0,1:T(8,128)(2,1)}, u32[]{:S(2)}) copy-start(bf16[256,8192]{0,1:T(8,128)(2,1)} %all-gather.2.cloned.1.call-done) | copy-start | bytes 12582916
  82.3 8.7 %copy-start.6 = (bf16[4,256,64]{1,2,0:T(8,128)(2,1)S(1)}, bf16[4,256,64]{1,2,0:T(8,128)(2,1)}, u32[]{:S(2)}) copy-start(bf16[4,256,64]{1,2,0:T(8,128)(2,1)} %get-tuple-element.9) | copy-start | bytes 393220
  90.7 1.8 %copy-start.5 = (bf16[2048,64]{0,1:T(8,128)(2,1)S(1)}, bf16[2048,64]{0,1:T(8,128)(2,1)}, u32[]{:S(2)}) copy-start(bf16[2048,64]{0,1:T(8,128)(2,1)} %param.10) | copy-start | bytes 786436
  90.7 6.1 %collective-permute-start.17 = (f32[2048]{0:T(1024)S(1)}, f32[2048]{0:T(1024)S(1)}, u32[]{:S(2)}, u32[]{:S(2)}) collective-permute-start(f32[2048]{0:T(1024)S(1)} %fusion), channel_id=1, source_target_pairs={{0,1},{1,0},{2,3},{3,2},{4,5},{5,4},{6,7},{7,6},{8,9},{9,8},{10,11... | collective-permute-start | bytes 24584 | tf_op jit(solution)/shard_map/ppermute | solution.py:50
  93.4 2.0 %copy-start.2 = (bf16[2048,896]{0,1:T(8,128)(2,1)S(1)}, bf16[2048,896]{0,1:T(8,128)(2,1)}, u32[]{:S(2)}) copy-start(bf16[2048,896]{0,1:T(8,128)(2,1)} %get-tuple-element.11) | copy-start | bytes 11010052
  96.8 3.7 %collective-permute-start.18 = (f32[2048]{0:T(1024)S(1)}, f32[2048]{0:T(1024)S(1)}, u32[]{:S(2)}, u32[]{:S(2)}) collective-permute-start(f32[2048]{0:T(1024)S(1)} %add.152), channel_id=1, source_target_pairs={{0,2},{1,3},{2,0},{3,1},{4,6},{5,7},{6,4},{7,5},{8,10},{9,11},{10,... | collective-permute-start | bytes 24584 | tf_op jit(solution)/shard_map/ppermute | solution.py:50
  100.5 5.2 %collective-permute-start.19 = (f32[2048]{0:T(1024)S(1)}, f32[2048]{0:T(1024)S(1)}, u32[]{:S(2)}, u32[]{:S(2)}) collective-permute-start(f32[2048]{0:T(1024)S(1)} %add.153), channel_id=1, source_target_pairs={{0,4},{1,5},{2,6},{3,7},{4,0},{5,1},{6,2},{7,3},{8,12},{9,13},{10,... | collective-permute-start | bytes 24584 | tf_op jit(solution)/shard_map/ppermute | solution.py:50
  105.7 3.7 %collective-permute-start.20 = (f32[2048]{0:T(1024)S(1)}, f32[2048]{0:T(1024)S(1)}, u32[]{:S(2)}, u32[]{:S(2)}) collective-permute-start(f32[2048]{0:T(1024)S(1)} %add.154), channel_id=1, source_target_pairs={{0,8},{1,9},{2,10},{3,11},{4,12},{5,13},{6,14},{7,15},{8,0},{9,1},... | collective-permute-start | bytes 24584 | tf_op jit(solution)/shard_map/ppermute | solution.py:50
  106.4 14.4 %collective-permute-start.9 = (f32[4,256,64]{1,2,0:T(8,128)S(1)}, f32[4,256,64]{1,2,0:T(8,128)S(1)}, u32[]{:S(2)}, u32[]{:S(2)}) collective-permute-start(f32[4,256,64]{1,2,0:T(8,128)S(1)} %slice_add_fusion.1), channel_id=1, source_target_pairs={{0,32},{32,0},{64,96},{96,64},{1,33},{33,1},{65,97},{97,65},{2,34}... | collective-permute-start | bytes 786440 | tf_op jit(solution)/shard_map/ppermute | solution.py:50
  109.3 10.9 %collective-permute-start.21 = (f32[2048]{0:T(1024)S(1)}, f32[2048]{0:T(1024)S(1)}, u32[]{:S(2)}, u32[]{:S(2)}) collective-permute-start(f32[2048]{0:T(1024)S(1)} %add.155), channel_id=1, source_target_pairs={{0,16},{1,17},{2,18},{3,19},{4,20},{5,21},{6,22},{7,23},{8,24},{9,... | collective-permute-start | bytes 24584 | tf_op jit(solution)/shard_map/ppermute | solution.py:50
  116.9 25.9 %collective-permute-start.6 = (bf16[256,896]{1,0:T(8,128)(2,1)S(1)}, bf16[256,896]{1,0:T(8,128)(2,1)S(1)}, u32[]{:S(2)}, u32[]{:S(2)}) collective-permute-start(bf16[256,896]{1,0:T(8,128)(2,1)S(1)} %convolution_convert_fusion.2), channel_id=1, source_target_pairs={{0,32},{32,64},{64,96},{96,0},{1,33},{33,65},{65,97},{97,1},{2,34}... | collective-permute-start | bytes 1376264 | tf_op jit(solution)/shard_map/ppermute | solution.py:92
  117.0 25.8 %collective-permute-start.7 = (bf16[256,896]{1,0:T(8,128)(2,1)S(1)}, bf16[256,896]{1,0:T(8,128)(2,1)S(1)}, u32[]{:S(2)}, u32[]{:S(2)}) collective-permute-start(bf16[256,896]{1,0:T(8,128)(2,1)S(1)} %convolution_convert_fusion.1), channel_id=1, source_target_pairs={{0,64},{32,96},{64,0},{96,32},{1,65},{33,97},{65,1},{97,33},{2,66}... | collective-permute-start | bytes 1376264 | tf_op jit(solution)/shard_map/ppermute | solution.py:92
  119.6 23.2 %collective-permute-start.8 = (bf16[256,896]{1,0:T(8,128)(2,1)S(1)}, bf16[256,896]{1,0:T(8,128)(2,1)S(1)}, u32[]{:S(2)}, u32[]{:S(2)}) collective-permute-start(bf16[256,896]{1,0:T(8,128)(2,1)S(1)} %convolution_convert_fusion), channel_id=1, source_target_pairs={{0,96},{32,0},{64,32},{96,64},{1,97},{33,1},{65,33},{97,65},{2,98}... | collective-permute-start | bytes 1376264 | tf_op jit(solution)/shard_map/ppermute | solution.py:92
  120.9 24.2 %collective-permute-start.10 = (f32[4,256,64]{1,2,0:T(8,128)S(1)}, f32[4,256,64]{1,2,0:T(8,128)S(1)}, u32[]{:S(2)}, u32[]{:S(2)}) collective-permute-start(f32[4,256,64]{1,2,0:T(8,128)S(1)} %fusion.58), channel_id=1, source_target_pairs={{0,64},{32,96},{64,0},{96,32},{1,65},{33,97},{65,1},{97,33},{2,66}... | collective-permute-start | bytes 786440 | tf_op jit(solution)/shard_map/ppermute | solution.py:50
Sparse Core Ops, SparseCore 0:
  10.8 59.3 all-gather.1

commit v5 on v4

--- a/solution.py
+++ b/solution.py
@@ -52,11 +52,30 @@
     return v
 
 
+def allreduce_tensor(v, t, shape):
+    nz, ny, nc = shape
+    idx = lambda z, y, c: (z * ny + y) * nc + c
+    v = v + lax.ppermute(v, "tensor", [(idx(z, y, c), idx(z, y, 1 - c)) for z in range(nz) for y in range(ny) for c in range(nc)])
+    for size, coord, make in (
+        (ny, (t // nc) % ny, lambda k: [(idx(z, y, c), idx(z, (y + k) % ny, c)) for z in range(nz) for y in range(ny) for c in range(nc)]),
+        (nz, t // (ny * nc), lambda k: [(idx(z, y, c), idx((z + k) % nz, y, c)) for z in range(nz) for y in range(ny) for c in range(nc)]),
+    ):
+        slots = jnp.zeros((size,) + v.shape, v.dtype)
+        slots = lax.dynamic_update_index_in_dim(slots, v, coord, 0)
+        for k in range(1, size):
+            slots = lax.dynamic_update_index_in_dim(slots, lax.ppermute(v, "tensor", make(k)), (coord + size - k) % size, 0)
+        v = slots[0]
+        for i in range(1, size):
+            v = v + slots[i]
+    return v
+
+
 def make_local(n_dp, n_t):
     pairs = transpose_pairs(n_dp, n_t)
 
     def body(inputs, output_gradient, frozen, adapter_down_factor, adapter_up_factor, magnitude):
         d = lax.axis_index("dp")
+        t = lax.axis_index("tensor")
         tok, _ = inputs.shape
         rows = frozen.shape[0]
         rank = adapter_down_factor.shape[0]
@@ -96,7 +115,7 @@
 
         product = jnp.einsum("tbj,bti->ji", og_all, x_all, preferred_element_type=jnp.float32)
         grad_scale_part = jnp.sum(product * merged, axis=1)
-        grad_scale = allreduce(grad_scale_part, "tensor", n_t)
+        grad_scale = allreduce_tensor(grad_scale_part, t, (n_dp, n_t // (2 * n_dp), 2))
 
         w = col_scale[:, None] * adapter_up_factor.astype(jnp.float32)
         g_part = dot2("tbj,jr->btr", og_all, split_bf16(w))

time: 154 us -> 159 us (1.032)
  other arithmetic: 3.89 us -> 6.28 us
  starting transfers between devices: 52.6 us -> 54.4 us
    ppermute x12 -> x7, starting transfers between devices: 32.9 us -> 18.5 us  [allreduce(): v = v + lax.ppermute(v, axis, [(i, i ^ k) for i in range(n)])]
    ppermute x0 -> x7, starting transfers between devices: none -> 13.8 us  [the longest x6 13.7 us: allreduce_tensor(): lax.ppermute(v, 'tensor', make(k))]
    dot_general x4, matrix products: 6.13 us -> 11.1 us  [ig_for(): return jnp.dot(block, merged_b, preferred_element_type=jnp.float32)]
    dot_general x1, matrix products: 8.34 us -> 4.22 us  [body(): jnp.einsum('tbj,bti->ji', og_all, x_all, preferred_element_type=jnp.float32)]
    ppermute x12 -> x7, waiting for transfers between devices: 15.8 us -> 13 us  [allreduce(): v = v + lax.ppermute(v, axis, [(i, i ^ k) for i in range(n)])]
    ppermute x3, starting transfers between devices: 3.3 us -> 5.69 us  [body(): lax.ppermute(sends[k - 1], 'dp', shift_pairs(n_dp, k))]
    convert_element_type x1, other arithmetic: 0.75 us -> 3.08 us  [body(): scaled = (og_all.astype(jnp.float32) * col_scale).astype(jnp.bfloat16)]
    unnamed x22 -> x30, local copies, waits for them, and re-layouts: 10 us -> 10 us
  transfers between devices with their start and end apart: 23 -> 25, of which waited for: 11 -> 11; matrix products, arithmetic and copies ran while one was open for 20% -> 20% of each run, Pallas kernels for 0% -> 0%
where the time goes in v5:
time: 159 us
  starting transfers between devices  54.4 us (34%)
  waiting for transfers between devices  41.9 us (26%)
  matrix products  26.1 us (16%)
  local copies, waits for them, and re-layouts  15.5 us (10%)
  between operations  14.6 us (9%)
  other arithmetic  6.28 us (4%)
    ppermute x3, waiting for transfers between devices, body(): lax.ppermute(sends[k - 1], 'dp', shift_pairs(n_dp, k))  19.8 us
    ppermute x7, starting transfers between devices, allreduce(): v = v + lax.ppermute(v, axis, [(i, i ^ k) for i in range(n)])  18.5 us
    ppermute x6, starting transfers between devices, gather_dp(): piece = lax.ppermute(v, 'dp', shift_pairs(n_dp, k))  15.7 us
    ppermute x6, starting transfers between devices, allreduce_tensor(): lax.ppermute(v, 'tensor', make(k))  13.7 us
    ppermute x7, waiting for transfers between devices, allreduce(): v = v + lax.ppermute(v, axis, [(i, i ^ k) for i in range(n)])  13 us
    dot_general x4, matrix products, ig_for(): return jnp.dot(block, merged_b, preferred_element_type=jnp.float32)  11.1 us
    unnamed x30, local copies, waits for them, and re-layouts  10 us
    ppermute x6, waiting for transfers between devices, gather_dp(): piece = lax.ppermute(v, 'dp', shift_pairs(n_dp, k))  8.01 us
  transfers between devices with their start and end apart: 25, of which 11 were waited for; matrix products, arithmetic and copies ran while one was open for 20% of the time, Pallas kernels for 0%

profile of v5, /device:TPU:0, one launch (start us, length us, event | category | flops | bytes accessed | tf_op | source)
XLA Modules:
  0.0 158.9 jit_solution(6350209668958788661)
XLA Ops:
  7.2 1.0 copy.16
  8.2 0.7 collective-permute-start
  8.9 0.6 copy-done.9
  9.6 6.2 %copy.17 = bf16[2048,896]{0,1:T(8,128)(2,1)} copy(bf16[2048,896]{1,0:T(8,128)(2,1)} %param.8) | data formatting | bytes 7340032 | tf_op args[2]
  15.9 0.3 fusion.44
  16.2 7.6 %multiply_reduce_fusion = (f32[2048]{0:T(1024)S(1)}, bf16[2048,896]{0,1:T(8,128)(2,1)}, f32[2048,896]{0,1:T(8,128)}) fusion(bf16[2048,64]{0,1:T(8,128)(2,1)S(1)} %copy-done.5, bf16[64,896]{1,0:T(8,128)(2,1)S(1)} %copy-done, bf16[2048,896]{0,1:T(8,128)(2,1)} %copy.17), kind=kOutput, calls=%fused_computation.3 | convolution fusion | flops 245889024 | bytes 15065088 | tf_op jit(solution)/shard_map/dot_general | solution.py:87
  24.0 1.3 collective-permute-done.1
  25.2 1.8 %collective-permute-start.2 = (f32[18432]{0:T(1024)S(1)}, f32[18432]{0:T(1024)S(1)}, u32[]{:S(2)}, u32[]{:S(2)}) collective-permute-start(f32[18432]{0:T(1024)S(1)} %fusion.43), channel_id=1, source_target_pairs={{0,2},{1,3},{2,0},{3,1},{4,6},{5,7},{6,4},{7,5},{8,10},{9,11},{10,... | collective-permute-start | bytes 221192 | tf_op jit(solution)/shard_map/ppermute | solution.py:50
  27.0 2.7 %collective-permute-done.2 = f32[18432]{0:T(1024)S(1)} collective-permute-done((f32[18432]{0:T(1024)S(1)}, f32[18432]{0:T(1024)S(1)}, u32[]{:S(2)}, u32[]{:S(2)}) %collective-permute-start.2) | collective-permute-done | bytes 73760 | tf_op jit(solution)/shard_map/ppermute | solution.py:50
  29.7 3.4 %collective-permute-start.3 = (f32[18432]{0:T(1024)S(1)}, f32[18432]{0:T(1024)S(1)}, u32[]{:S(2)}, u32[]{:S(2)}) collective-permute-start(f32[18432]{0:T(1024)S(1)} %add.219), channel_id=1, source_target_pairs={{0,4},{1,5},{2,6},{3,7},{4,0},{5,1},{6,2},{7,3},{8,12},{9,13},{10,... | collective-permute-start | bytes 221192 | tf_op jit(solution)/shard_map/ppermute | solution.py:50
  33.1 2.6 %collective-permute-done.3 = f32[18432]{0:T(1024)S(1)} collective-permute-done((f32[18432]{0:T(1024)S(1)}, f32[18432]{0:T(1024)S(1)}, u32[]{:S(2)}, u32[]{:S(2)}) %collective-permute-start.3) | collective-permute-done | bytes 73760 | tf_op jit(solution)/shard_map/ppermute | solution.py:50
  35.6 9.5 %collective-permute-start.4 = (f32[18432]{0:T(1024)S(1)}, f32[18432]{0:T(1024)S(1)}, u32[]{:S(2)}, u32[]{:S(2)}) collective-permute-start(f32[18432]{0:T(1024)S(1)} %add.220), channel_id=1, source_target_pairs={{0,8},{1,9},{2,10},{3,11},{4,12},{5,13},{6,14},{7,15},{8,0},{9,1},... | collective-permute-start | bytes 221192 | tf_op jit(solution)/shard_map/ppermute | solution.py:50
  45.1 8.7 %collective-permute-start.12 = (bf16[256,896]{1,0:T(8,128)(2,1)S(1)}, bf16[256,896]{1,0:T(8,128)(2,1)S(1)}, u32[]{:S(2)}, u32[]{:S(2)}) collective-permute-start(bf16[256,896]{1,0:T(8,128)(2,1)S(1)} %copy-done.4), channel_id=1, source_target_pairs={{0,64},{32,96},{64,0},{96,32},{1,65},{33,97},{65,1},{97,33},{2,66}... | collective-permute-start | bytes 1376264 | tf_op jit(solution)/shard_map/ppermute | solution.py:42
  53.9 0.6 collective-permute-start.13
  54.5 0.2 copy.20
  54.8 3.1 %collective-permute-start.5 = (f32[18432]{0:T(1024)S(1)}, f32[18432]{0:T(1024)S(1)}, u32[]{:S(2)}, u32[]{:S(2)}) collective-permute-start(f32[18432]{0:T(1024)S(1)} %add.221), channel_id=1, source_target_pairs={{0,16},{1,17},{2,18},{3,19},{4,20},{5,21},{6,22},{7,23},{8,24},{9,... | collective-permute-start | bytes 221192 | tf_op jit(solution)/shard_map/ppermute | solution.py:50
  57.9 0.1 broadcast_in_dim.58
  58.1 4.2 %collective-permute-done.5 = f32[18432]{0:T(1024)S(1)} collective-permute-done((f32[18432]{0:T(1024)S(1)}, f32[18432]{0:T(1024)S(1)}, u32[]{:S(2)}, u32[]{:S(2)}) %collective-permute-start.5) | collective-permute-done | bytes 73760 | tf_op jit(solution)/shard_map/ppermute | solution.py:50
  62.6 1.1 collective-permute-start.14
  63.7 1.3 collective-permute-start.15
  65.2 6.1 %collective-permute-done.14 = f32[256,64]{0,1:T(8,128)S(1)} collective-permute-done((f32[256,64]{0,1:T(8,128)S(1)}, f32[256,64]{0,1:T(8,128)S(1)}, u32[]{:S(2)}, u32[]{:S(2)}) %collective-permute-start.14) | collective-permute-done | bytes 65568 | tf_op jit(solution)/shard_map/ppermute | solution.py:42
  71.3 3.9 %collective-permute-start.16 = (f32[256,64]{0,1:T(8,128)S(1)}, f32[256,64]{0,1:T(8,128)S(1)}, u32[]{:S(2)}, u32[]{:S(2)}) collective-permute-start(f32[256,64]{0,1:T(8,128)S(1)} %copy.26), channel_id=1, source_target_pairs={{0,96},{32,0},{64,32},{96,64},{1,97},{33,1},{65,33},{97,65},{2,98}... | collective-permute-start | bytes 196616 | tf_op jit(solution)/shard_map/ppermute | solution.py:42
  75.2 0.1 collective-permute-done.15
  75.4 1.8 %collective-permute-done.16 = f32[256,64]{0,1:T(8,128)S(1)} collective-permute-done((f32[256,64]{0,1:T(8,128)S(1)}, f32[256,64]{0,1:T(8,128)S(1)}, u32[]{:S(2)}, u32[]{:S(2)}) %collective-permute-start.16) | collective-permute-done | bytes 65568 | tf_op jit(solution)/shard_map/ppermute | solution.py:42
  77.1 0.7 subtract_convert_fusion.1
  77.8 1.2 copy.21
  79.1 0.8 copy-done.8
  79.8 1.2 copy.22
  81.1 1.2 copy.23
  82.5 3.1 %multiply_convert_fusion = bf16[256,4,2048]{0,2,1:T(8,128)(2,1)S(1)} fusion(f32[2048]{0:T(1024)S(1)} %get-tuple-element.6, bf16[256,8192]{0,1:T(8,128)(2,1)} %all-gather.2.cloned.1.call-done), kind=kLoop, calls=%fused_computation | loop fusion | flops 6291456 | bytes 8396800 | tf_op jit(solution)/shard_map/convert_element_type | solution.py:102
  85.6 0.2 copy-done.3
  85.7 2.1 %convolution_convert_fusion.2 = bf16[256,896]{1,0:T(8,128)(2,1)} fusion(bf16[2048,896]{0,1:T(8,128)(2,1)S(1)} %copy-done.3, bf16[256,4,2048]{0,2,1:T(8,128)(2,1)S(1)} %multiply_convert_fusion, s32[]{:T(128)S(6)} %select_n.112), kind=kOutput, calls=%fused_computation.8 | convolution fusion | flops 939753472 | bytes 5177348 | tf_op jit(solution)/shard_map/dot_general | solution.py:106
  87.8 2.1 %convolution_convert_fusion.1 = bf16[256,896]{1,0:T(8,128)(2,1)} fusion(bf16[2048,896]{0,1:T(8,128)(2,1)S(1)} %copy-done.3, bf16[256,4,2048]{0,2,1:T(8,128)(2,1)S(1)} %multiply_convert_fusion, s32[]{:T(128)S(6)} %select_n.114), kind=kOutput, calls=%fused_computation.7 | convolution fusion | flops 939753472 | bytes 5177348 | tf_op jit(solution)/shard_map/dot_general | solution.py:106
  89.9 1.1 copy-done.1
  91.0 4.2 %fusion = f32[2048]{0:T(1024)S(1)} fusion(f32[2048,896]{0,1:T(8,128)S(1)} %bitcast.75, bf16[4,256,896]{1,2,0:T(8,128)(2,1)S(1)} %constant_dynamic-update-slice_fusion.1, bf16[256,4,2048]{0,2,1:T(8,128)(2,1)S(1)} %bitcast.71), kind=kOutput, calls=%fused_computation.2 | convolution fusion | flops 3761764352 | bytes 13377536 | tf_op jit(solution)/shard_map/tbj,bti->ji/dot_general | solution.py:116
  95.4 1.5 convolution_bitcast_fusion
  96.8 0.9 fusion.26
  97.8 2.1 %convolution_convert_fusion = bf16[256,896]{1,0:T(8,128)(2,1)} fusion(bf16[2048,896]{0,1:T(8,128)(2,1)S(1)} %copy-done.3, bf16[256,4,2048]{0,2,1:T(8,128)(2,1)S(1)} %multiply_convert_fusion, s32[]{:T(128)S(6)} %select_n.116), kind=kOutput, calls=%fused_computation.6 | convolution fusion | flops 939753472 | bytes 5177348 | tf_op jit(solution)/shard_map/dot_general | solution.py:106
  99.9 0.9 collective-permute-start.18
  100.8 2.9 %collective-permute-start.19 = (f32[2048]{0:T(1024)S(1)}, f32[2048]{0:T(1024)S(1)}, u32[]{:S(2)}, u32[]{:S(2)}) collective-permute-start(f32[2048]{0:T(1024)S(1)} %add.243), channel_id=1, source_target_pairs={{0,4},{1,5},{2,6},{3,7},{4,0},{5,1},{6,2},{7,3},{8,12},{9,13},{10,... | collective-permute-start | bytes 24584 | tf_op jit(solution)/shard_map/ppermute | solution.py:66
  103.6 1.5 collective-permute-start.20
  105.1 0.7 convolution_bitcast_fusion.1
  105.8 0.1 dynamic_update_slice.59
  105.9 0.1 dynamic_update_slice.60
  106.1 0.1 dynamic_update_slice.61
  106.2 1.0 collective-permute-done.20
  107.3 0.1 dynamic_update_slice.62
  107.4 1.2 collective-permute-start.21
  108.6 5.1 %collective-permute-start.22 = (f32[2048]{0:T(1024)S(1)}, f32[2048]{0:T(1024)S(1)}, u32[]{:S(2)}, u32[]{:S(2)}) collective-permute-start(f32[2048]{0:T(1024)S(1)} %bitcast.80), channel_id=1, source_target_pairs={{0,16},{1,17},{2,18},{3,19},{4,20},{5,21},{6,22},{7,23},{8,24},{9,... | collective-permute-start | bytes 24584 | tf_op jit(solution)/shard_map/ppermute | solution.py:66
  113.6 2.2 %collective-permute-start.23 = (f32[2048]{0:T(1024)S(1)}, f32[2048]{0:T(1024)S(1)}, u32[]{:S(2)}, u32[]{:S(2)}) collective-permute-start(f32[2048]{0:T(1024)S(1)} %bitcast.81), channel_id=1, source_target_pairs={{0,24},{1,25},{2,26},{3,27},{4,28},{5,29},{6,30},{7,31},{8,0},{9,1... | collective-permute-start | bytes 24584 | tf_op jit(solution)/shard_map/ppermute | solution.py:66
  116.0 2.0 %collective-permute-start.6 = (bf16[256,896]{1,0:T(8,128)(2,1)}, bf16[256,896]{1,0:T(8,128)(2,1)}, u32[]{:S(2)}, u32[]{:S(2)}) collective-permute-start(bf16[256,896]{1,0:T(8,128)(2,1)} %convolution_convert_fusion.2), channel_id=1, source_target_pairs={{0,32},{32,64},{64,96},{96,0},{1,33},{33,65},{65,97},{97,1},{2,34}... | collective-permute-start | bytes 1376264 | tf_op jit(solution)/shard_map/ppermute | solution.py:111
  118.0 0.1 dynamic_update_slice.63
  118.2 0.8 collective-permute-start.7
  119.0 0.1 dynamic_update_slice.64
  119.1 2.8 %collective-permute-start.8 = (bf16[256,896]{1,0:T(8,128)(2,1)S(1)}, bf16[256,896]{1,0:T(8,128)(2,1)}, u32[]{:S(2)}, u32[]{:S(2)}) collective-permute-start(bf16[256,896]{1,0:T(8,128)(2,1)S(1)} %copy-done.11), channel_id=1, source_target_pairs={{0,96},{32,0},{64,32},{96,64},{1,97},{33,1},{65,33},{97,65},{2,98}... | collective-permute-start | bytes 1376264 | tf_op jit(solution)/shard_map/ppermute | solution.py:111
  122.1 0.1 dynamic_update_slice.66
  122.2 0.6 div.28
  122.8 2.3 %collective-permute-done.9 = f32[4,256,64]{1,2,0:T(8,128)S(1)} collective-permute-done((f32[4,256,64]{1,2,0:T(8,128)S(1)}, f32[4,256,64]{1,2,0:T(8,128)S(1)}, u32[]{:S(2)}, u32[]{:S(2)}) %collective-permute-start.9) | collective-permute-done | bytes 262176 | tf_op jit(solution)/shard_map/ppermute | solution.py:50
  125.2 0.6 collective-permute-start.10
  125.8 6.8 %collective-permute-done.6 = bf16[256,896]{1,0:T(8,128)(2,1)} collective-permute-done((bf16[256,896]{1,0:T(8,128)(2,1)}, bf16[256,896]{1,0:T(8,128)(2,1)}, u32[]{:S(2)}, u32[]{:S(2)}) %collective-permute-start.6) | collective-permute-done | bytes 458784 | tf_op jit(solution)/shard_map/ppermute | solution.py:111
  132.6 13.0 %collective-permute-done.7 = bf16[256,896]{1,0:T(8,128)(2,1)} collective-permute-done((bf16[256,896]{1,0:T(8,128)(2,1)}, bf16[256,896]{1,0:T(8,128)(2,1)}, u32[]{:S(2)}, u32[]{:S(2)}) %collective-permute-start.7) | collective-permute-done | bytes 458784 | tf_op jit(solution)/shard_map/ppermute | solution.py:111
  145.6 4.9 %fusion.15 = bf16[256,896]{1,0:T(8,128)(2,1)} fusion(bf16[2048,896]{0,1:T(8,128)(2,1)} %get-tuple-element.11, bf16[256,4,2048]{0,2,1:T(8,128)(2,1)} %copy-done.2, s32[]{:T(128)S(6)} %select_n.110, bf16[256,896]{1,0:T(8,128)(2,1)} %collective-permute-done.8, bf16[256,896]{1,0:T(8,128)(2,1)} %collective-permute-done.7, ...), kind=kOutput, calls=%fused_computation.19 | convolution fusion | flops 941129728 | bytes 6553604 | tf_op jit(solution)/shard_map/dot_general | solution.py:106
  150.6 0.7 convolution_bitcast_fusion.2
  151.3 0.7 fusion.33
  (76 shorter events, 1.4 us)
Async XLA Ops:
  7.2 8.7 %copy-start = (bf16[64,896]{1,0:T(8,128)(2,1)S(1)}, bf16[64,896]{1,0:T(8,128)(2,1)}, u32[]{:S(2)}) copy-start(bf16[64,896]{1,0:T(8,128)(2,1)} %param.9) | copy-start | bytes 344068
  7.2 75.3 %all-gather.2.cloned.1.call-start = ((), (), s32[]{:S(2)}) async-start(), calls=%async_computation | async-start | bytes 4325376 | tf_op jit(solution)/shard_map/all_gather | solution.py:84
  8.2 0.7 collective-permute-start
  8.9 0.7 copy-start.9
  9.6 6.3 %copy-start.4 = (bf16[256,896]{1,0:T(8,128)(2,1)S(1)}, bf16[256,896]{1,0:T(8,128)(2,1)}, u32[]{:S(2)}) copy-start(bf16[256,896]{1,0:T(8,128)(2,1)} %param.6) | copy-start | bytes 1376260
  9.6 6.6 %copy-start.5 = (bf16[2048,64]{0,1:T(8,128)(2,1)S(1)}, bf16[2048,64]{0,1:T(8,128)(2,1)}, u32[]{:S(2)}) copy-start(bf16[2048,64]{0,1:T(8,128)(2,1)} %param.10) | copy-start | bytes 786436
  23.9 41.1 %copy-start.10 = (f32[2048]{0:T(1024)S(1)}, f32[2048]{0:T(1024)}, u32[]{:S(2)}) copy-start(f32[2048]{0:T(1024)} %param.11) | copy-start | bytes 24580
  23.9 1.3 collective-permute-start.1
  25.2 4.4 %collective-permute-start.2 = (f32[18432]{0:T(1024)S(1)}, f32[18432]{0:T(1024)S(1)}, u32[]{:S(2)}, u32[]{:S(2)}) collective-permute-start(f32[18432]{0:T(1024)S(1)} %fusion.43), channel_id=1, source_target_pairs={{0,2},{1,3},{2,0},{3,1},{4,6},{5,7},{6,4},{7,5},{8,10},{9,11},{10,... | collective-permute-start | bytes 221192 | tf_op jit(solution)/shard_map/ppermute | solution.py:50
  29.7 5.9 %collective-permute-start.3 = (f32[18432]{0:T(1024)S(1)}, f32[18432]{0:T(1024)S(1)}, u32[]{:S(2)}, u32[]{:S(2)}) collective-permute-start(f32[18432]{0:T(1024)S(1)} %add.219), channel_id=1, source_target_pairs={{0,4},{1,5},{2,6},{3,7},{4,0},{5,1},{6,2},{7,3},{8,12},{9,13},{10,... | collective-permute-start | bytes 221192 | tf_op jit(solution)/shard_map/ppermute | solution.py:50
  35.6 19.1 %collective-permute-start.4 = (f32[18432]{0:T(1024)S(1)}, f32[18432]{0:T(1024)S(1)}, u32[]{:S(2)}, u32[]{:S(2)}) collective-permute-start(f32[18432]{0:T(1024)S(1)} %add.220), channel_id=1, source_target_pairs={{0,8},{1,9},{2,10},{3,11},{4,12},{5,13},{6,14},{7,15},{8,0},{9,1},... | collective-permute-start | bytes 221192 | tf_op jit(solution)/shard_map/ppermute | solution.py:50
  45.1 32.7 %collective-permute-start.11 = (bf16[256,896]{1,0:T(8,128)(2,1)S(1)}, bf16[256,896]{1,0:T(8,128)(2,1)}, u32[]{:S(2)}, u32[]{:S(2)}) collective-permute-start(bf16[256,896]{1,0:T(8,128)(2,1)S(1)} %copy-done.4), channel_id=1, source_target_pairs={{0,32},{32,64},{64,96},{96,0},{1,33},{33,65},{65,97},{97,1},{2,34}... | collective-permute-start | bytes 1376264 | tf_op jit(solution)/shard_map/ppermute | solution.py:42
  45.1 33.9 %collective-permute-start.12 = (bf16[256,896]{1,0:T(8,128)(2,1)S(1)}, bf16[256,896]{1,0:T(8,128)(2,1)S(1)}, u32[]{:S(2)}, u32[]{:S(2)}) collective-permute-start(bf16[256,896]{1,0:T(8,128)(2,1)S(1)} %copy-done.4), channel_id=1, source_target_pairs={{0,64},{32,96},{64,0},{96,32},{1,65},{33,97},{65,1},{97,33},{2,66}... | collective-permute-start | bytes 1376264 | tf_op jit(solution)/shard_map/ppermute | solution.py:42
  53.9 27.2 %collective-permute-start.13 = (bf16[256,896]{1,0:T(8,128)(2,1)S(1)}, bf16[256,896]{1,0:T(8,128)(2,1)}, u32[]{:S(2)}, u32[]{:S(2)}) collective-permute-start(bf16[256,896]{1,0:T(8,128)(2,1)S(1)} %copy-done.4), channel_id=1, source_target_pairs={{0,96},{32,0},{64,32},{96,64},{1,97},{33,1},{65,33},{97,65},{2,98}... | collective-permute-start | bytes 1376264 | tf_op jit(solution)/shard_map/ppermute | solution.py:42
  54.8 7.5 %collective-permute-start.5 = (f32[18432]{0:T(1024)S(1)}, f32[18432]{0:T(1024)S(1)}, u32[]{:S(2)}, u32[]{:S(2)}) collective-permute-start(f32[18432]{0:T(1024)S(1)} %add.221), channel_id=1, source_target_pairs={{0,16},{1,17},{2,18},{3,19},{4,20},{5,21},{6,22},{7,23},{8,24},{9,... | collective-permute-start | bytes 221192 | tf_op jit(solution)/shard_map/ppermute | solution.py:50
  62.6 8.7 %collective-permute-start.14 = (f32[256,64]{0,1:T(8,128)S(1)}, f32[256,64]{0,1:T(8,128)S(1)}, u32[]{:S(2)}, u32[]{:S(2)}) collective-permute-start(f32[256,64]{0,1:T(8,128)S(1)} %copy.26), channel_id=1, source_target_pairs={{0,32},{32,64},{64,96},{96,0},{1,33},{33,65},{65,97},{97,1},{2,34}... | collective-permute-start | bytes 196616 | tf_op jit(solution)/shard_map/ppermute | solution.py:42
  63.7 11.6 %collective-permute-start.15 = (f32[256,64]{0,1:T(8,128)S(1)}, f32[256,64]{0,1:T(8,128)S(1)}, u32[]{:S(2)}, u32[]{:S(2)}) collective-permute-start(f32[256,64]{0,1:T(8,128)S(1)} %copy.26), channel_id=1, source_target_pairs={{0,64},{32,96},{64,0},{96,32},{1,65},{33,97},{65,1},{97,33},{2,66}... | collective-permute-start | bytes 196616 | tf_op jit(solution)/shard_map/ppermute | solution.py:42
  71.3 5.8 %collective-permute-start.16 = (f32[256,64]{0,1:T(8,128)S(1)}, f32[256,64]{0,1:T(8,128)S(1)}, u32[]{:S(2)}, u32[]{:S(2)}) collective-permute-start(f32[256,64]{0,1:T(8,128)S(1)} %copy.26), channel_id=1, source_target_pairs={{0,96},{32,0},{64,32},{96,64},{1,97},{33,1},{65,33},{97,65},{2,98}... | collective-permute-start | bytes 196616 | tf_op jit(solution)/shard_map/ppermute | solution.py:42
  79.0 0.8 copy-start.8
  82.4 3.3 %copy-start.3 = (bf16[2048,896]{0,1:T(8,128)(2,1)S(1)}, bf16[2048,896]{0,1:T(8,128)(2,1)}, u32[]{:S(2)}) copy-start(bf16[2048,896]{0,1:T(8,128)(2,1)} %get-tuple-element.11) | copy-start | bytes 11010052
  82.5 7.4 %slice-start = ((s8[7340032]{0:T(1024)(128)(4,1)}), s8[4194304]{0:T(1024)(128)(4,1)S(1)}, s32[]{:S(2)}) async-start(s8[7340032]{0:T(1024)(128)(4,1)} %bitcast.74), calls=%async_computation.1 | async-start | bytes 8388608
  85.5 12.2 %copy-start.2 = (bf16[256,4,2048]{0,2,1:T(8,128)(2,1)}, bf16[256,4,2048]{0,2,1:T(8,128)(2,1)S(1)}, u32[]{:S(2)}) copy-start(bf16[256,4,2048]{0,2,1:T(8,128)(2,1)S(1)} %multiply_convert_fusion) | copy-start | bytes 12582916
  85.7 4.1 %slice-start.1 = ((s8[7340032]{0:T(1024)(128)(4,1)}), s8[3145728]{0:T(1024)(128)(4,1)S(1)}, s32[]{:S(2)}) async-start(s8[7340032]{0:T(1024)(128)(4,1)} %bitcast.74), calls=%async_computation.2 | async-start | bytes 6291456
  87.8 3.2 %copy-start.1 = (bf16[256,8192]{0,1:T(8,128)(2,1)S(1)}, bf16[256,8192]{0,1:T(8,128)(2,1)}, u32[]{:S(2)}) copy-start(bf16[256,8192]{0,1:T(8,128)(2,1)} %all-gather.2.cloned.1.call-done) | copy-start | bytes 12582916
  91.0 4.3 %copy-start.7 = (bf16[4,256,64]{1,2,0:T(8,128)(2,1)S(1)}, bf16[4,256,64]{1,2,0:T(8,128)(2,1)}, u32[]{:S(2)}) copy-start(bf16[4,256,64]{1,2,0:T(8,128)(2,1)} %get-tuple-element.9) | copy-start | bytes 393220
  95.3 1.6 copy-start.6
  95.3 4.6 %collective-permute-start.17 = (f32[2048]{0:T(1024)S(1)}, f32[2048]{0:T(1024)S(1)}, u32[]{:S(2)}, u32[]{:S(2)}) collective-permute-start(f32[2048]{0:T(1024)S(1)} %fusion), channel_id=1, source_target_pairs={{0,1},{1,0},{2,3},{3,2},{4,5},{5,4},{6,7},{7,6},{8,9},{9,8},{10,11... | collective-permute-start | bytes 24584 | tf_op jit(solution)/shard_map/ppermute | solution.py:58
  99.9 19.3 %copy-start.11 = (bf16[256,896]{1,0:T(8,128)(2,1)S(1)}, bf16[256,896]{1,0:T(8,128)(2,1)}, u32[]{:S(2)}) copy-start(bf16[256,896]{1,0:T(8,128)(2,1)} %convolution_convert_fusion) | copy-start | bytes 1376260
  99.9 6.1 %collective-permute-start.18 = (f32[2048]{0:T(1024)S(1)}, f32[2048]{0:T(1024)S(1)}, u32[]{:S(2)}, u32[]{:S(2)}) collective-permute-start(f32[2048]{0:T(1024)S(1)} %add.243), channel_id=1, source_target_pairs={{0,2},{1,3},{2,4},{3,5},{4,6},{5,7},{6,0},{7,1},{8,10},{9,11},{10,... | collective-permute-start | bytes 24584 | tf_op jit(solution)/shard_map/ppermute | solution.py:66
  100.8 5.3 %collective-permute-start.19 = (f32[2048]{0:T(1024)S(1)}, f32[2048]{0:T(1024)S(1)}, u32[]{:S(2)}, u32[]{:S(2)}) collective-permute-start(f32[2048]{0:T(1024)S(1)} %add.243), channel_id=1, source_target_pairs={{0,4},{1,5},{2,6},{3,7},{4,0},{5,1},{6,2},{7,3},{8,12},{9,13},{10,... | collective-permute-start | bytes 24584 | tf_op jit(solution)/shard_map/ppermute | solution.py:66
  103.6 3.7 %collective-permute-start.20 = (f32[2048]{0:T(1024)S(1)}, f32[2048]{0:T(1024)S(1)}, u32[]{:S(2)}, u32[]{:S(2)}) collective-permute-start(f32[2048]{0:T(1024)S(1)} %add.243), channel_id=1, source_target_pairs={{0,6},{1,7},{2,0},{3,1},{4,2},{5,3},{6,4},{7,5},{8,14},{9,15},{10,... | collective-permute-start | bytes 24584 | tf_op jit(solution)/shard_map/ppermute | solution.py:66
  107.4 10.8 %collective-permute-start.21 = (f32[2048]{0:T(1024)S(1)}, f32[2048]{0:T(1024)S(1)}, u32[]{:S(2)}, u32[]{:S(2)}) collective-permute-start(f32[2048]{0:T(1024)S(1)} %bitcast.79), channel_id=1, source_target_pairs={{0,8},{1,9},{2,10},{3,11},{4,12},{5,13},{6,14},{7,15},{8,16},{9,17... | collective-permute-start | bytes 24584 | tf_op jit(solution)/shard_map/ppermute | solution.py:66
  108.6 10.5 %collective-permute-start.22 = (f32[2048]{0:T(1024)S(1)}, f32[2048]{0:T(1024)S(1)}, u32[]{:S(2)}, u32[]{:S(2)}) collective-permute-start(f32[2048]{0:T(1024)S(1)} %bitcast.80), channel_id=1, source_target_pairs={{0,16},{1,17},{2,18},{3,19},{4,20},{5,21},{6,22},{7,23},{8,24},{9,... | collective-permute-start | bytes 24584 | tf_op jit(solution)/shard_map/ppermute | solution.py:66
  113.6 8.4 %collective-permute-start.23 = (f32[2048]{0:T(1024)S(1)}, f32[2048]{0:T(1024)S(1)}, u32[]{:S(2)}, u32[]{:S(2)}) collective-permute-start(f32[2048]{0:T(1024)S(1)} %bitcast.81), channel_id=1, source_target_pairs={{0,24},{1,25},{2,26},{3,27},{4,28},{5,29},{6,30},{7,31},{8,0},{9,1... | collective-permute-start | bytes 24584 | tf_op jit(solution)/shard_map/ppermute | solution.py:66
  115.9 9.3 %collective-permute-start.9 = (f32[4,256,64]{1,2,0:T(8,128)S(1)}, f32[4,256,64]{1,2,0:T(8,128)S(1)}, u32[]{:S(2)}, u32[]{:S(2)}) collective-permute-start(f32[4,256,64]{1,2,0:T(8,128)S(1)} %slice_add_fusion.1), channel_id=1, source_target_pairs={{0,32},{32,0},{64,96},{96,64},{1,33},{33,1},{65,97},{97,65},{2,34}... | collective-permute-start | bytes 786440 | tf_op jit(solution)/shard_map/ppermute | solution.py:50
  116.0 16.6 %collective-permute-start.6 = (bf16[256,896]{1,0:T(8,128)(2,1)}, bf16[256,896]{1,0:T(8,128)(2,1)}, u32[]{:S(2)}, u32[]{:S(2)}) collective-permute-start(bf16[256,896]{1,0:T(8,128)(2,1)} %convolution_convert_fusion.2), channel_id=1, source_target_pairs={{0,32},{32,64},{64,96},{96,0},{1,33},{33,65},{65,97},{97,1},{2,34}... | collective-permute-start | bytes 1376264 | tf_op jit(solution)/shard_map/ppermute | solution.py:111
  118.2 27.5 %collective-permute-start.7 = (bf16[256,896]{1,0:T(8,128)(2,1)}, bf16[256,896]{1,0:T(8,128)(2,1)}, u32[]{:S(2)}, u32[]{:S(2)}) collective-permute-start(bf16[256,896]{1,0:T(8,128)(2,1)} %convolution_convert_fusion.1), channel_id=1, source_target_pairs={{0,64},{32,96},{64,0},{96,32},{1,65},{33,97},{65,1},{97,33},{2,66}... | collective-permute-start | bytes 1376264 | tf_op jit(solution)/shard_map/ppermute | solution.py:111
  119.1 26.5 %collective-permute-start.8 = (bf16[256,896]{1,0:T(8,128)(2,1)S(1)}, bf16[256,896]{1,0:T(8,128)(2,1)}, u32[]{:S(2)}, u32[]{:S(2)}) collective-permute-start(bf16[256,896]{1,0:T(8,128)(2,1)S(1)} %copy-done.11), channel_id=1, source_target_pairs={{0,96},{32,0},{64,32},{96,64},{1,97},{33,1},{65,33},{97,65},{2,98}... | collective-permute-start | bytes 1376264 | tf_op jit(solution)/shard_map/ppermute | solution.py:111
  125.2 25.3 %collective-permute-start.10 = (f32[4,256,64]{1,2,0:T(8,128)S(1)}, f32[4,256,64]{1,2,0:T(8,128)S(1)}, u32[]{:S(2)}, u32[]{:S(2)}) collective-permute-start(f32[4,256,64]{1,2,0:T(8,128)S(1)} %fusion.58), channel_id=1, source_target_pairs={{0,64},{32,96},{64,0},{96,32},{1,65},{33,97},{65,1},{97,33},{2,66}... | collective-permute-start | bytes 786440 | tf_op jit(solution)/shard_map/ppermute | solution.py:50
Sparse Core Ops, SparseCore 0:
  10.8 59.2 all-gather.1

commit v6 on v4

--- a/solution.py
+++ b/solution.py
@@ -72,9 +72,9 @@
         squares = jnp.sum(merged * merged, axis=1)
         h_local = jnp.dot(inputs, adapter_down_factor.T, preferred_element_type=jnp.float32)
 
-        first = allreduce(jnp.concatenate([squares, h_local.reshape(-1)]), "tensor", n_t)
-        total_squares = first[:rows]
-        h_all = gather_dp(first[rows:].reshape(tok, rank), n_dp, d)
+        total_squares = allreduce(squares, "tensor", n_t)
+        h_sum = allreduce(h_local, "tensor", n_t)
+        h_all = gather_dp(h_sum, n_dp, d)
 
         weight_row_norm = jnp.sqrt(total_squares + epsilon)
         col_scale = magnitude / weight_row_norm

time: 154 us -> 158 us (1.026)
  waiting for transfers between devices: 42.5 us -> 44.8 us
    ppermute x6, waiting for transfers between devices: 7.67 us -> 11.2 us  [gather_dp(): piece = lax.ppermute(v, 'dp', shift_pairs(n_dp, k))]
    ppermute x12 -> x17, starting transfers between devices: 32.9 us -> 36.3 us  [allreduce(): v = v + lax.ppermute(v, axis, [(i, i ^ k) for i in range(n)])]
    ppermute x6, starting transfers between devices: 15.7 us -> 13.2 us  [gather_dp(): piece = lax.ppermute(v, 'dp', shift_pairs(n_dp, k))]
    ppermute x12 -> x17, waiting for transfers between devices: 15.8 us -> 14.7 us  [allreduce(): v = v + lax.ppermute(v, axis, [(i, i ^ k) for i in range(n)])]
  transfers between devices with their start and end apart: 23 -> 28, of which waited for: 11 -> 13; matrix products, arithmetic and copies ran while one was open for 20% -> 20% of each run, Pallas kernels for 0% -> 0%
where the time goes in v6:
time: 158 us; the launch traced here: 157 us
  starting transfers between devices  53.4 us (34%)
  waiting for transfers between devices  44.8 us (28%)
  matrix products  26.5 us (17%)
  between operations  14.5 us (9%)
  local copies, waits for them, and re-layouts  14.1 us (9%)
  other arithmetic  3.91 us (2%)
    ppermute x17, starting transfers between devices, allreduce(): v = v + lax.ppermute(v, axis, [(i, i ^ k) for i in range(n)])  36.3 us
    ppermute x3, waiting for transfers between devices, body(): lax.ppermute(sends[k - 1], 'dp', shift_pairs(n_dp, k))  18.9 us
    ppermute x17, waiting for transfers between devices, allreduce(): v = v + lax.ppermute(v, axis, [(i, i ^ k) for i in range(n)])  14.7 us
    ppermute x6, starting transfers between devices, gather_dp(): piece = lax.ppermute(v, 'dp', shift_pairs(n_dp, k))  13.2 us
    ppermute x6, waiting for transfers between devices, gather_dp(): piece = lax.ppermute(v, 'dp', shift_pairs(n_dp, k))  11.2 us
    unnamed x22, local copies, waits for them, and re-layouts  9.96 us
    dot_general x1, matrix products, body(): jnp.einsum('tbj,bti->ji', og_all, x_all, preferred_element_type=jnp.float32)  8.34 us
    dot_general x1, matrix products, body(): jnp.dot(adapter_up_factor, adapter_down_factor, preferred_element_type=jn...  7.8 us
  transfers between devices with their start and end apart: 28, of which 13 were waited for; matrix products, arithmetic and copies ran while one was open for 20% of the time, Pallas kernels for 0%

profile of v6, /device:TPU:0, one launch (start us, length us, event | category | flops | bytes accessed | tf_op | source)
XLA Modules:
  0.0 157.2 jit_solution(10067508030782627157)
XLA Ops:
  7.2 1.0 copy.16
  8.2 0.7 collective-permute-start
  8.9 0.6 copy-done.8
  9.6 1.3 fusion.42
  10.9 0.1 collective-permute-start.14
  11.0 1.2 collective-permute-done.14
  12.3 1.8 %collective-permute-start.15 = (f32[256,64]{0,1:T(8,128)S(1)}, f32[256,64]{0,1:T(8,128)S(1)}, u32[]{:S(2)}, u32[]{:S(2)}) collective-permute-start(f32[256,64]{0,1:T(8,128)S(1)} %add.166), channel_id=1, source_target_pairs={{0,2},{1,3},{2,0},{3,1},{4,6},{5,7},{6,4},{7,5},{8,10},{9,11},{10,... | collective-permute-start | bytes 196616 | tf_op jit(solution)/shard_map/ppermute | solution.py:50
  14.0 2.6 %collective-permute-done.15 = f32[256,64]{0,1:T(8,128)S(1)} collective-permute-done((f32[256,64]{0,1:T(8,128)S(1)}, f32[256,64]{0,1:T(8,128)S(1)}, u32[]{:S(2)}, u32[]{:S(2)}) %collective-permute-start.15) | collective-permute-done | bytes 65568 | tf_op jit(solution)/shard_map/ppermute | solution.py:50
  16.6 3.4 %collective-permute-start.16 = (f32[256,64]{0,1:T(8,128)S(1)}, f32[256,64]{0,1:T(8,128)S(1)}, u32[]{:S(2)}, u32[]{:S(2)}) collective-permute-start(f32[256,64]{0,1:T(8,128)S(1)} %add.167), channel_id=1, source_target_pairs={{0,4},{1,5},{2,6},{3,7},{4,0},{5,1},{6,2},{7,3},{8,12},{9,13},{10,... | collective-permute-start | bytes 196616 | tf_op jit(solution)/shard_map/ppermute | solution.py:50
  20.0 6.2 %copy.17 = bf16[2048,896]{0,1:T(8,128)(2,1)} copy(bf16[2048,896]{1,0:T(8,128)(2,1)} %param.8) | data formatting | bytes 7340032 | tf_op args[2]
  26.3 9.3 %collective-permute-start.17 = (f32[256,64]{0,1:T(8,128)S(1)}, f32[256,64]{0,1:T(8,128)S(1)}, u32[]{:S(2)}, u32[]{:S(2)}) collective-permute-start(f32[256,64]{0,1:T(8,128)S(1)} %add.168), channel_id=1, source_target_pairs={{0,8},{1,9},{2,10},{3,11},{4,12},{5,13},{6,14},{7,15},{8,0},{9,1},... | collective-permute-start | bytes 196616 | tf_op jit(solution)/shard_map/ppermute | solution.py:50
  35.6 7.8 %multiply_reduce_fusion = (f32[2048]{0:T(1024)S(1)}, bf16[2048,896]{0,1:T(8,128)(2,1)}, f32[2048,896]{0,1:T(8,128)}) fusion(bf16[2048,64]{0,1:T(8,128)(2,1)S(1)} %copy-done.4, bf16[64,896]{1,0:T(8,128)(2,1)S(1)} %copy-done, bf16[2048,896]{0,1:T(8,128)(2,1)} %copy.17), kind=kOutput, calls=%fused_computation.3 | convolution fusion | flops 245889024 | bytes 15065088 | tf_op jit(solution)/shard_map/dot_general | solution.py:68
  43.4 1.2 collective-permute-done.1
  44.6 0.7 collective-permute-start.2
  45.3 3.0 %collective-permute-done.2 = f32[2048]{0:T(1024)S(1)} collective-permute-done((f32[2048]{0:T(1024)S(1)}, f32[2048]{0:T(1024)S(1)}, u32[]{:S(2)}, u32[]{:S(2)}) %collective-permute-start.2) | collective-permute-done | bytes 8224 | tf_op jit(solution)/shard_map/ppermute | solution.py:50
  48.3 0.5 collective-permute-start.3
  48.8 8.3 %collective-permute-start.12 = (bf16[256,896]{1,0:T(8,128)(2,1)S(1)}, bf16[256,896]{1,0:T(8,128)(2,1)S(1)}, u32[]{:S(2)}, u32[]{:S(2)}) collective-permute-start(bf16[256,896]{1,0:T(8,128)(2,1)S(1)} %copy-done.3), channel_id=1, source_target_pairs={{0,64},{32,96},{64,0},{96,32},{1,65},{33,97},{65,1},{97,33},{2,66}... | collective-permute-start | bytes 1376264 | tf_op jit(solution)/shard_map/ppermute | solution.py:42
  57.1 0.7 collective-permute-start.13
  57.8 0.2 copy.19
  58.0 2.0 %collective-permute-start.4 = (f32[2048]{0:T(1024)S(1)}, f32[2048]{0:T(1024)S(1)}, u32[]{:S(2)}, u32[]{:S(2)}) collective-permute-start(f32[2048]{0:T(1024)S(1)} %add.144), channel_id=1, source_target_pairs={{0,8},{1,9},{2,10},{3,11},{4,12},{5,13},{6,14},{7,15},{8,0},{9,1},... | collective-permute-start | bytes 24584 | tf_op jit(solution)/shard_map/ppermute | solution.py:50
  60.0 2.6 %collective-permute-start.18 = (f32[256,64]{0,1:T(8,128)S(1)}, f32[256,64]{0,1:T(8,128)S(1)}, u32[]{:S(2)}, u32[]{:S(2)}) collective-permute-start(f32[256,64]{0,1:T(8,128)S(1)} %add.169), channel_id=1, source_target_pairs={{0,16},{1,17},{2,18},{3,19},{4,20},{5,21},{6,22},{7,23},{8,24},{9,... | collective-permute-start | bytes 196616 | tf_op jit(solution)/shard_map/ppermute | solution.py:50
  62.7 0.1 broadcast_in_dim.35
  62.9 3.2 %collective-permute-start.5 = (f32[2048]{0:T(1024)S(1)}, f32[2048]{0:T(1024)S(1)}, u32[]{:S(2)}, u32[]{:S(2)}) collective-permute-start(f32[2048]{0:T(1024)S(1)} %add.145), channel_id=1, source_target_pairs={{0,16},{1,17},{2,18},{3,19},{4,20},{5,21},{6,22},{7,23},{8,24},{9,... | collective-permute-start | bytes 24584 | tf_op jit(solution)/shard_map/ppermute | solution.py:50
  66.1 0.8 collective-permute-done.18
  66.9 1.1 collective-permute-start.19
  68.0 0.1 collective-permute-done.5
  68.1 2.2 %collective-permute-start.20 = (f32[256,64]{0,1:T(8,128)S(1)}, f32[256,64]{0,1:T(8,128)S(1)}, u32[]{:S(2)}, u32[]{:S(2)}) collective-permute-start(f32[256,64]{0,1:T(8,128)S(1)} %get-tuple-element.11), channel_id=1, source_target_pairs={{0,64},{32,96},{64,0},{96,32},{1,65},{33,97},{65,1},{97,33},{2,66}... | collective-permute-start | bytes 196616 | tf_op jit(solution)/shard_map/ppermute | solution.py:42
  70.3 7.8 %collective-permute-done.19 = f32[256,64]{0,1:T(8,128)S(1)} collective-permute-done((f32[256,64]{0,1:T(8,128)S(1)}, f32[256,64]{0,1:T(8,128)S(1)}, u32[]{:S(2)}, u32[]{:S(2)}) %collective-permute-start.19) | collective-permute-done | bytes 65568 | tf_op jit(solution)/shard_map/ppermute | solution.py:42
  78.1 0.9 collective-permute-start.21
  79.1 0.1 collective-permute-done.20
  79.2 3.2 %collective-permute-done.21 = f32[256,64]{0,1:T(8,128)S(1)} collective-permute-done((f32[256,64]{0,1:T(8,128)S(1)}, f32[256,64]{0,1:T(8,128)S(1)}, u32[]{:S(2)}, u32[]{:S(2)}) %collective-permute-start.21) | collective-permute-done | bytes 65568 | tf_op jit(solution)/shard_map/ppermute | solution.py:42
  82.4 0.7 subtract_convert_fusion.1
  83.1 1.2 copy.20
  84.3 0.8 copy-done.7
  85.1 1.2 copy.21
  86.3 1.2 copy.22
  87.7 8.3 %fusion = f32[2048]{0:T(1024)S(1)} fusion(f32[2048,896]{0,1:T(8,128)} %get-tuple-element.21, bf16[4,256,896]{1,2,0:T(8,128)(2,1)S(1)} %constant_dynamic-update-slice_fusion, bf16[256,4,2048]{0,2,1:T(8,128)(2,1)} %bitcast.64), kind=kOutput, calls=%fused_computation.2 | convolution fusion | flops 3761764352 | bytes 13377536 | tf_op jit(solution)/shard_map/tbj,bti->ji/dot_general | solution.py:97
  96.1 0.3 collective-permute-start.22
  96.4 1.5 convolution_bitcast_fusion
  97.9 0.9 fusion.26
  98.8 0.7 multiply_convert_fusion
  99.6 1.3 copy-done.2
  100.8 1.3 convolution_convert_fusion.2
  102.2 1.1 collective-permute-start.23
  103.2 1.3 convolution_convert_fusion.1
  104.5 1.4 collective-permute-done.23
  105.9 2.6 %collective-permute-start.24 = (f32[2048]{0:T(1024)S(1)}, f32[2048]{0:T(1024)S(1)}, u32[]{:S(2)}, u32[]{:S(2)}) collective-permute-start(f32[2048]{0:T(1024)S(1)} %add.173), channel_id=1, source_target_pairs={{0,4},{1,5},{2,6},{3,7},{4,0},{5,1},{6,2},{7,3},{8,12},{9,13},{10,... | collective-permute-start | bytes 24584 | tf_op jit(solution)/shard_map/ppermute | solution.py:50
  108.5 0.7 convolution_bitcast_fusion.1
  109.2 1.9 %collective-permute-done.24 = f32[2048]{0:T(1024)S(1)} collective-permute-done((f32[2048]{0:T(1024)S(1)}, f32[2048]{0:T(1024)S(1)}, u32[]{:S(2)}, u32[]{:S(2)}) %collective-permute-start.24) | collective-permute-done | bytes 8224 | tf_op jit(solution)/shard_map/ppermute | solution.py:50
  111.1 0.9 collective-permute-start.25
  112.0 0.1 collective-permute-start.9
  112.1 2.6 %collective-permute-done.25 = f32[2048]{0:T(1024)S(1)} collective-permute-done((f32[2048]{0:T(1024)S(1)}, f32[2048]{0:T(1024)S(1)}, u32[]{:S(2)}, u32[]{:S(2)}) %collective-permute-start.25) | collective-permute-done | bytes 8224 | tf_op jit(solution)/shard_map/ppermute | solution.py:50
  114.7 4.7 %collective-permute-start.26 = (f32[2048]{0:T(1024)S(1)}, f32[2048]{0:T(1024)S(1)}, u32[]{:S(2)}, u32[]{:S(2)}) collective-permute-start(f32[2048]{0:T(1024)S(1)} %add.175), channel_id=1, source_target_pairs={{0,16},{1,17},{2,18},{3,19},{4,20},{5,21},{6,22},{7,23},{8,24},{9,... | collective-permute-start | bytes 24584 | tf_op jit(solution)/shard_map/ppermute | solution.py:50
  119.5 1.3 convolution_convert_fusion
  120.8 0.1 collective-permute-start.6
  120.8 2.7 %collective-permute-start.7 = (bf16[256,896]{1,0:T(8,128)(2,1)S(1)}, bf16[256,896]{1,0:T(8,128)(2,1)S(1)}, u32[]{:S(2)}, u32[]{:S(2)}) collective-permute-start(bf16[256,896]{1,0:T(8,128)(2,1)S(1)} %convolution_convert_fusion.1), channel_id=1, source_target_pairs={{0,64},{32,96},{64,0},{96,32},{1,65},{33,97},{65,1},{97,33},{2,66}... | collective-permute-start | bytes 1376264 | tf_op jit(solution)/shard_map/ppermute | solution.py:92
  123.5 0.6 collective-permute-start.8
  124.1 0.6 add_divide_fusion
  124.7 0.1 fusion.56
  124.7 3.0 %collective-permute-start.10 = (f32[4,256,64]{1,2,0:T(8,128)S(1)}, f32[4,256,64]{1,2,0:T(8,128)S(1)}, u32[]{:S(2)}, u32[]{:S(2)}) collective-permute-start(f32[4,256,64]{1,2,0:T(8,128)S(1)} %fusion.56), channel_id=1, source_target_pairs={{0,64},{32,96},{64,0},{96,32},{1,65},{33,97},{65,1},{97,33},{2,66}... | collective-permute-start | bytes 786440 | tf_op jit(solution)/shard_map/ppermute | solution.py:50
  127.7 18.9 %collective-permute-done.6 = bf16[256,896]{1,0:T(8,128)(2,1)S(1)} collective-permute-done((bf16[256,896]{1,0:T(8,128)(2,1)S(1)}, bf16[256,896]{1,0:T(8,128)(2,1)S(1)}, u32[]{:S(2)}, u32[]{:S(2)}) %collective-permute-start.6) | collective-permute-done | bytes 458784 | tf_op jit(solution)/shard_map/ppermute | solution.py:92
  146.7 2.2 %fusion.15 = bf16[256,896]{1,0:T(8,128)(2,1)} fusion(bf16[2048,896]{0,1:T(8,128)(2,1)S(1)} %copy-done.2, bf16[256,4,2048]{0,2,1:T(8,128)(2,1)S(1)} %multiply_convert_fusion, s32[]{:T(128)S(6)} %select_n.50, bf16[256,896]{1,0:T(8,128)(2,1)S(1)} %collective-permute-done.8, bf16[256,896]{1,0:T(8,128)(2,1)S(1)} %collective-permute-done.7, ...), kind=kOutput, calls=%fused_computation.19 | convolution fusion | flops 941129728 | bytes 6553604 | tf_op jit(solution)/shard_map/dot_general | solution.py:87
  149.0 0.7 convolution_bitcast_fusion.2
  149.7 0.7 fusion.33
  (60 shorter events, 0.5 us)
Async XLA Ops:
  7.2 2.4 %copy-start = (bf16[64,896]{1,0:T(8,128)(2,1)S(1)}, bf16[64,896]{1,0:T(8,128)(2,1)}, u32[]{:S(2)}) copy-start(bf16[64,896]{1,0:T(8,128)(2,1)} %param.9) | copy-start | bytes 344068
  7.2 80.5 %all-gather.2.cloned.1.call-start = ((), (), s32[]{:S(2)}) async-start(), calls=%async_computation | async-start | bytes 4325376 | tf_op jit(solution)/shard_map/all_gather | solution.py:65
  8.2 0.7 collective-permute-start
  8.9 0.7 copy-start.8
  10.9 1.3 collective-permute-start.14
  12.3 4.3 %collective-permute-start.15 = (f32[256,64]{0,1:T(8,128)S(1)}, f32[256,64]{0,1:T(8,128)S(1)}, u32[]{:S(2)}, u32[]{:S(2)}) collective-permute-start(f32[256,64]{0,1:T(8,128)S(1)} %add.166), channel_id=1, source_target_pairs={{0,2},{1,3},{2,0},{3,1},{4,6},{5,7},{6,4},{7,5},{8,10},{9,11},{10,... | collective-permute-start | bytes 196616 | tf_op jit(solution)/shard_map/ppermute | solution.py:50
  16.6 19.0 %copy-start.4 = (bf16[2048,64]{0,1:T(8,128)(2,1)S(1)}, bf16[2048,64]{0,1:T(8,128)(2,1)}, u32[]{:S(2)}) copy-start(bf16[2048,64]{0,1:T(8,128)(2,1)} %param.10) | copy-start | bytes 786436
  16.6 9.6 %collective-permute-start.16 = (f32[256,64]{0,1:T(8,128)S(1)}, f32[256,64]{0,1:T(8,128)S(1)}, u32[]{:S(2)}, u32[]{:S(2)}) collective-permute-start(f32[256,64]{0,1:T(8,128)S(1)} %add.167), channel_id=1, source_target_pairs={{0,4},{1,5},{2,6},{3,7},{4,0},{5,1},{6,2},{7,3},{8,12},{9,13},{10,... | collective-permute-start | bytes 196616 | tf_op jit(solution)/shard_map/ppermute | solution.py:50
  26.3 22.5 %copy-start.3 = (bf16[256,896]{1,0:T(8,128)(2,1)S(1)}, bf16[256,896]{1,0:T(8,128)(2,1)}, u32[]{:S(2)}) copy-start(bf16[256,896]{1,0:T(8,128)(2,1)} %param.6) | copy-start | bytes 1376260
  26.3 33.7 %collective-permute-start.17 = (f32[256,64]{0,1:T(8,128)S(1)}, f32[256,64]{0,1:T(8,128)S(1)}, u32[]{:S(2)}, u32[]{:S(2)}) collective-permute-start(f32[256,64]{0,1:T(8,128)S(1)} %add.168), channel_id=1, source_target_pairs={{0,8},{1,9},{2,10},{3,11},{4,12},{5,13},{6,14},{7,15},{8,0},{9,1},... | collective-permute-start | bytes 196616 | tf_op jit(solution)/shard_map/ppermute | solution.py:50
  43.4 24.7 %copy-start.9 = (f32[2048]{0:T(1024)S(1)}, f32[2048]{0:T(1024)}, u32[]{:S(2)}) copy-start(f32[2048]{0:T(1024)} %param.11) | copy-start | bytes 24580
  43.4 1.2 collective-permute-start.1
  44.6 3.7 %collective-permute-start.2 = (f32[2048]{0:T(1024)S(1)}, f32[2048]{0:T(1024)S(1)}, u32[]{:S(2)}, u32[]{:S(2)}) collective-permute-start(f32[2048]{0:T(1024)S(1)} %add.142), channel_id=1, source_target_pairs={{0,2},{1,3},{2,0},{3,1},{4,6},{5,7},{6,4},{7,5},{8,10},{9,11},{10,... | collective-permute-start | bytes 24584 | tf_op jit(solution)/shard_map/ppermute | solution.py:50
  48.3 9.7 %collective-permute-start.3 = (f32[2048]{0:T(1024)S(1)}, f32[2048]{0:T(1024)S(1)}, u32[]{:S(2)}, u32[]{:S(2)}) collective-permute-start(f32[2048]{0:T(1024)S(1)} %add.143), channel_id=1, source_target_pairs={{0,4},{1,5},{2,6},{3,7},{4,0},{5,1},{6,2},{7,3},{8,12},{9,13},{10,... | collective-permute-start | bytes 24584 | tf_op jit(solution)/shard_map/ppermute | solution.py:50
  48.8 34.3 %collective-permute-start.11 = (bf16[256,896]{1,0:T(8,128)(2,1)S(1)}, bf16[256,896]{1,0:T(8,128)(2,1)}, u32[]{:S(2)}, u32[]{:S(2)}) collective-permute-start(bf16[256,896]{1,0:T(8,128)(2,1)S(1)} %copy-done.3), channel_id=1, source_target_pairs={{0,32},{32,64},{64,96},{96,0},{1,33},{33,65},{65,97},{97,1},{2,34}... | collective-permute-start | bytes 1376264 | tf_op jit(solution)/shard_map/ppermute | solution.py:42
  48.8 35.6 %collective-permute-start.12 = (bf16[256,896]{1,0:T(8,128)(2,1)S(1)}, bf16[256,896]{1,0:T(8,128)(2,1)S(1)}, u32[]{:S(2)}, u32[]{:S(2)}) collective-permute-start(bf16[256,896]{1,0:T(8,128)(2,1)S(1)} %copy-done.3), channel_id=1, source_target_pairs={{0,64},{32,96},{64,0},{96,32},{1,65},{33,97},{65,1},{97,33},{2,66}... | collective-permute-start | bytes 1376264 | tf_op jit(solution)/shard_map/ppermute | solution.py:42
  57.1 29.2 %collective-permute-start.13 = (bf16[256,896]{1,0:T(8,128)(2,1)S(1)}, bf16[256,896]{1,0:T(8,128)(2,1)}, u32[]{:S(2)}, u32[]{:S(2)}) collective-permute-start(bf16[256,896]{1,0:T(8,128)(2,1)S(1)} %copy-done.3), channel_id=1, source_target_pairs={{0,96},{32,0},{64,32},{96,64},{1,97},{33,1},{65,33},{97,65},{2,98}... | collective-permute-start | bytes 1376264 | tf_op jit(solution)/shard_map/ppermute | solution.py:42
  58.0 4.9 %collective-permute-start.4 = (f32[2048]{0:T(1024)S(1)}, f32[2048]{0:T(1024)S(1)}, u32[]{:S(2)}, u32[]{:S(2)}) collective-permute-start(f32[2048]{0:T(1024)S(1)} %add.144), channel_id=1, source_target_pairs={{0,8},{1,9},{2,10},{3,11},{4,12},{5,13},{6,14},{7,15},{8,0},{9,1},... | collective-permute-start | bytes 24584 | tf_op jit(solution)/shard_map/ppermute | solution.py:50
  60.0 6.9 %collective-permute-start.18 = (f32[256,64]{0,1:T(8,128)S(1)}, f32[256,64]{0,1:T(8,128)S(1)}, u32[]{:S(2)}, u32[]{:S(2)}) collective-permute-start(f32[256,64]{0,1:T(8,128)S(1)} %add.169), channel_id=1, source_target_pairs={{0,16},{1,17},{2,18},{3,19},{4,20},{5,21},{6,22},{7,23},{8,24},{9,... | collective-permute-start | bytes 196616 | tf_op jit(solution)/shard_map/ppermute | solution.py:50
  62.9 5.2 %collective-permute-start.5 = (f32[2048]{0:T(1024)S(1)}, f32[2048]{0:T(1024)S(1)}, u32[]{:S(2)}, u32[]{:S(2)}) collective-permute-start(f32[2048]{0:T(1024)S(1)} %add.145), channel_id=1, source_target_pairs={{0,16},{1,17},{2,18},{3,19},{4,20},{5,21},{6,22},{7,23},{8,24},{9,... | collective-permute-start | bytes 24584 | tf_op jit(solution)/shard_map/ppermute | solution.py:50
  66.9 11.2 %collective-permute-start.19 = (f32[256,64]{0,1:T(8,128)S(1)}, f32[256,64]{0,1:T(8,128)S(1)}, u32[]{:S(2)}, u32[]{:S(2)}) collective-permute-start(f32[256,64]{0,1:T(8,128)S(1)} %get-tuple-element.11), channel_id=1, source_target_pairs={{0,32},{32,64},{64,96},{96,0},{1,33},{33,65},{65,97},{97,1},{2,34}... | collective-permute-start | bytes 196616 | tf_op jit(solution)/shard_map/ppermute | solution.py:42
  68.1 11.0 %collective-permute-start.20 = (f32[256,64]{0,1:T(8,128)S(1)}, f32[256,64]{0,1:T(8,128)S(1)}, u32[]{:S(2)}, u32[]{:S(2)}) collective-permute-start(f32[256,64]{0,1:T(8,128)S(1)} %get-tuple-element.11), channel_id=1, source_target_pairs={{0,64},{32,96},{64,0},{96,32},{1,65},{33,97},{65,1},{97,33},{2,66}... | collective-permute-start | bytes 196616 | tf_op jit(solution)/shard_map/ppermute | solution.py:42
  78.1 4.3 %collective-permute-start.21 = (f32[256,64]{0,1:T(8,128)S(1)}, f32[256,64]{0,1:T(8,128)S(1)}, u32[]{:S(2)}, u32[]{:S(2)}) collective-permute-start(f32[256,64]{0,1:T(8,128)S(1)} %get-tuple-element.11), channel_id=1, source_target_pairs={{0,96},{32,0},{64,32},{96,64},{1,97},{33,1},{65,33},{97,65},{2,98}... | collective-permute-start | bytes 196616 | tf_op jit(solution)/shard_map/ppermute | solution.py:42
  84.3 0.8 copy-start.7
  87.7 8.7 %copy-start.1 = (bf16[256,8192]{0,1:T(8,128)(2,1)S(1)}, bf16[256,8192]{0,1:T(8,128)(2,1)}, u32[]{:S(2)}) copy-start(bf16[256,8192]{0,1:T(8,128)(2,1)} %all-gather.2.cloned.1.call-done) | copy-start | bytes 12582916
  87.7 8.7 %copy-start.6 = (bf16[4,256,64]{1,2,0:T(8,128)(2,1)S(1)}, bf16[4,256,64]{1,2,0:T(8,128)(2,1)}, u32[]{:S(2)}) copy-start(bf16[4,256,64]{1,2,0:T(8,128)(2,1)} %get-tuple-element.9) | copy-start | bytes 393220
  96.1 1.8 %copy-start.5 = (bf16[2048,64]{0,1:T(8,128)(2,1)S(1)}, bf16[2048,64]{0,1:T(8,128)(2,1)}, u32[]{:S(2)}) copy-start(bf16[2048,64]{0,1:T(8,128)(2,1)} %param.10) | copy-start | bytes 786436
  96.1 6.1 %collective-permute-start.22 = (f32[2048]{0:T(1024)S(1)}, f32[2048]{0:T(1024)S(1)}, u32[]{:S(2)}, u32[]{:S(2)}) collective-permute-start(f32[2048]{0:T(1024)S(1)} %fusion), channel_id=1, source_target_pairs={{0,1},{1,0},{2,3},{3,2},{4,5},{5,4},{6,7},{7,6},{8,9},{9,8},{10,11... | collective-permute-start | bytes 24584 | tf_op jit(solution)/shard_map/ppermute | solution.py:50
  98.8 2.0 %copy-start.2 = (bf16[2048,896]{0,1:T(8,128)(2,1)S(1)}, bf16[2048,896]{0,1:T(8,128)(2,1)}, u32[]{:S(2)}) copy-start(bf16[2048,896]{0,1:T(8,128)(2,1)} %get-tuple-element.15) | copy-start | bytes 11010052
  102.2 3.7 %collective-permute-start.23 = (f32[2048]{0:T(1024)S(1)}, f32[2048]{0:T(1024)S(1)}, u32[]{:S(2)}, u32[]{:S(2)}) collective-permute-start(f32[2048]{0:T(1024)S(1)} %add.172), channel_id=1, source_target_pairs={{0,2},{1,3},{2,0},{3,1},{4,6},{5,7},{6,4},{7,5},{8,10},{9,11},{10,... | collective-permute-start | bytes 24584 | tf_op jit(solution)/shard_map/ppermute | solution.py:50
  105.9 5.2 %collective-permute-start.24 = (f32[2048]{0:T(1024)S(1)}, f32[2048]{0:T(1024)S(1)}, u32[]{:S(2)}, u32[]{:S(2)}) collective-permute-start(f32[2048]{0:T(1024)S(1)} %add.173), channel_id=1, source_target_pairs={{0,4},{1,5},{2,6},{3,7},{4,0},{5,1},{6,2},{7,3},{8,12},{9,13},{10,... | collective-permute-start | bytes 24584 | tf_op jit(solution)/shard_map/ppermute | solution.py:50
  111.1 3.7 %collective-permute-start.25 = (f32[2048]{0:T(1024)S(1)}, f32[2048]{0:T(1024)S(1)}, u32[]{:S(2)}, u32[]{:S(2)}) collective-permute-start(f32[2048]{0:T(1024)S(1)} %add.174), channel_id=1, source_target_pairs={{0,8},{1,9},{2,10},{3,11},{4,12},{5,13},{6,14},{7,15},{8,0},{9,1},... | collective-permute-start | bytes 24584 | tf_op jit(solution)/shard_map/ppermute | solution.py:50
  112.0 12.6 %collective-permute-start.9 = (f32[4,256,64]{1,2,0:T(8,128)S(1)}, f32[4,256,64]{1,2,0:T(8,128)S(1)}, u32[]{:S(2)}, u32[]{:S(2)}) collective-permute-start(f32[4,256,64]{1,2,0:T(8,128)S(1)} %slice_add_fusion.1), channel_id=1, source_target_pairs={{0,32},{32,0},{64,96},{96,64},{1,33},{33,1},{65,97},{97,65},{2,34}... | collective-permute-start | bytes 786440 | tf_op jit(solution)/shard_map/ppermute | solution.py:50
  114.7 9.4 %collective-permute-start.26 = (f32[2048]{0:T(1024)S(1)}, f32[2048]{0:T(1024)S(1)}, u32[]{:S(2)}, u32[]{:S(2)}) collective-permute-start(f32[2048]{0:T(1024)S(1)} %add.175), channel_id=1, source_target_pairs={{0,16},{1,17},{2,18},{3,19},{4,20},{5,21},{6,22},{7,23},{8,24},{9,... | collective-permute-start | bytes 24584 | tf_op jit(solution)/shard_map/ppermute | solution.py:50
  120.8 25.9 %collective-permute-start.6 = (bf16[256,896]{1,0:T(8,128)(2,1)S(1)}, bf16[256,896]{1,0:T(8,128)(2,1)S(1)}, u32[]{:S(2)}, u32[]{:S(2)}) collective-permute-start(bf16[256,896]{1,0:T(8,128)(2,1)S(1)} %convolution_convert_fusion.2), channel_id=1, source_target_pairs={{0,32},{32,64},{64,96},{96,0},{1,33},{33,65},{65,97},{97,1},{2,34}... | collective-permute-start | bytes 1376264 | tf_op jit(solution)/shard_map/ppermute | solution.py:92
  120.8 25.8 %collective-permute-start.7 = (bf16[256,896]{1,0:T(8,128)(2,1)S(1)}, bf16[256,896]{1,0:T(8,128)(2,1)S(1)}, u32[]{:S(2)}, u32[]{:S(2)}) collective-permute-start(bf16[256,896]{1,0:T(8,128)(2,1)S(1)} %convolution_convert_fusion.1), channel_id=1, source_target_pairs={{0,64},{32,96},{64,0},{96,32},{1,65},{33,97},{65,1},{97,33},{2,66}... | collective-permute-start | bytes 1376264 | tf_op jit(solution)/shard_map/ppermute | solution.py:92
  123.5 23.2 %collective-permute-start.8 = (bf16[256,896]{1,0:T(8,128)(2,1)S(1)}, bf16[256,896]{1,0:T(8,128)(2,1)S(1)}, u32[]{:S(2)}, u32[]{:S(2)}) collective-permute-start(bf16[256,896]{1,0:T(8,128)(2,1)S(1)} %convolution_convert_fusion), channel_id=1, source_target_pairs={{0,96},{32,0},{64,32},{96,64},{1,97},{33,1},{65,33},{97,65},{2,98}... | collective-permute-start | bytes 1376264 | tf_op jit(solution)/shard_map/ppermute | solution.py:92
  124.7 24.2 %collective-permute-start.10 = (f32[4,256,64]{1,2,0:T(8,128)S(1)}, f32[4,256,64]{1,2,0:T(8,128)S(1)}, u32[]{:S(2)}, u32[]{:S(2)}) collective-permute-start(f32[4,256,64]{1,2,0:T(8,128)S(1)} %fusion.56), channel_id=1, source_target_pairs={{0,64},{32,96},{64,0},{96,32},{1,65},{33,97},{65,1},{97,33},{2,66}... | collective-permute-start | bytes 786440 | tf_op jit(solution)/shard_map/ppermute | solution.py:50
Sparse Core Ops, SparseCore 0:
  10.8 57.8 all-gather.1
